TPU v7x, 256 devices: a whole 4x4x8 slice. The times are simulated.
256 devices in a mesh: walker: 2 (over core), grp: 128 (over z, x, y).
Axes of the slice: x: 4, y: 4, z: 8, core: 2. Of those that a mesh axis runs over, the one named last changes fastest.
Arguments:
- feats: bfloat16 [4096, 256], P(('walker', 'grp')), parts along dimension 0, may hold values from -6 to 6
- perm: int32 [4096], P('walker'), parts along dimension 0, may hold values from 0 to 2047, each once
- w_left: bfloat16 [256, 256], replicated, may hold values from -0.375 to 0.375
- w_right: bfloat16 [256, 256], replicated, may hold values from -0.375 to 0.375
- bias_in: float32 [256], replicated, may hold values from -3 to 3
- w_hidden: bfloat16 [256, 256], replicated, may hold values from -0.375 to 0.375
- bias_hidden: float32 [256], replicated, may hold values from -3 to 3
- w_out: float32 [256], replicated, may hold values from -0.375 to 0.375
- pair_strength: float32 [128], replicated, may hold values from 16 to 32
Outputs:
- log_pivot: float32 [256], P('walker'), parts along dimension 0
- panel_cols: float32 [3584, 256], P(('walker', 'grp')), parts along dimension 0
- schur: float32 [3584, 1792], P(('walker', 'grp')), parts along dimension 0
There are 2 independent parts, one for each index of `walker`. A program takes and returns all parts, laid end to end along the dimension named above; an argument that names none is the same for every part. Nothing has to cross between parts.
Inputs may be any that keep to these rules, and one draw needn't show every extreme that they name: `perm`: each position 0 to 2047 appears exactly once.
All inputs are finite; a program needn't handle non-finite values.
Results may differ from a plain program's by a relative error of at most 0.0062.
Values may be sent and summed in bfloat16 or wider, within the bound.
No kernel may reach another device: no remote copies, remote signals or barrier semaphores. Data moves between devices by JAX's collectives and lax.ppermute only.
A program may use at most 64 MiB of HBM per device.

v0:
```python
import jax
import jax.numpy as jnp
from jax import lax
from jax.sharding import PartitionSpec as P


def orbitals(left_part, right_part, bias_in, w_hidden, bias_hidden, w_out):
    pre = (
        left_part.astype(jnp.float32)[:, None, :]
        + right_part.astype(jnp.float32)[None, :, :]
        + bias_in
    )
    gated = jax.nn.silu(pre).astype(jnp.bfloat16).reshape(-1, pre.shape[-1])
    hidden = jax.nn.silu(jnp.dot(gated, w_hidden, preferred_element_type=jnp.float32) + bias_hidden)
    values = jnp.dot(hidden, w_out, precision=lax.Precision.HIGHEST)
    return values.reshape(left_part.shape[0], right_part.shape[0])


def column_width():
    return 128


def forward_terms(left_rows, right_cols, params):
    count = right_cols.shape[0]
    width = column_width()
    pieces = right_cols.reshape(count // width, width, right_cols.shape[1])
    result = lax.map(lambda piece: orbitals(left_rows, piece, *params), pieces)
    return jnp.transpose(result, (1, 0, 2)).reshape(left_rows.shape[0], count)


def backward_terms(right_rows, left_cols, params):
    count = left_cols.shape[0]
    width = column_width()
    pieces = left_cols.reshape(count // width, width, left_cols.shape[1])
    result = lax.map(lambda piece: orbitals(piece, right_rows, *params), pieces)
    return result.reshape(count, right_rows.shape[0]).T


def factor_block(block):
    size = block.shape[0]
    position = jnp.arange(size)

    def advance(step, carry):
        matrix, lower, pivots = carry
        first = (2 * step).astype(jnp.int32)
        col_even = lax.dynamic_slice_in_dim(matrix, first, 1, 1)[:, 0]
        col_odd = lax.dynamic_slice_in_dim(matrix, first + 1, 1, 1)[:, 0]
        pivot = lax.dynamic_index_in_dim(col_odd, first, 0, keepdims=False)
        keep = position >= first
        zeros = jnp.zeros_like(col_even)
        lower_even = jnp.where(keep, col_odd / pivot, zeros)
        lower_odd = jnp.where(keep, -col_even / pivot, zeros)
        lower = lax.dynamic_update_slice(
            lower, jnp.stack([lower_even, lower_odd], axis=1), (jnp.int32(0), first)
        )
        rest = position > first + 1
        keep_even = jnp.where(rest, col_even, zeros)
        keep_odd = jnp.where(rest, col_odd, zeros)
        matrix = (
            matrix
            + (keep_odd[:, None] * keep_even[None, :] - keep_even[:, None] * keep_odd[None, :])
            / pivot
        )
        pivots = lax.dynamic_update_slice(pivots, pivot[None], (step.astype(jnp.int32),))
        return (matrix, lower, pivots)

    start = (block, jnp.zeros_like(block), jnp.zeros((size // 2,), block.dtype))
    matrix, lower, pivots = lax.fori_loop(0, size // 2, advance, start)
    return (lower, pivots)


def pair_scale(columns, pivots):
    count = columns.shape[0]
    grouped = columns.reshape(count, -1, 2)
    swapped = jnp.stack([grouped[:, :, 1], -grouped[:, :, 0]], axis=2).reshape(count, -1)
    return swapped / jnp.repeat(pivots, 2)[None, :]


def solve_rows(lower, rows):
    return jax.scipy.linalg.solve_triangular(lower, rows.T, lower=True, unit_diagonal=True).T


def on_device(feats, perm, w_left, w_right, bias_in, w_hidden, bias_hidden, w_out, pair_strength):
    groups = lax.axis_size("grp")
    device = lax.axis_index("grp")
    electrons = perm.shape[0]
    panel = 2 * pair_strength.shape[0]
    share = panel // groups
    tail = (electrons - panel) // groups
    params = (bias_in, w_hidden, bias_hidden, w_out)
    left_own = jnp.dot(feats, w_left, preferred_element_type=jnp.float32).astype(jnp.bfloat16)
    right_own = jnp.dot(feats, w_right, preferred_element_type=jnp.float32).astype(jnp.bfloat16)
    left_every, right_every = (
        lax.all_gather(left_own, "grp", axis=0, tiled=True),
        lax.all_gather(right_own, "grp", axis=0, tiled=True),
    )
    left_all = jnp.take(left_every, perm, axis=0)
    right_all = jnp.take(right_every, perm, axis=0)
    top_start = device * share
    tail_start = panel + device * tail
    left_rows = jnp.concatenate(
        [
            lax.dynamic_slice_in_dim(left_all, top_start, share, 0),
            lax.dynamic_slice_in_dim(left_all, tail_start, tail, 0),
        ],
        axis=0,
    )
    right_rows = jnp.concatenate(
        [
            lax.dynamic_slice_in_dim(right_all, top_start, share, 0),
            lax.dynamic_slice_in_dim(right_all, tail_start, tail, 0),
        ],
        axis=0,
    )
    top_rows = forward_terms(left_rows[:share], right_all[:panel], params) - backward_terms(
        right_rows[:share], left_all[:panel], params
    )
    tail_rows = forward_terms(left_rows[share:], right_all, params) - backward_terms(
        right_rows[share:], left_all, params
    )
    block_rows = lax.all_gather(top_rows, "grp", axis=0, tiled=True)
    pattern = jnp.array([[0.0, 1.0], [-1.0, 0.0]], dtype=pair_strength.dtype)
    block = block_rows + jnp.kron(jnp.diag(pair_strength), pattern)
    lower, pivots = factor_block(block)
    log_pivot = jnp.log(jnp.abs(pivots))
    below_own = tail_rows[:, :panel]
    trailing_own = tail_rows[:, panel:]
    panel_own = solve_rows(lower, below_own)
    scaled_own = pair_scale(panel_own, pivots)
    schur = trailing_own - jnp.dot(
        panel_own,
        lax.all_gather(scaled_own, "grp", axis=0, tiled=True).T,
        precision=lax.Precision.HIGHEST,
    )
    return (log_pivot, panel_own, schur)


def solution(mesh):
    return jax.shard_map(
        on_device,
        mesh=mesh,
        in_specs=(P(("walker", "grp"), None), P("walker"), P(), P(), P(), P(), P(), P(), P()),
        out_specs=(P("walker"), P(("walker", "grp"), None), P(("walker", "grp"), None)),
        check_vma=False,
    )
```

profile of v0, /device:TPU:6, one launch (start us, length us, event | category | flops | bytes accessed | tf_op | source)
XLA Modules:
  0.0 1272.6 jit_solution(9753338062024064957)
XLA Ops:
  12.1 7.3 broadcast_multiply_fusion
  19.5 13.2 %mul.191 = f32[256,256]{1,0:T(8,128)} reshape(f32[128,2,128,2]{3,2,1,0:T(8,128)} %broadcast_multiply_fusion) | data formatting | bytes 524288 | tf_op jit(solution)/shard_map/jit(kron)/mul | solution.py:123
  33.8 83.8 %all-gather.6.cloned.1.call-done = bf16[2048,256]{1,0:T(8,128)(2,1)} async-done(((bf16[16,256]{1,0:T(8,128)(2,1)}), bf16[2048,256]{1,0:T(8,128)(2,1)}) %all-gather.6.cloned.1.call-update) | async-done | bytes 1048592 | tf_op jit(solution)/shard_map/all_gather | solution.py:94
  117.5 8.0 gather_fusion
  125.5 97.7 %all-gather.8.cloned.1.call-done = bf16[2048,256]{1,0:T(8,128)(2,1)} async-done(((bf16[16,256]{1,0:T(8,128)(2,1)}), bf16[2048,256]{1,0:T(8,128)(2,1)}) %all-gather.8.cloned.1.call-update) | async-done | bytes 1048592 | tf_op jit(solution)/shard_map/all_gather | solution.py:95
  223.2 8.0 gather_fusion.1
  234.8 64.1 %while.65 = (s32[]{:T(128)}, f32[16,14,128]{2,1,0:T(8,128)S(1)}, bf16[14,256]{1,0:T(8,128)(2,1)S(1)}, bf16[16,128,256]{2,1,0:T(8,128)(2,1)}, f32[256]{0:T(256)S(...) while((s32[]{:T(128)}, f32[16,14,128]{2,1,0:T(8,128)S(1)}, ...), condition=%wide.region_7.9_spmd, body=%wide.region_6.8_spmd.sunk | while | flops 245927424 | bytes 9696365 | solution.py:27
  299.6 2.5 while.64
  302.2 315.5 %all-gather = f32[128,2,256]{2,1,0:T(2,128)S(1)} all-gather(f32[1,2,256]{2,1,0:T(2,128)S(1)} %fusion.53), channel_id=1, replica_groups=mesh['walker'=2,'grp'=128] {'grp'}, dimensions={0}, use_global_device_ids=true | all-gather | bytes 264192 | tf_op jit(solution)/shard_map/all_gather | solution.py:121
  618.5 107.8 %while.66 = (s32[]{:T(128)}, f32[16,128,14]{2,1,0:T(8,128)}, bf16[16,128,256]{2,1,0:T(8,128)(2,1)S(1)}, bf16[14,256]{1,0:T(8,128)(2,1)S(1)}, f32[256]{0:T(256)S(...) while((s32[]{:T(128)}, f32[16,128,14]{2,1,0:T(8,128)}, ...), condition=%wide.region_9.11_spmd, body=%wide.region_8.10_spmd.sunk | while | flops 245927424 | bytes 11606153 | solution.py:35
  620.3 2.1 convolution_add_fusion.11
  627.1 2.1 convolution_add_fusion.11
  633.8 2.1 convolution_add_fusion.11
  640.5 2.1 convolution_add_fusion.11
  647.3 2.1 convolution_add_fusion.11
  667.5 2.1 convolution_add_fusion.11
  674.2 2.1 convolution_add_fusion.11
  707.9 2.1 convolution_add_fusion.11
  721.4 2.1 convolution_add_fusion.11
  729.2 365.8 %while.68 = (s32[]{:T(128)}, f32[256,256]{0,1:T(8,128)S(1)}, f32[256,256]{0,1:T(8,128)S(1)}, f32[128]{0:T(128)S(1)}, s32[]{:T(128)}, /*index=5*/s32[]{:T(128)}, s32[]{:T(128)}, s32[]{:T(128)}, s32[]{:T(128)}, s32[]{:T(128)}) while((s32[]{:T(128)}, f32[256,256]{0,1:T(8,128)S(1)}, f32[256,256]{0,1:T(8,128)S(1)}, ...), condition=%wide.region_5.7_spmd.clone.clone, body=%wide.region_4.6_spmd.clone.clone.sunk | while | flops 331276 | bytes 548637 | solution.py:68
  1095.1 5.4 while.67
  1100.6 20.5 %custom-call.4 = f32[2,128,128]{1,2,0:T(8,128)S(1)} custom-call(f32[2,128,128]{2,1,0:T(8,128)} %get-tuple-element.340), custom_call_target="InvertDiagBlocksLowerTriangular" | custom-call | tf_op jit(solution)/shard_map/jit(_solve_triangular)/triangular_solve | solution.py:80
  1123.5 138.6 %all-gather.10.cloned.1.call-done = f32[128,14,256]{2,1,0:T(8,128)} async-done(((f32[1,14,256]{2,1,0:T(8,128)}), f32[128,14,256]{2,1,0:T(8,128)}) %all-gather.10.cloned.1.call-update) | async-done | bytes 1835024 | tf_op jit(solution)/shard_map/all_gather | solution.py:132
  1263.8 2.3 convolution_subtract_fusion
  (1543 shorter events, 533.3 us)
Async XLA Ops:
  7.2 110.4 %all-gather.6.cloned.1.call-start = ((), (), s32[]{:S(2)}) async-start(), calls=%async_computation | async-start | bytes 1056768 | tf_op jit(solution)/shard_map/all_gather | solution.py:94
  9.5 213.7 %all-gather.8.cloned.1.call-start = ((), (), s32[]{:S(2)}) async-start(), calls=%async_computation.1 | async-start | bytes 1056768 | tf_op jit(solution)/shard_map/all_gather | solution.py:95
  11.3 1250.9 %all-gather.10.cloned.1.call-start = ((), (), s32[]{:S(2)}) async-start(), calls=%async_computation.2 | async-start | bytes 2113536 | tf_op jit(solution)/shard_map/all_gather | solution.py:132
  19.4 14.3 %copy-start.8 = (s32[2048]{0:T(1024)S(1)}, s32[2048]{0:T(1024)}, u32[]{:S(2)}) copy-start(s32[2048]{0:T(1024)} %param.23) | copy-start | bytes 24580
  234.3 65.3 %copy-start.3 = (f32[2,128,2]{2,1,0:T(8,128)S(1)}, f32[2,128,2]{2,1,0:T(8,128)}, u32[]{:S(2)}) copy-start(f32[2,128,2]{2,1,0:T(8,128)} %custom-call.10) | copy-start | bytes 6148
  299.6 2.6 copy-start.10
  620.3 2.1 copy-start.16
  627.1 2.1 copy-start.16
  633.8 2.1 copy-start.16
  640.5 2.1 copy-start.16
  647.3 2.1 copy-start.16
  654.0 2.1 copy-start.16
  667.5 2.1 copy-start.16
  674.2 2.1 copy-start.16
  681.0 2.1 copy-start.16
  687.7 2.1 copy-start.16
  694.5 2.1 copy-start.16
  701.2 2.1 copy-start.16
  707.9 2.1 copy-start.16
  721.4 2.1 copy-start.16
  726.3 2.8 copy-start.12
  729.1 365.9 %copy-start.11 = (s32[256]{0:T(256)S(1)}, s32[256]{0:T(256)}, u32[]{:S(2)}) copy-start(s32[256]{0:T(256)} %iota_add_fusion) | copy-start | bytes 3076
  729.2 365.9 %copy-start.17 = (s32[2]{0:T(128)S(1)}, s32[2]{0:T(128)}, u32[]{:S(2)}) copy-start(s32[2]{0:T(128)} %iota_multiply_fusion) | copy-start | bytes 28
  1121.6 142.3 %copy-start.7 = (f32[14,256]{1,0:T(8,128)}, f32[14,256]{1,0:T(8,128)S(1)}, u32[]{:S(2)}) copy-start(f32[14,256]{1,0:T(8,128)S(1)} %fusion.50) | copy-start | bytes 43012
  (13 other events, 16.2 us)
Sparse Core Ops, SparseCore 0:
  12.0 105.5 all-gather.5
  121.5 101.6 all-gather.7
  1123.1 138.9 all-gather.9
where the time goes:
time: 1280 us; the launch traced here: 1270 us
  waiting for transfers between devices  320 us (25%)
  blocking collectives  315 us (25%)
  other arithmetic  256 us (20%)
  local copies, waits for them, and re-layouts  242 us (19%)
  matrix products  113 us (9%)
  between operations  14.3 us (1%)
    all_gather x1, blocking collectives, on_device(): block_rows = lax.all_gather(top_rows, 'grp', axis=0, tiled=True)  315 us
    all_gather x1, waiting for transfers between devices, on_device(): lax.all_gather(scaled_own, 'grp', axis=0, tiled=True)  139 us
    add x128, other arithmetic, advance(): matrix + (keep_odd[:, None] * keep_even[None, :] - keep_even[:, None] * k...  104 us
    all_gather x1, waiting for transfers between devices, on_device(): lax.all_gather(right_own, 'grp', axis=0, tiled=True)  97.7 us
    dynamic_update_slice x128, local copies, waits for them, and re-layouts, advance(): lax.dynamic_update_slice(pivots, pivot[None], (step.astype(jnp.int32),))  86.2 us
    select_n x128, other arithmetic, advance(): lower_odd = jnp.where(keep, -col_even / pivot, zeros)  84.3 us
    all_gather x1, waiting for transfers between devices, on_device(): lax.all_gather(left_own, 'grp', axis=0, tiled=True)  83.8 us
    dynamic_slice x128, local copies, waits for them, and re-layouts, advance(): pivot = lax.dynamic_index_in_dim(col_odd, first, 0, keepdims=False)  75.5 us
  transfers between devices with their start and end apart: 3, of which 3 were waited for; matrix products, arithmetic and copies ran while one was open for 3% of the time, Pallas kernels for 0%

commit v1 on v0

v1 whole, which is shorter than its diff:
```python
import jax
import jax.numpy as jnp
from jax import lax
from jax.experimental import pallas as pl
from jax.experimental.pallas import tpu as pltpu
from jax.sharding import PartitionSpec as P


def orbitals(left_part, right_part, bias_in, w_hidden, bias_hidden, w_out):
    pre = (
        left_part.astype(jnp.float32)[:, None, :]
        + right_part.astype(jnp.float32)[None, :, :]
        + bias_in
    )
    gated = jax.nn.silu(pre).astype(jnp.bfloat16).reshape(-1, pre.shape[-1])
    hidden = jax.nn.silu(jnp.dot(gated, w_hidden, preferred_element_type=jnp.float32) + bias_hidden)
    values = jnp.dot(hidden, w_out, precision=lax.Precision.HIGHEST)
    return values.reshape(left_part.shape[0], right_part.shape[0])


def column_width():
    return 128


def forward_terms(left_rows, right_cols, params):
    count = right_cols.shape[0]
    width = column_width()
    pieces = right_cols.reshape(count // width, width, right_cols.shape[1])
    result = lax.map(lambda piece: orbitals(left_rows, piece, *params), pieces)
    return jnp.transpose(result, (1, 0, 2)).reshape(left_rows.shape[0], count)


def backward_terms(right_rows, left_cols, params):
    count = left_cols.shape[0]
    width = column_width()
    pieces = left_cols.reshape(count // width, width, left_cols.shape[1])
    result = lax.map(lambda piece: orbitals(piece, right_rows, *params), pieces)
    return result.reshape(count, right_rows.shape[0]).T


def factor_kernel(m_in_ref, m_ref):
    m_ref[...] = m_in_ref[...]
    rows, size = m_ref.shape
    lane = lax.broadcasted_iota(jnp.int32, (1, size), 1)
    lanes = lax.broadcasted_iota(jnp.int32, (rows, size), 1)
    row_idx = lax.broadcasted_iota(jnp.int32, (rows, 1), 0)

    def step(k, carry):
        first = 2 * k
        r0 = m_ref[pl.ds(first, 1), :]
        r1 = m_ref[pl.ds(first + 1, 1), :]
        pivot = jnp.sum(jnp.where(lane == first + 1, r0, 0.0), axis=1, keepdims=True)
        keep_lane = lane > first + 1
        even_lane = jnp.where(keep_lane, -r0 / pivot, 0.0)
        odd_lane = jnp.where(keep_lane, -r1 / pivot, 0.0)
        m = m_ref[...]
        col_even = jnp.sum(jnp.where(lanes == first, m, 0.0), axis=1, keepdims=True)
        col_odd = jnp.sum(jnp.where(lanes == first + 1, m, 0.0), axis=1, keepdims=True)
        keep_row = row_idx > first + 1
        col_even = jnp.where(keep_row, col_even, 0.0)
        col_odd = jnp.where(keep_row, col_odd, 0.0)
        m_ref[...] = m + (col_odd * even_lane - col_even * odd_lane)
        return carry

    lax.fori_loop(0, size // 2, step, 0)


def factor_augmented(matrix):
    return pl.pallas_call(
        factor_kernel,
        out_shape=jax.ShapeDtypeStruct(matrix.shape, matrix.dtype),
        in_specs=[pl.BlockSpec(memory_space=pltpu.VMEM)],
        out_specs=pl.BlockSpec(memory_space=pltpu.VMEM),
    )(matrix)


def pair_scale(columns, pivots):
    count = columns.shape[0]
    grouped = columns.reshape(count, -1, 2)
    swapped = jnp.stack([grouped[:, :, 1], -grouped[:, :, 0]], axis=2).reshape(count, -1)
    return swapped / jnp.repeat(pivots, 2)[None, :]


def on_device(feats, perm, w_left, w_right, bias_in, w_hidden, bias_hidden, w_out, pair_strength):
    groups = lax.axis_size("grp")
    device = lax.axis_index("grp")
    electrons = perm.shape[0]
    hid = w_left.shape[1]
    panel = 2 * pair_strength.shape[0]
    share = panel // groups
    tail = (electrons - panel) // groups
    params = (bias_in, w_hidden, bias_hidden, w_out)
    w_both = jnp.concatenate([w_left, w_right], axis=1)
    both_own = jnp.dot(feats, w_both, preferred_element_type=jnp.float32).astype(jnp.bfloat16)
    both_every = lax.all_gather(both_own, "grp", axis=0, tiled=True)
    both_all = jnp.take(both_every, perm, axis=0)
    left_all = both_all[:, :hid]
    right_all = both_all[:, hid:]
    top_start = device * share
    tail_start = panel + device * tail
    left_top = lax.dynamic_slice_in_dim(left_all, top_start, share, 0)
    right_top = lax.dynamic_slice_in_dim(right_all, top_start, share, 0)
    left_tail = lax.dynamic_slice_in_dim(left_all, tail_start, tail, 0)
    right_tail = lax.dynamic_slice_in_dim(right_all, tail_start, tail, 0)
    top_rows = forward_terms(left_top, right_all[:panel], params) - backward_terms(
        right_top, left_all[:panel], params
    )
    pad = (-share) % 8
    top_padded = jnp.pad(top_rows, ((0, pad), (0, 0)))
    gathered = lax.all_gather(top_padded, "grp", axis=0, tiled=False)
    block_rows = gathered[:, :share, :].reshape(panel, panel)
    tail_rows = forward_terms(left_tail, right_all, params) - backward_terms(
        right_tail, left_all, params
    )
    pattern = jnp.array([[0.0, 1.0], [-1.0, 0.0]], dtype=pair_strength.dtype)
    block = block_rows + jnp.kron(jnp.diag(pair_strength), pattern)
    below_own = tail_rows[:, :panel]
    trailing_own = tail_rows[:, panel:]
    extra = (-tail) % 8
    augmented = jnp.concatenate(
        [block, below_own, jnp.zeros((extra, panel), block.dtype)], axis=0
    )
    factored = factor_augmented(augmented)
    pairs = factored[:panel].reshape(panel // 2, 2, panel // 2, 2)
    pivots = jnp.diagonal(pairs[:, 0, :, 1])
    log_pivot = jnp.log(jnp.abs(pivots))
    panel_own = factored[panel:panel + tail]
    scaled_own = pair_scale(panel_own, pivots)
    schur = trailing_own - jnp.dot(
        panel_own,
        lax.all_gather(scaled_own, "grp", axis=0, tiled=True).T,
        precision=lax.Precision.HIGHEST,
    )
    return (log_pivot, panel_own, schur)


def solution(mesh):
    return jax.shard_map(
        on_device,
        mesh=mesh,
        in_specs=(P(("walker", "grp"), None), P("walker"), P(), P(), P(), P(), P(), P(), P()),
        out_specs=(P("walker"), P(("walker", "grp"), None), P(("walker", "grp"), None)),
        check_vma=False,
    )
```

time: 1280 us -> 504 us (0.39)
  blocking collectives: 315 us -> 0 us
  other arithmetic: 256 us -> 27 us
  local copies, waits for them, and re-layouts: 242 us -> 116 us
  waiting for transfers between devices: 320 us -> 210 us
  Pallas kernels: 0 us -> 22.2 us
    all_gather x1 -> x0, blocking collectives: 315 us -> none  [on_device(): block_rows = lax.all_gather(top_rows, 'grp', axis=0, tiled=True)]
    add x128 -> x0, other arithmetic: 104 us -> none  [advance(): matrix + (keep_odd[:, None] * keep_even[None, :] - keep_even[:, None] * k...]
    dynamic_update_slice x128 -> x0, local copies, waits for them, and re-layouts: 86.2 us -> none  [advance(): lax.dynamic_update_slice(pivots, pivot[None], (step.astype(jnp.int32),))]
    select_n x385 -> x1, other arithmetic: 86.3 us -> 0.45 us  [on_device(): both_all = jnp.take(both_every, perm, axis=0)]
    all_gather x2, waiting for transfers between devices: 181 us -> 98.7 us  [the longest x1 98.7 us: on_device(): both_every = lax.all_gather(both_own, 'grp', axis=0, tiled=True)]
    dynamic_slice x130 -> x2, local copies, waits for them, and re-layouts: 75.5 us -> 0.03 us  [the longest x1 0.02 us: on_device(): right_tail = lax.dynamic_slice_in_dim(right_all, tail_start, tail, 0)]
    all_gather x1, waiting for transfers between devices: 139 us -> 112 us  [on_device(): lax.all_gather(scaled_own, 'grp', axis=0, tiled=True)]
    pallas_call x0 -> x1, Pallas kernels: none -> 22.2 us  [factor_augmented(): pl.pallas_call(factor_kernel, out_shape=jax.ShapeDtypeStruct(matrix.shape...]
  transfers between devices with their start and end apart: 3 -> 3, of which waited for: 3 -> 2; matrix products, arithmetic and copies ran while one was open for 3% -> 26% of each run, Pallas kernels for 0% -> 0%
where the time goes in v1:
time: 504 us; the launch traced here: 503 us
  waiting for transfers between devices  210 us (42%)
  local copies, waits for them, and re-layouts  116 us (23%)
  matrix products  111 us (22%)
  other arithmetic  27 us (5%)
  Pallas kernels  22.2 us (4%)
  between operations  14.1 us (3%)
    all_gather x1, waiting for transfers between devices, on_device(): lax.all_gather(scaled_own, 'grp', axis=0, tiled=True)  112 us
    all_gather x1, waiting for transfers between devices, on_device(): both_every = lax.all_gather(both_own, 'grp', axis=0, tiled=True)  98.7 us
    dot_general x36, matrix products, orbitals(): values = jnp.dot(hidden, w_out, precision=lax.Precision.HIGHEST)  65.5 us
    dot_general x36, matrix products, orbitals(): jnp.dot(gated, w_hidden, preferred_element_type=jnp.float32) + bias_hidden  41.3 us
    add x18, local copies, waits for them, and re-layouts, orbitals(): left_part.astype(jnp.float32)[:, None, :]  24.1 us
    pallas_call x1, Pallas kernels, factor_augmented(): pl.pallas_call(factor_kernel, out_shape=jax.ShapeDtypeStruct(matrix.shape...  22.2 us
    reshape x1, local copies, waits for them, and re-layouts, on_device(): pairs = factored[:panel].reshape(panel // 2, 2, panel // 2, 2)  18.1 us
    mul x1, local copies, waits for them, and re-layouts, on_device(): block = block_rows + jnp.kron(jnp.diag(pair_strength), pattern)  12.7 us
  transfers between devices with their start and end apart: 3, of which 2 were waited for; matrix products, arithmetic and copies ran while one was open for 26% of the time, Pallas kernels for 0%

profile of v1, /device:TPU:6, one launch (start us, length us, event | category | flops | bytes accessed | tf_op | source)
XLA Modules:
  0.0 503.2 jit_solution(2773539052331956030)
XLA Ops:
  10.5 7.3 %broadcast_multiply_fusion = f32[128,2,128,2]{3,2,1,0:T(8,128)} fusion(f32[2,2]{1,0:T(2,128)} %constant.98.clone, f32[128,128]{1,0:T(8,128)S(1)} %fusion.48), kind=kLoop, calls=%fused_computation.65 | loop fusion | flops 65536 | bytes 327696 | tf_op jit(solution)/shard_map/jit(kron)/mul | solution.py:116
  17.7 12.7 %mul.68 = f32[256,256]{1,0:T(8,128)S(1)} reshape(f32[128,2,128,2]{3,2,1,0:T(8,128)} %broadcast_multiply_fusion) | data formatting | bytes 524288 | tf_op jit(solution)/shard_map/jit(kron)/mul | solution.py:116
  31.1 98.7 %all-gather.6.cloned.1.call-done = bf16[2048,512]{1,0:T(8,128)(2,1)} async-done(((bf16[16,512]{1,0:T(8,128)(2,1)}), bf16[2048,512]{1,0:T(8,128)(2,1)}) %all-gather.6.cloned.1.call-update) | async-done | bytes 2097168 | tf_op jit(solution)/shard_map/all_gather | solution.py:95
  129.8 9.4 %gather_fusion = bf16[2048,512]{1,0:T(8,128)(2,1)S(1)} fusion(bf16[2048,512]{1,0:T(8,128)(2,1)} %all-gather.6.cloned.1.call-done, s32[2048]{0:T(1024)S(1)} %fusion.49), kind=kCustom, calls=%fused_computation | custom fusion | bytes 4202496 | tf_op jit(solution)/shard_map/jit(_take)/gather | solution.py:96
  140.6 59.8 %while.42 = (s32[]{:T(128)}, f32[16,14,128]{2,1,0:T(8,128)}, bf16[14,256]{1,0:T(8,128)(2,1)S(1)}, bf16[16,128,256]{2,1,0:T(8,128)(2,1)S(1)}, f32[256]{0:T(256)S(...) while((s32[]{:T(128)}, f32[16,14,128]{2,1,0:T(8,128)}, ...), condition=%wide.region_5.6_spmd, body=%wide.region_4.5_spmd.sunk | while | flops 245927424 | bytes 9695841 | solution.py:29
  200.5 2.2 while.41
  205.2 117.8 %while.43 = (s32[]{:T(128)}, f32[16,128,14]{2,1,0:T(8,128)}, bf16[16,128,256]{2,1,0:T(8,128)(2,1)S(1)}, bf16[14,256]{1,0:T(8,128)(2,1)S(1)}, f32[256]{0:T(256)S(...) while((s32[]{:T(128)}, f32[16,128,14]{2,1,0:T(8,128)}, ...), condition=%wide.region_7.8_spmd, body=%wide.region_6.7_spmd.sunk | while | flops 245927424 | bytes 11676425 | solution.py:37
  207.6 2.1 convolution_add_fusion.11
  214.9 2.1 convolution_add_fusion.11
  222.3 2.1 convolution_add_fusion.11
  229.7 2.1 convolution_add_fusion.11
  237.0 2.1 convolution_add_fusion.11
  251.7 2.1 convolution_add_fusion.11
  259.1 2.1 convolution_add_fusion.11
  281.2 2.1 convolution_add_fusion.11
  288.5 2.1 convolution_add_fusion.11
  295.9 2.1 convolution_add_fusion.11
  310.6 2.1 convolution_add_fusion.11
  318.0 2.1 convolution_add_fusion.11
  327.9 22.2 %shard_map.121 = f32[272,256]{1,0:T(8,128)} custom-call(f32[272,256]{1,0:T(8,128)} %maximum_maximum_fusion.m_in_ref), custom_call_target="tpu_custom_call" | custom-call | tf_op jit(solution)/shard_map/pallas_call | solution.py:69
  352.1 18.1 %reshape.143 = f32[128,2,128,2]{3,2,1,0:T(8,128)} reshape(f32[256,256]{1,0:T(8,128)S(1)} %slice.60) | data formatting | bytes 524288 | tf_op jit(solution)/shard_map/reshape | solution.py:124
  370.1 7.8 %slice_reduce_fusion = f32[128,128]{1,0:T(8,128)S(1)} fusion(f32[128,2,128,2]{3,2,1,0:T(8,128)} %reshape.143), kind=kLoop, calls=%fused_computation.64 | loop fusion | bytes 131072 | tf_op jit(solution)/shard_map/slice | solution.py:125
  380.9 111.7 %all-gather.10.cloned.1.call-done = f32[128,14,256]{2,1,0:T(8,128)} async-done(((f32[1,14,256]{2,1,0:T(8,128)}), f32[128,14,256]{2,1,0:T(8,128)}) %all-gather.10.cloned.1.call-update) | async-done | bytes 1835024 | tf_op jit(solution)/shard_map/all_gather | solution.py:131
  494.3 2.3 convolution_subtract_fusion
  (519 shorter events, 172.5 us)
Async XLA Ops:
  7.2 122.6 %all-gather.6.cloned.1.call-start = ((), (), s32[]{:S(2)}) async-start(), calls=%async_computation | async-start | bytes 2113536 | tf_op jit(solution)/shard_map/all_gather | solution.py:95
  9.6 316.0 %all-gather.8.cloned.1.call-start = ((), (), s32[]{:S(2)}) async-start(), calls=%async_computation.1 | async-start | bytes 1056768 | tf_op jit(solution)/shard_map/all_gather | solution.py:110
  17.7 13.4 %copy-start.10 = (s32[2048]{0:T(1024)S(1)}, s32[2048]{0:T(1024)}, u32[]{:S(2)}) copy-start(s32[2048]{0:T(1024)} %param.19) | copy-start | bytes 24580
  140.6 59.9 %copy-start.5 = (f32[2,128,2]{2,1,0:T(8,128)S(1)}, f32[2,128,2]{2,1,0:T(8,128)}, u32[]{:S(2)}) copy-start(f32[2,128,2]{2,1,0:T(8,128)} %custom-call.5) | copy-start | bytes 6148
  204.9 287.8 %all-gather.10.cloned.1.call-start = ((), (), s32[]{:S(2)}) async-start(), calls=%async_computation.2 | async-start | bytes 2113536 | tf_op jit(solution)/shard_map/all_gather | solution.py:131
  209.7 2.8 copy-start.3
  209.7 2.8 copy-start.9
  217.1 2.8 copy-start.3
  224.4 2.8 copy-start.3
  231.8 2.8 copy-start.3
  231.8 2.8 copy-start.9
  239.2 2.8 copy-start.3
  239.2 2.8 copy-start.9
  246.5 2.8 copy-start.3
  253.9 2.8 copy-start.3
  268.6 2.8 copy-start.3
  276.0 2.8 copy-start.3
  283.3 2.8 copy-start.3
  298.1 2.8 copy-start.3
  305.4 2.8 copy-start.3
  312.8 2.8 copy-start.3
  320.1 2.8 copy-start.3
  322.9 4.2 copy-start.11
  350.9 143.5 %copy-start.4 = (f32[14,256]{1,0:T(8,128)}, f32[14,256]{1,0:T(8,128)S(1)}, u32[]{:S(2)}) copy-start(f32[14,256]{1,0:T(8,128)S(1)} %slice.62) | copy-start | bytes 43012
  (85 other events, 111.5 us)
Sparse Core Ops, SparseCore 0:
  12.0 117.7 all-gather.5
  205.0 99.9 all-gather.7
  380.5 112.0 all-gather.9

commit v2 on v1

v2 whole, which is shorter than its diff:
```python
import numpy as np
import jax
import jax.numpy as jnp
from jax import lax
from jax.experimental import pallas as pl
from jax.experimental.pallas import tpu as pltpu
from jax.sharding import Mesh
from jax.sharding import PartitionSpec as P


def silu(v):
    half = 0.5 * v
    return half * (1.0 + jnp.tanh(half))


def orbital_kernel(col_ref, mat_ref, bias_in_ref, w_hid_t_ref, bias_hid_ref, w_out_ref, out_ref):
    rows = col_ref.shape[1]
    bias_in = bias_in_ref[...]
    bias_hid = bias_hid_ref[...]
    w_out = w_out_ref[...]
    w_hid_t = w_hid_t_ref[...]

    def one(d, r):
        pre = (col_ref[d, r] + mat_ref[d]) + bias_in
        gated = silu(pre).astype(jnp.bfloat16)
        hidden = jnp.dot(w_hid_t, gated, preferred_element_type=jnp.float32)
        hidden = silu(hidden + bias_hid)
        return jnp.sum(hidden * w_out, axis=0, keepdims=True)

    def body(r, carry):
        out_ref[pl.ds(r, 1), :] = one(0, r) - one(1, r)
        return carry

    lax.fori_loop(0, rows, body, 0)


def orbital_rows(cols, mats, bias_in, w_hid_t, bias_hid, w_out):
    _, rows, feat, _ = cols.shape
    count = mats.shape[2]
    width = min(count, 256)
    flops = 2 * rows * count * (2 * feat * feat + 12 * feat)
    return pl.pallas_call(
        orbital_kernel,
        grid=(count // width,),
        out_shape=jax.ShapeDtypeStruct((rows, count), jnp.float32),
        in_specs=[
            pl.BlockSpec((2, rows, feat, 1), lambda j: (0, 0, 0, 0)),
            pl.BlockSpec((2, feat, width), lambda j: (0, 0, j)),
            pl.BlockSpec((feat, 1), lambda j: (0, 0)),
            pl.BlockSpec((feat, feat), lambda j: (0, 0)),
            pl.BlockSpec((feat, 1), lambda j: (0, 0)),
            pl.BlockSpec((feat, 1), lambda j: (0, 0)),
        ],
        out_specs=pl.BlockSpec((rows, width), lambda j: (0, j)),
        cost_estimate=pl.CostEstimate(
            flops=flops,
            transcendentals=4 * rows * count * feat,
            bytes_accessed=4 * (2 * feat * count + rows * count),
        ),
    )(cols, mats, bias_in, w_hid_t, bias_hid, w_out)


def factor_kernel(m_in_ref, ps_ref, pc_ref, piv_ref, scaled_ref, m_ref):
    rows, size = m_ref.shape
    lane = lax.broadcasted_iota(jnp.int32, (1, size), 1)
    lanes = lax.broadcasted_iota(jnp.int32, (rows, size), 1)
    row_idx = lax.broadcasted_iota(jnp.int32, (rows, 1), 0)
    m0 = m_in_ref[...]
    strength = ps_ref[...]
    m0 = m0 + jnp.where((row_idx % 2 == 0) & (lanes == row_idx + 1) & (row_idx < size), strength, 0.0)
    m0 = m0 - jnp.where((row_idx % 2 == 1) & (lanes == row_idx - 1) & (row_idx < size), strength, 0.0)
    m_ref[...] = m0
    below = rows - size

    def step(k, carry):
        pivots, scaled = carry
        first = 2 * k
        r0 = m_ref[pl.ds(first, 1), :]
        r1 = m_ref[pl.ds(first + 1, 1), :]
        pivot = jnp.sum(jnp.where(lane == first + 1, r0, 0.0), axis=1, keepdims=True)
        keep_lane = lane > first + 1
        even_lane = jnp.where(keep_lane, -r0 / pivot, 0.0)
        odd_lane = jnp.where(keep_lane, -r1 / pivot, 0.0)
        m = m_ref[...]
        col_even = jnp.sum(jnp.where(lanes == first, m, 0.0), axis=1, keepdims=True)
        col_odd = jnp.sum(jnp.where(lanes == first + 1, m, 0.0), axis=1, keepdims=True)
        low_even = col_even[size:]
        low_odd = col_odd[size:]
        low_lanes = lanes[size:]
        scaled = jnp.where(low_lanes == first, low_odd / pivot, scaled)
        scaled = jnp.where(low_lanes == first + 1, -low_even / pivot, scaled)
        pivots = jnp.where(lane == k, pivot, pivots)
        keep_row = row_idx > first + 1
        col_even = jnp.where(keep_row, col_even, 0.0)
        col_odd = jnp.where(keep_row, col_odd, 0.0)
        m_ref[...] = m + (col_odd * even_lane - col_even * odd_lane)
        return (pivots, scaled)

    start = (jnp.zeros((1, size), jnp.float32), jnp.zeros((below, size), jnp.float32))
    pivots, scaled = lax.fori_loop(0, size // 2, step, start)
    pc_ref[...] = m_ref[size:, :]
    piv_ref[...] = pivots
    scaled_ref[...] = scaled


def factor_augmented(matrix, strength_col, size):
    rows, width = matrix.shape
    below = rows - size
    vmem = pl.BlockSpec(memory_space=pltpu.VMEM)
    return pl.pallas_call(
        factor_kernel,
        out_shape=(
            jax.ShapeDtypeStruct((below, width), jnp.float32),
            jax.ShapeDtypeStruct((1, width), jnp.float32),
            jax.ShapeDtypeStruct((below, width), jnp.float32),
        ),
        in_specs=[vmem, vmem],
        out_specs=(vmem, vmem, vmem),
        scratch_shapes=[pltpu.VMEM((rows, width), jnp.float32)],
    )(matrix, strength_col)


def gather_rows(x, stages):
    for axes in stages:
        x = lax.all_gather(x, axes, axis=0, tiled=True)
    return x


def make_on_device(stages, grp_axes):
    def on_device(feats, perm, w_left, w_right, bias_in, w_hidden, bias_hidden, w_out, pair_strength):
        groups = lax.psum(1, grp_axes)
        device = lax.axis_index(grp_axes)
        electrons = perm.shape[0]
        hid = w_left.shape[1]
        panel = 2 * pair_strength.shape[0]
        share = panel // groups
        tail = (electrons - panel) // groups
        w_both = jnp.concatenate([w_left, w_right], axis=1)
        both_own = jnp.dot(feats, w_both, preferred_element_type=jnp.float32).astype(jnp.bfloat16)
        both_every = gather_rows(both_own, stages)
        both_all = jnp.take(both_every, perm, axis=0).astype(jnp.float32)
        mats = jnp.stack([both_all[:, hid:].T, both_all[:, :hid].T])
        params = (
            bias_in[:, None],
            w_hidden.T,
            bias_hidden[:, None],
            w_out[:, None],
        )
        top_start = device * share
        tail_start = panel + device * tail
        top_own = lax.dynamic_slice_in_dim(both_all, top_start, share, 0)
        tail_own = lax.dynamic_slice_in_dim(both_all, tail_start, tail, 0)
        top_cols = jnp.stack([top_own[:, :hid], top_own[:, hid:]])[..., None]
        tail_cols = jnp.stack([tail_own[:, :hid], tail_own[:, hid:]])[..., None]
        top_rows = orbital_rows(top_cols, mats[:, :, :panel], *params)
        pad = (-share) % 8
        top_padded = jnp.pad(top_rows, ((0, pad), (0, 0)))
        gathered = gather_rows(top_padded, stages)
        block_rows = gathered.reshape(groups, share + pad, panel)[:, :share, :].reshape(panel, panel)
        tail_rows = orbital_rows(tail_cols, mats, *params)
        below_own = tail_rows[:, :panel]
        trailing_own = tail_rows[:, panel:]
        extra = (-tail) % 8
        augmented = jnp.concatenate(
            [block_rows, below_own, jnp.zeros((extra, panel), jnp.float32)], axis=0
        )
        strength_col = jnp.concatenate(
            [jnp.repeat(pair_strength, 2), jnp.zeros((tail + extra,), jnp.float32)]
        )[:, None]
        pc, piv_row, scaled = factor_augmented(augmented, strength_col, panel)
        pivots = piv_row[0, : panel // 2]
        log_pivot = jnp.log(jnp.abs(pivots))
        panel_own = pc[:tail]
        scaled_own = scaled[:tail]
        schur = trailing_own - jnp.dot(
            panel_own,
            gather_rows(scaled_own, stages).T,
            precision=lax.Precision.HIGHEST,
        )
        return (log_pivot, panel_own, schur)

    return on_device


def split_grp(mesh):
    devs = mesh.devices
    try:
        coords = np.array([[d.coords[2], d.coords[0], d.coords[1]] for d in devs[0]])
        sizes = tuple(len(np.unique(coords[:, i])) for i in range(3))
        grid = coords.reshape(sizes + (3,))
        ok = int(np.prod(sizes)) == devs.shape[1]
        for i in range(3):
            idx = np.arange(sizes[i]).reshape([-1 if j == i else 1 for j in range(3)])
            ok = ok and bool(np.all(grid[..., i] == idx))
    except Exception:
        ok = False
    if not ok:
        return None
    return Mesh(devs.reshape((devs.shape[0],) + sizes), ("walker", "z", "x", "y"))


def solution(mesh):
    split = split_grp(mesh)
    if split is None:
        use, grp_axes, stages = mesh, "grp", ("grp",)
    else:
        use, grp_axes, stages = split, ("z", "x", "y"), (("x", "y"), "z")
    rows = ("walker",) + ((grp_axes,) if isinstance(grp_axes, str) else grp_axes)
    return jax.shard_map(
        make_on_device(stages, grp_axes),
        mesh=use,
        in_specs=(P(rows, None), P("walker"), P(), P(), P(), P(), P(), P(), P()),
        out_specs=(P("walker"), P(rows, None), P(rows, None)),
        check_vma=False,
    )
```

time: 504 us -> 291 us (0.58)
  waiting for transfers between devices: 210 us -> 71.6 us
  matrix products: 111 us -> 4.88 us
  local copies, waits for them, and re-layouts: 116 us -> 31.9 us
  blocking collectives: 0 us -> 72.5 us
  Pallas kernels: 22.2 us -> 84.5 us
  other arithmetic: 27 us -> 11.4 us
    all_gather x3, waiting for transfers between devices: 210 us -> 71.5 us  [gather_rows(): x = lax.all_gather(x, axes, axis=0, tiled=True)]
    dot_general x73 -> x1, matrix products: 109 us -> 3.76 us  [on_device(): jnp.dot(panel_own, gather_rows(scaled_own, stages).T, precision=lax.Preci...]
    all_gather x0 -> x3, blocking collectives: none -> 72.5 us  [gather_rows(): x = lax.all_gather(x, axes, axis=0, tiled=True)]
    pallas_call x1 -> x3, Pallas kernels: 22.2 us -> 84.5 us  [the longest x2 62.3 us: orbital_rows(): pl.pallas_call(orbital_kernel, grid=(count // width,), out_shape=jax.Shap...]
    add x18 -> x0, local copies, waits for them, and re-layouts: 24.1 us -> none  [orbitals(): left_part.astype(jnp.float32)[:, None, :]]
    dynamic_update_slice x36 -> x0, local copies, waits for them, and re-layouts: 19.8 us -> none  [the longest x18 10.1 us: backward_terms(): result = lax.map(lambda piece: orbitals(piece, right_rows, *params), pieces)]
    reshape x4 -> x2, local copies, waits for them, and re-layouts: 19.9 us -> 0.33 us  [the longest x1 0.18 us: on_device(): gathered.reshape(groups, share + pad, panel)[:, :share, :]]
    mul x1 -> x0, local copies, waits for them, and re-layouts: 12.7 us -> none  [on_device(): block = block_rows + jnp.kron(jnp.diag(pair_strength), pattern)]
  transfers between devices with their start and end apart: 3 -> 3, of which waited for: 2 -> 2; matrix products, arithmetic and copies ran while one was open for 26% -> 6% of each run, Pallas kernels for 0% -> 20%
where the time goes in v2:
time: 291 us
  Pallas kernels  84.5 us (29%)
  blocking collectives  72.5 us (25%)
  waiting for transfers between devices  71.6 us (25%)
  local copies, waits for them, and re-layouts  31.9 us (11%)
  between operations  13.9 us (5%)
  other arithmetic  11.4 us (4%)
  matrix products  4.88 us (2%)
    all_gather x3, blocking collectives, gather_rows(): x = lax.all_gather(x, axes, axis=0, tiled=True)  72.5 us
    all_gather x3, waiting for transfers between devices, gather_rows(): x = lax.all_gather(x, axes, axis=0, tiled=True)  71.5 us
    pallas_call x2, Pallas kernels, orbital_rows(): pl.pallas_call(orbital_kernel, grid=(count // width,), out_shape=jax.Shap...  62.3 us
    pallas_call x1, Pallas kernels, factor_augmented(): pl.pallas_call(factor_kernel, out_shape=(jax.ShapeDtypeStruct((below, wid...  22.2 us
    gather x2, local copies, waits for them, and re-layouts, on_device(): both_all = jnp.take(both_every, perm, axis=0).astype(jnp.float32)  11.9 us
    another operation x2, other arithmetic, on_device(): mats = jnp.stack([both_all[:, hid:].T, both_all[:, :hid].T])  6.11 us
  transfers between devices with their start and end apart: 3, of which 2 were waited for; matrix products, arithmetic and copies ran while one was open for 6% of the time, Pallas kernels for 20%

profile of v2, /device:TPU:6, one launch (start us, length us, event | category | flops | bytes accessed | tf_op | source)
XLA Modules:
  0.0 290.7 jit_solution(15561680310072631293)
XLA Ops:
  7.9 1.1 fusion
  9.0 25.6 %all_gather.18 = bf16[256,512]{1,0:T(8,128)(2,1)} all-gather(bf16[16,512]{1,0:T(8,128)(2,1)S(1)} %fusion), channel_id=1, replica_groups=mesh['walker'=2,'z'=8,'x'=4,'y'=4] {'x','y'}, dimensions={0}, use_global_device_ids=true | all-gather | bytes 278528 | tf_op jit(solution)/shard_map/all_gather | solution.py:125
  34.7 1.5 copy.46.bias_in_ref
  36.1 1.5 copy.47.bias_hid_ref
  37.6 1.5 copy.48.w_out_ref
  39.1 1.7 copy.44
  42.1 34.6 %all-gather.5.cloned.1.call-done = bf16[2048,512]{1,0:T(8,128)(2,1)} async-done(((bf16[256,512]{1,0:T(8,128)(2,1)}), bf16[2048,512]{1,0:T(8,128)(2,1)}) %all-gather.5.cloned.1.call-update) | async-done | bytes 2097168 | tf_op jit(solution)/shard_map/all_gather | solution.py:125
  76.7 9.4 %gather_fusion = bf16[2048,512]{1,0:T(8,128)(2,1)S(1)} fusion(bf16[2048,512]{1,0:T(8,128)(2,1)} %all-gather.5.cloned.1.call-done, s32[2048]{0:T(1024)S(1)} %fusion.5), kind=kCustom, calls=%fused_computation | custom fusion | bytes 4202496 | tf_op jit(solution)/shard_map/jit(_take)/gather | solution.py:141
  86.2 2.5 copy.41
  88.7 1.9 select_convert_fusion
  90.5 2.0 slice_bitcast_fusion.1
  94.6 1.8 fusion.1.mat_ref
  96.5 3.0 %shard_map.112 = f32[2,256]{1,0:T(2,128)} custom-call(f32[2,2,256,1]{3,2,1,0:T(8,128)} %copy.45.col_ref, f32[2,256,256]{2,1,0:T(8,128)} %fusion.1.mat_ref, f32[256,1]{1,0:T(8,128)} %copy.46.bias_in_ref, bf16[256,256]{1,0:T(8,128)(2,1)} %bitcast.35, f32[256,1]{1,0:T(8,128)} %copy.47.bias_hid_ref, f32[256,1]{1,0:T(8,128)} %copy.48.w_out_ref), custom_call_target="tpu_custom_call" | custom-call | flops 137363456 | bytes 526336 | tf_op jit(solution)/shard_map/pallas_call | solution.py:42
  100.1 25.3 %all_gather.20 = f32[128,256]{1,0:T(8,128)} all-gather(f32[8,256]{1,0:T(8,128)S(1)} %pad.5), channel_id=1, replica_groups=mesh['walker'=2,'z'=8,'x'=4,'y'=4] {'x','y'}, dimensions={0}, use_global_device_ids=true | all-gather | bytes 139264 | tf_op jit(solution)/shard_map/all_gather | solution.py:125
  126.5 1.2 dynamic-slice_bitcast_fusion.1
  127.9 2.4 copy.51.col_ref
  130.3 4.3 %pad_maximum_fusion.mat_ref = f32[2,256,2048]{2,1,0:T(8,128)} fusion(f32[1,256,2048]{2,1,0:T(8,128)} %get-tuple-element.12, f32[1,256,2048]{2,1,0:T(8,128)S(1)} %get-tuple-element.11), kind=kLoop, calls=%fused_computation.2 | loop fusion | flops 1048576 | bytes 8388608 | tf_op jit(solution)/shard_map/stack | solution.py:142
  134.6 59.4 %shard_map.113 = f32[14,2048]{1,0:T(8,128)} custom-call(f32[2,14,256,1]{3,2,1,0:T(8,128)} %copy.51.col_ref, f32[2,256,2048]{2,1,0:T(8,128)} %pad_maximum_fusion.mat_ref, f32[256,1]{1,0:T(8,128)} %copy.46.bias_in_ref, bf16[256,256]{1,0:T(8,128)(2,1)} %bitcast.36, f32[256,1]{1,0:T(8,128)} %copy.47.bias_hid_ref, f32[256,1]{1,0:T(8,128)} %copy.48.w_out_ref), custom_call_target="tpu_custom_call" | custom-call | flops 7692353536 | bytes 4308992 | tf_op jit(solution)/shard_map/pallas_call | solution.py:42
  194.8 1.3 slice.58
  197.1 22.2 %shard_map.114 = (f32[16,256]{1,0:T(8,128)}, f32[1,256]{1,0:T(1,128)}, f32[16,256]{1,0:T(8,128)}) custom-call(f32[272,256]{1,0:T(8,128)} %maximum_maximum_fusion.m_in_ref, f32[272,1]{1,0:T(8,128)} %broadcast_in_dim.47.ps_ref), custom_call_target="tpu_custom_call" | custom-call | tf_op jit(solution)/shard_map/pallas_call | solution.py:110
  220.0 21.6 %all-gather = f32[16,14,256]{2,1,0:T(8,128)S(1)} all-gather(f32[1,14,256]{2,1,0:T(8,128)S(1)} %slice_bitcast_fusion.2), channel_id=1, replica_groups=mesh['walker'=2,'z'=8,'x'=4,'y'=4] {'x','y'}, dimensions={0}, use_global_device_ids=true | all-gather | bytes 243712 | tf_op jit(solution)/shard_map/all_gather | solution.py:125
  242.3 1.2 log_bitcast_fusion
  243.5 36.9 %all-gather.9.cloned.1.call-done = f32[1792,256]{1,0:T(8,128)} async-done(((f32[224,256]{1,0:T(8,128)}), f32[1792,256]{1,0:T(8,128)}) %all-gather.9.cloned.1.call-update) | async-done | bytes 1835024 | tf_op jit(solution)/shard_map/all_gather | solution.py:125
  280.4 3.8 %convolution_subtract_fusion = f32[14,1792]{1,0:T(8,128)} fusion(f32[14,256]{1,0:T(8,128)} %bitcast.38, f32[1792,256]{1,0:T(8,128)} %all-gather.9.cloned.1.call-done, f32[14,2048]{1,0:T(8,128)S(1)} %copy-done.2), kind=kOutput, calls=%fused_computation.4 | convolution fusion | flops 77095424 | bytes 2050048 | tf_op jit(solution)/shard_map/dot_general | solution.py:175
  (37 shorter events, 9.5 us)
Async XLA Ops:
  7.2 0.7 copy-start
  7.2 69.6 %all-gather.5.cloned.1.call-start = ((), (), s32[]{:S(2)}) async-start(), calls=%async_computation | async-start | bytes 2359296 | tf_op jit(solution)/shard_map/all_gather | solution.py:125
  34.6 160.2 %all-gather.7.cloned.1.call-start = ((), (), s32[]{:S(2)}) async-start(), calls=%async_computation.1 | async-start | bytes 1179648 | tf_op jit(solution)/shard_map/all_gather | solution.py:125
  90.5 2.7 copy-start.1
  94.6 30.8 %copy-start.3 = (f32[128]{0:T(128)S(1)}, f32[128]{0:T(128)}, u32[]{:S(2)}) copy-start(f32[128]{0:T(128)} %param.17) | copy-start | bytes 1540
  125.4 155.0 %all-gather.9.cloned.1.call-start = ((), (), s32[]{:S(2)}) async-start(), calls=%async_computation.2 | async-start | bytes 2064384 | tf_op jit(solution)/shard_map/all_gather | solution.py:125
  194.0 86.4 %copy-start.2 = (f32[14,2048]{1,0:T(8,128)S(1)}, f32[14,2048]{1,0:T(8,128)}, u32[]{:S(2)}) copy-start(f32[14,2048]{1,0:T(8,128)} %shard_map.113) | copy-start | bytes 344068
Sparse Core Ops, SparseCore 0:
  34.7 41.9 all-gather.4
  125.5 35.1 all-gather.6
  242.4 37.8 all-gather.8

commit v3 on v2

--- a/solution.py
+++ b/solution.py
@@ -8,12 +8,8 @@
 from jax.sharding import PartitionSpec as P
 
 
-def silu(v):
-    half = 0.5 * v
-    return half * (1.0 + jnp.tanh(half))
-
-
-def orbital_kernel(col_ref, mat_ref, bias_in_ref, w_hid_t_ref, bias_hid_ref, w_out_ref, out_ref):
+def orbital_kernel(col_ref, mat_ref, bias_in_ref, w_hid_t_ref, bias_hid_ref, w_out_ref, *rest):
+    out_ref = rest[-1]
     rows = col_ref.shape[1]
     bias_in = bias_in_ref[...]
     bias_hid = bias_hid_ref[...]
@@ -21,11 +17,10 @@
     w_hid_t = w_hid_t_ref[...]
 
     def one(d, r):
-        pre = (col_ref[d, r] + mat_ref[d]) + bias_in
-        gated = silu(pre).astype(jnp.bfloat16)
-        hidden = jnp.dot(w_hid_t, gated, preferred_element_type=jnp.float32)
-        hidden = silu(hidden + bias_hid)
-        return jnp.sum(hidden * w_out, axis=0, keepdims=True)
+        half = (col_ref[d, r] + mat_ref[d]) + bias_in
+        gated = (half * (1.0 + jnp.tanh(half))).astype(jnp.bfloat16)
+        half = jnp.dot(w_hid_t, gated, preferred_element_type=jnp.float32) + bias_hid
+        return jnp.sum(half * (1.0 + jnp.tanh(half)) * w_out, axis=0, keepdims=True)
 
     def body(r, carry):
         out_ref[pl.ds(r, 1), :] = one(0, r) - one(1, r)
@@ -34,33 +29,37 @@
     lax.fori_loop(0, rows, body, 0)
 
 
-def orbital_rows(cols, mats, bias_in, w_hid_t, bias_hid, w_out):
+def orbital_rows(cols, mats, params, first, blocks, width, after=None):
     _, rows, feat, _ = cols.shape
-    count = mats.shape[2]
-    width = min(count, 256)
+    count = blocks * width
     flops = 2 * rows * count * (2 * feat * feat + 12 * feat)
+    operands = [cols, mats, *params]
+    in_specs = [
+        pl.BlockSpec((2, rows, feat, 1), lambda j: (0, 0, 0, 0)),
+        pl.BlockSpec((2, feat, width), lambda j: (0, 0, j + first)),
+        pl.BlockSpec((feat, 1), lambda j: (0, 0)),
+        pl.BlockSpec((feat, feat), lambda j: (0, 0)),
+        pl.BlockSpec((feat, 1), lambda j: (0, 0)),
+        pl.BlockSpec((feat, 1), lambda j: (0, 0)),
+    ]
+    if after is not None:
+        operands.append(after)
+        in_specs.append(pl.BlockSpec(after.shape, lambda j: (0, 0)))
     return pl.pallas_call(
         orbital_kernel,
-        grid=(count // width,),
+        grid=(blocks,),
         out_shape=jax.ShapeDtypeStruct((rows, count), jnp.float32),
-        in_specs=[
-            pl.BlockSpec((2, rows, feat, 1), lambda j: (0, 0, 0, 0)),
-            pl.BlockSpec((2, feat, width), lambda j: (0, 0, j)),
-            pl.BlockSpec((feat, 1), lambda j: (0, 0)),
-            pl.BlockSpec((feat, feat), lambda j: (0, 0)),
-            pl.BlockSpec((feat, 1), lambda j: (0, 0)),
-            pl.BlockSpec((feat, 1), lambda j: (0, 0)),
-        ],
+        in_specs=in_specs,
         out_specs=pl.BlockSpec((rows, width), lambda j: (0, j)),
         cost_estimate=pl.CostEstimate(
             flops=flops,
             transcendentals=4 * rows * count * feat,
             bytes_accessed=4 * (2 * feat * count + rows * count),
         ),
-    )(cols, mats, bias_in, w_hid_t, bias_hid, w_out)
-
-
-def factor_kernel(m_in_ref, ps_ref, pc_ref, piv_ref, scaled_ref, m_ref):
+    )(*operands)
+
+
+def factor_kernel(m_in_ref, ps_ref, after_ref, pc_ref, piv_ref, scaled_ref, m_ref):
     rows, size = m_ref.shape
     lane = lax.broadcasted_iota(jnp.int32, (1, size), 1)
     lanes = lax.broadcasted_iota(jnp.int32, (rows, size), 1)
@@ -103,7 +102,7 @@
     scaled_ref[...] = scaled
 
 
-def factor_augmented(matrix, strength_col, size):
+def factor_augmented(matrix, strength_col, size, after):
     rows, width = matrix.shape
     below = rows - size
     vmem = pl.BlockSpec(memory_space=pltpu.VMEM)
@@ -114,10 +113,10 @@
             jax.ShapeDtypeStruct((1, width), jnp.float32),
             jax.ShapeDtypeStruct((below, width), jnp.float32),
         ),
-        in_specs=[vmem, vmem],
+        in_specs=[vmem, vmem, vmem],
         out_specs=(vmem, vmem, vmem),
         scratch_shapes=[pltpu.VMEM((rows, width), jnp.float32)],
-    )(matrix, strength_col)
+    )(matrix, strength_col, after)
 
 
 def gather_rows(x, stages):
@@ -139,27 +138,30 @@
         both_own = jnp.dot(feats, w_both, preferred_element_type=jnp.float32).astype(jnp.bfloat16)
         both_every = gather_rows(both_own, stages)
         both_all = jnp.take(both_every, perm, axis=0).astype(jnp.float32)
-        mats = jnp.stack([both_all[:, hid:].T, both_all[:, :hid].T])
+        halves = 0.5 * both_all
+        mats = jnp.stack([halves[:, hid:].T, halves[:, :hid].T])
         params = (
-            bias_in[:, None],
-            w_hidden.T,
-            bias_hidden[:, None],
+            0.5 * bias_in[:, None],
+            (w_hidden.T * 0.5).astype(w_hidden.dtype),
+            0.5 * bias_hidden[:, None],
             w_out[:, None],
         )
+        width = panel
         top_start = device * share
         tail_start = panel + device * tail
-        top_own = lax.dynamic_slice_in_dim(both_all, top_start, share, 0)
-        tail_own = lax.dynamic_slice_in_dim(both_all, tail_start, tail, 0)
+        top_own = lax.dynamic_slice_in_dim(halves, top_start, share, 0)
+        tail_own = lax.dynamic_slice_in_dim(halves, tail_start, tail, 0)
         top_cols = jnp.stack([top_own[:, :hid], top_own[:, hid:]])[..., None]
         tail_cols = jnp.stack([tail_own[:, :hid], tail_own[:, hid:]])[..., None]
-        top_rows = orbital_rows(top_cols, mats[:, :, :panel], *params)
+        top_rows = orbital_rows(top_cols, mats, params, 0, 1, width)
         pad = (-share) % 8
         top_padded = jnp.pad(top_rows, ((0, pad), (0, 0)))
         gathered = gather_rows(top_padded, stages)
         block_rows = gathered.reshape(groups, share + pad, panel)[:, :share, :].reshape(panel, panel)
-        tail_rows = orbital_rows(tail_cols, mats, *params)
-        below_own = tail_rows[:, :panel]
-        trailing_own = tail_rows[:, panel:]
+        blocks = electrons // width
+        early = (blocks - 1) // 2
+        below_own = orbital_rows(tail_cols, mats, params, 0, 1, width)
+        trailing_a = orbital_rows(tail_cols, mats, params, 1, early, width)
         extra = (-tail) % 8
         augmented = jnp.concatenate(
             [block_rows, below_own, jnp.zeros((extra, panel), jnp.float32)], axis=0
@@ -167,14 +169,19 @@
         strength_col = jnp.concatenate(
             [jnp.repeat(pair_strength, 2), jnp.zeros((tail + extra,), jnp.float32)]
         )[:, None]
-        pc, piv_row, scaled = factor_augmented(augmented, strength_col, panel)
+        pc, piv_row, scaled = factor_augmented(augmented, strength_col, panel, trailing_a[:8, :128])
         pivots = piv_row[0, : panel // 2]
         log_pivot = jnp.log(jnp.abs(pivots))
         panel_own = pc[:tail]
         scaled_own = scaled[:tail]
+        scaled_all = gather_rows(scaled_own, stages)
+        trailing_b = orbital_rows(
+            tail_cols, mats, params, 1 + early, blocks - 1 - early, width, after=piv_row
+        )
+        trailing_own = jnp.concatenate([trailing_a, trailing_b], axis=1)
         schur = trailing_own - jnp.dot(
             panel_own,
-            gather_rows(scaled_own, stages).T,
+            scaled_all.T,
             precision=lax.Precision.HIGHEST,
         )
         return (log_pivot, panel_own, schur)

time: 291 us -> 263 us (0.904)
  waiting for transfers between devices: 71.6 us -> 43.3 us
    all_gather x3, waiting for transfers between devices: 71.5 us -> 43.2 us  [gather_rows(): x = lax.all_gather(x, axes, axis=0, tiled=True)]
    mul x0 -> x4, other arithmetic: none -> 4.2 us  [the longest x1 2.18 us: on_device(): halves = 0.5 * both_all]
    broadcast_in_dim x2 -> x0, local copies, waits for them, and re-layouts: 2.92 us -> none  [the longest x1 1.46 us: on_device(): bias_hidden[:, None]]
    another operation x2 -> x1, other arithmetic: 6.11 us -> 4.29 us  [on_device(): mats = jnp.stack([halves[:, hid:].T, halves[:, :hid].T])]
    pallas_call x2 -> x4, Pallas kernels: 62.3 us -> 62.8 us  [orbital_rows(): pl.pallas_call(orbital_kernel, grid=(blocks,), out_shape=jax.ShapeDtypeSt...]
  transfers between devices with their start and end apart: 3 -> 3, of which waited for: 2 -> 2; matrix products, arithmetic and copies ran while one was open for 6% -> 6% of each run, Pallas kernels for 20% -> 23%
where the time goes in v3:
time: 263 us
  Pallas kernels  85 us (32%)
  blocking collectives  72.4 us (28%)
  waiting for transfers between devices  43.3 us (16%)
  local copies, waits for them, and re-layouts  30.3 us (12%)
  between operations  13.9 us (5%)
  other arithmetic  12.6 us (5%)
  matrix products  4.86 us (2%)
    all_gather x3, blocking collectives, gather_rows(): x = lax.all_gather(x, axes, axis=0, tiled=True)  72.4 us
    pallas_call x4, Pallas kernels, orbital_rows(): pl.pallas_call(orbital_kernel, grid=(blocks,), out_shape=jax.ShapeDtypeSt...  62.8 us
    all_gather x3, waiting for transfers between devices, gather_rows(): x = lax.all_gather(x, axes, axis=0, tiled=True)  43.2 us
    pallas_call x1, Pallas kernels, factor_augmented(): pl.pallas_call(factor_kernel, out_shape=(jax.ShapeDtypeStruct((below, wid...  22.2 us
    gather x2, local copies, waits for them, and re-layouts, on_device(): both_all = jnp.take(both_every, perm, axis=0).astype(jnp.float32)  11.9 us
  transfers between devices with their start and end apart: 3, of which 2 were waited for; matrix products, arithmetic and copies ran while one was open for 6% of the time, Pallas kernels for 23%

profile of v3, /device:TPU:6, one launch (start us, length us, event | category | flops | bytes accessed | tf_op | source)
XLA Modules:
  0.0 262.5 jit_solution(1287488778587138921)
XLA Ops:
  7.9 1.1 fusion
  9.0 25.6 %all_gather.18 = bf16[256,512]{1,0:T(8,128)(2,1)} all-gather(bf16[16,512]{1,0:T(8,128)(2,1)S(1)} %fusion), channel_id=1, replica_groups=mesh['walker'=2,'z'=8,'x'=4,'y'=4] {'x','y'}, dimensions={0}, use_global_device_ids=true | all-gather | bytes 278528 | tf_op jit(solution)/shard_map/all_gather | solution.py:124
  37.6 1.5 copy.64.w_out_ref
  42.2 34.6 %all-gather.5.cloned.1.call-done = bf16[2048,512]{1,0:T(8,128)(2,1)} async-done(((bf16[256,512]{1,0:T(8,128)(2,1)}), bf16[2048,512]{1,0:T(8,128)(2,1)}) %all-gather.5.cloned.1.call-update) | async-done | bytes 2097168 | tf_op jit(solution)/shard_map/all_gather | solution.py:124
  76.8 9.4 %gather_fusion = bf16[2048,512]{1,0:T(8,128)(2,1)S(1)} fusion(bf16[2048,512]{1,0:T(8,128)(2,1)} %all-gather.5.cloned.1.call-done, s32[2048]{0:T(1024)S(1)} %fusion.4), kind=kCustom, calls=%fused_computation | custom fusion | bytes 4202496 | tf_op jit(solution)/shard_map/jit(_take)/gather | solution.py:140
  86.2 2.5 copy.57
  88.7 2.2 convert_multiply_fusion
  90.9 2.1 slice_bitcast_fusion.1
  94.9 4.3 %pad_maximum_fusion.mat_ref = f32[2,256,2048]{2,1,0:T(8,128)} fusion(f32[1,256,2048]{2,1,0:T(8,128)} %get-tuple-element.12, f32[1,256,2048]{2,1,0:T(8,128)S(1)} %get-tuple-element.11), kind=kLoop, calls=%fused_computation.1 | loop fusion | flops 1048576 | bytes 8388608 | tf_op jit(solution)/shard_map/stack | solution.py:142
  99.2 2.9 %shard_map.112 = f32[2,256]{1,0:T(2,128)} custom-call(f32[2,2,256,1]{3,2,1,0:T(8,128)} %copy.61.col_ref, f32[2,256,2048]{2,1,0:T(8,128)} %pad_maximum_fusion.mat_ref, f32[256,1]{1,0:T(8,128)} %copy.62.bias_in_ref, bf16[256,256]{1,0:T(8,128)(2,1)} %multiply_bitcast_fusion.w_hid_t_ref, f32[256,1]{1,0:T(8,128)} %copy.63.bias_hid_ref, f32[256,1]{1,0:T(8,128)} %copy.64.w_out_ref), custom_call_target="tpu_custom_call" | custom-call | flops 137363456 | bytes 526336 | tf_op jit(solution)/shard_map/pallas_call | solution.py:48
  102.8 25.2 %all_gather.20 = f32[128,256]{1,0:T(8,128)} all-gather(f32[8,256]{1,0:T(8,128)S(1)} %pad.5), channel_id=1, replica_groups=mesh['walker'=2,'z'=8,'x'=4,'y'=4] {'x','y'}, dimensions={0}, use_global_device_ids=true | all-gather | bytes 139264 | tf_op jit(solution)/shard_map/all_gather | solution.py:124
  129.2 1.2 dynamic-slice_bitcast_fusion.1
  130.5 2.4 copy.67.col_ref
  132.9 22.1 %shard_map.114 = f32[14,768]{1,0:T(8,128)} custom-call(f32[2,14,256,1]{3,2,1,0:T(8,128)} %copy.67.col_ref, f32[2,256,2048]{2,1,0:T(8,128)} %pad_maximum_fusion.mat_ref, f32[256,1]{1,0:T(8,128)} %copy.62.bias_in_ref, bf16[256,256]{1,0:T(8,128)(2,1)} %multiply_bitcast_fusion.w_hid_t_ref, f32[256,1]{1,0:T(8,128)} %copy.63.bias_hid_ref, f32[256,1]{1,0:T(8,128)} %copy.64.w_out_ref), custom_call_target="tpu_custom_call" | custom-call | flops 2884632576 | bytes 1615872 | tf_op jit(solution)/shard_map/pallas_call | solution.py:48
  155.1 1.3 slice.49.after_ref
  156.3 9.3 %shard_map.113 = f32[14,256]{1,0:T(8,128)} custom-call(f32[2,14,256,1]{3,2,1,0:T(8,128)} %copy.67.col_ref, f32[2,256,2048]{2,1,0:T(8,128)} %pad_maximum_fusion.mat_ref, f32[256,1]{1,0:T(8,128)} %copy.62.bias_in_ref, bf16[256,256]{1,0:T(8,128)(2,1)} %multiply_bitcast_fusion.w_hid_t_ref, f32[256,1]{1,0:T(8,128)} %copy.63.bias_hid_ref, f32[256,1]{1,0:T(8,128)} %copy.64.w_out_ref), custom_call_target="tpu_custom_call" | custom-call | flops 961544192 | bytes 538624 | tf_op jit(solution)/shard_map/pallas_call | solution.py:48
  165.6 1.3 slice.48
  167.1 1.6 maximum_maximum_fusion.m_in_ref
  168.6 22.2 %shard_map.115 = (f32[16,256]{1,0:T(8,128)}, f32[1,256]{1,0:T(1,128)}, f32[16,256]{1,0:T(8,128)}) custom-call(f32[272,256]{1,0:T(8,128)} %maximum_maximum_fusion.m_in_ref, f32[272,1]{1,0:T(8,128)} %broadcast_in_dim.41.ps_ref, f32[8,128]{1,0:T(8,128)} %slice.49.after_ref), custom_call_target="tpu_custom_call" | custom-call | tf_op jit(solution)/shard_map/pallas_call | solution.py:109
  191.6 21.6 %all-gather = f32[16,14,256]{2,1,0:T(8,128)S(1)} all-gather(f32[1,14,256]{2,1,0:T(8,128)S(1)} %slice_bitcast_fusion.2), channel_id=1, replica_groups=mesh['walker'=2,'z'=8,'x'=4,'y'=4] {'x','y'}, dimensions={0}, use_global_device_ids=true | all-gather | bytes 243712 | tf_op jit(solution)/shard_map/all_gather | solution.py:124
  214.0 1.1 log_bitcast_fusion
  215.1 28.6 %shard_map.116 = f32[14,1024]{1,0:T(8,128)} custom-call(f32[2,14,256,1]{3,2,1,0:T(8,128)} %copy.67.col_ref, f32[2,256,2048]{2,1,0:T(8,128)} %pad_maximum_fusion.mat_ref, f32[256,1]{1,0:T(8,128)} %copy.62.bias_in_ref, bf16[256,256]{1,0:T(8,128)(2,1)} %multiply_bitcast_fusion.w_hid_t_ref, f32[256,1]{1,0:T(8,128)} %copy.63.bias_hid_ref, ...), custom_call_target="tpu_custom_call" | custom-call | flops 3846176768 | bytes 2154496 | tf_op jit(solution)/shard_map/pallas_call | solution.py:48
  243.7 8.6 %all-gather.9.cloned.1.call-done = f32[1792,256]{1,0:T(8,128)} async-done(((f32[224,256]{1,0:T(8,128)}), f32[1792,256]{1,0:T(8,128)}) %all-gather.9.cloned.1.call-update) | async-done | bytes 1835024 | tf_op jit(solution)/shard_map/all_gather | solution.py:124
  252.2 3.7 %convolution_subtract_fusion = f32[14,1792]{1,0:T(8,128)} fusion(f32[14,256]{1,0:T(8,128)S(1)} %bitcast.38, f32[1792,256]{1,0:T(8,128)} %all-gather.9.cloned.1.call-done, f32[14,1024]{1,0:T(8,128)} %shard_map.116, f32[14,768]{1,0:T(8,128)S(1)} %copy-done.2), kind=kOutput, calls=%fused_computation.3 | convolution fusion | flops 77120512 | bytes 2050048 | tf_op jit(solution)/shard_map/dot_general | solution.py:182
  (43 shorter events, 12.4 us)
Async XLA Ops:
  7.2 0.7 copy-start
  7.2 69.6 %all-gather.5.cloned.1.call-start = ((), (), s32[]{:S(2)}) async-start(), calls=%async_computation | async-start | bytes 2359296 | tf_op jit(solution)/shard_map/all_gather | solution.py:124
  34.6 131.0 %all-gather.7.cloned.1.call-start = ((), (), s32[]{:S(2)}) async-start(), calls=%async_computation.1 | async-start | bytes 1179648 | tf_op jit(solution)/shard_map/all_gather | solution.py:124
  90.9 2.6 %copy-start.1 = (f32[2048,512]{0,1:T(8,128)}, f32[2048,512]{0,1:T(8,128)S(1)}, u32[]{:S(2)}) copy-start(f32[2048,512]{0,1:T(8,128)S(1)} %convert_multiply_fusion) | copy-start | bytes 12582916
  99.2 28.8 %copy-start.4 = (f32[128]{0:T(128)S(1)}, f32[128]{0:T(128)}, u32[]{:S(2)}) copy-start(f32[128]{0:T(128)} %param.17) | copy-start | bytes 1540
  128.0 124.2 %all-gather.9.cloned.1.call-start = ((), (), s32[]{:S(2)}) async-start(), calls=%async_computation.2 | async-start | bytes 2064384 | tf_op jit(solution)/shard_map/all_gather | solution.py:124
  215.1 37.1 %copy-start.2 = (f32[14,768]{1,0:T(8,128)S(1)}, f32[14,768]{1,0:T(8,128)}, u32[]{:S(2)}) copy-start(f32[14,768]{1,0:T(8,128)} %shard_map.114) | copy-start | bytes 129028
  215.1 37.1 %copy-start.3 = (f32[16,256]{1,0:T(8,128)S(1)}, f32[16,256]{1,0:T(8,128)}, u32[]{:S(2)}) copy-start(f32[16,256]{1,0:T(8,128)} %get-tuple-element.7) | copy-start | bytes 49156
Sparse Core Ops, SparseCore 0:
  34.7 42.0 all-gather.4
  128.1 35.5 all-gather.6
  214.1 38.0 all-gather.8

commit v4 on v3

--- a/solution.py
+++ b/solution.py
@@ -11,16 +11,16 @@
 def orbital_kernel(col_ref, mat_ref, bias_in_ref, w_hid_t_ref, bias_hid_ref, w_out_ref, *rest):
     out_ref = rest[-1]
     rows = col_ref.shape[1]
-    bias_in = bias_in_ref[...]
-    bias_hid = bias_hid_ref[...]
-    w_out = w_out_ref[...]
+    copies = mat_ref.shape[2] // col_ref.shape[3]
     w_hid_t = w_hid_t_ref[...]
 
     def one(d, r):
-        half = (col_ref[d, r] + mat_ref[d]) + bias_in
+        col = col_ref[d, r]
+        col = jnp.concatenate([col] * copies, axis=1) if copies > 1 else col
+        half = (col + mat_ref[d]) + bias_in_ref[...]
         gated = (half * (1.0 + jnp.tanh(half))).astype(jnp.bfloat16)
-        half = jnp.dot(w_hid_t, gated, preferred_element_type=jnp.float32) + bias_hid
-        return jnp.sum(half * (1.0 + jnp.tanh(half)) * w_out, axis=0, keepdims=True)
+        half = jnp.dot(w_hid_t, gated, preferred_element_type=jnp.float32) + bias_hid_ref[...]
+        return jnp.sum(half * (1.0 + jnp.tanh(half)) * w_out_ref[...], axis=0, keepdims=True)
 
     def body(r, carry):
         out_ref[pl.ds(r, 1), :] = one(0, r) - one(1, r)
@@ -30,17 +30,17 @@
 
 
 def orbital_rows(cols, mats, params, first, blocks, width, after=None):
-    _, rows, feat, _ = cols.shape
+    _, rows, feat, lanes = cols.shape
     count = blocks * width
     flops = 2 * rows * count * (2 * feat * feat + 12 * feat)
     operands = [cols, mats, *params]
     in_specs = [
-        pl.BlockSpec((2, rows, feat, 1), lambda j: (0, 0, 0, 0)),
+        pl.BlockSpec((2, rows, feat, lanes), lambda j: (0, 0, 0, 0)),
         pl.BlockSpec((2, feat, width), lambda j: (0, 0, j + first)),
-        pl.BlockSpec((feat, 1), lambda j: (0, 0)),
+        pl.BlockSpec((feat, width), lambda j: (0, 0)),
         pl.BlockSpec((feat, feat), lambda j: (0, 0)),
-        pl.BlockSpec((feat, 1), lambda j: (0, 0)),
-        pl.BlockSpec((feat, 1), lambda j: (0, 0)),
+        pl.BlockSpec((feat, width), lambda j: (0, 0)),
+        pl.BlockSpec((feat, width), lambda j: (0, 0)),
     ]
     if after is not None:
         operands.append(after)
@@ -120,9 +120,15 @@
 
 
 def gather_rows(x, stages):
+    return gather_stages(x, stages)[-1]
+
+
+def gather_stages(x, stages):
+    outs = []
     for axes in stages:
         x = lax.all_gather(x, axes, axis=0, tiled=True)
-    return x
+        outs.append(x)
+    return outs
 
 
 def make_on_device(stages, grp_axes):
@@ -137,26 +143,34 @@
         w_both = jnp.concatenate([w_left, w_right], axis=1)
         both_own = jnp.dot(feats, w_both, preferred_element_type=jnp.float32).astype(jnp.bfloat16)
         both_every = gather_rows(both_own, stages)
-        both_all = jnp.take(both_every, perm, axis=0).astype(jnp.float32)
-        halves = 0.5 * both_all
-        mats = jnp.stack([halves[:, hid:].T, halves[:, :hid].T])
+        width = panel
+        lanes = 128
+
+        def columns(rows_both):
+            stacked = jnp.stack([rows_both[:, :hid], rows_both[:, hid:]])[..., None]
+            return jnp.broadcast_to(stacked, stacked.shape[:-1] + (lanes,))
+
+        def transposed(rows_both):
+            return jnp.stack([rows_both[:, hid:].T, rows_both[:, :hid].T])
+
         params = (
-            0.5 * bias_in[:, None],
+            jnp.broadcast_to(0.5 * bias_in[:, None], (hid, width)),
             (w_hidden.T * 0.5).astype(w_hidden.dtype),
-            0.5 * bias_hidden[:, None],
-            w_out[:, None],
-        )
-        width = panel
-        top_start = device * share
-        tail_start = panel + device * tail
-        top_own = lax.dynamic_slice_in_dim(halves, top_start, share, 0)
-        tail_own = lax.dynamic_slice_in_dim(halves, tail_start, tail, 0)
-        top_cols = jnp.stack([top_own[:, :hid], top_own[:, hid:]])[..., None]
-        tail_cols = jnp.stack([tail_own[:, :hid], tail_own[:, hid:]])[..., None]
-        top_rows = orbital_rows(top_cols, mats, params, 0, 1, width)
+            jnp.broadcast_to(0.5 * bias_hidden[:, None], (hid, width)),
+            jnp.broadcast_to(w_out[:, None], (hid, width)),
+        )
+        top_both = 0.5 * jnp.take(both_every, perm[:panel], axis=0).astype(jnp.float32)
+        top_own = lax.dynamic_slice_in_dim(top_both, device * share, share, 0)
+        top_rows = orbital_rows(columns(top_own), transposed(top_both), params, 0, 1, width)
         pad = (-share) % 8
         top_padded = jnp.pad(top_rows, ((0, pad), (0, 0)))
-        gathered = gather_rows(top_padded, stages)
+        partial = gather_stages(top_padded, stages)
+        gathered = partial[-1]
+        late_every, _ = lax.optimization_barrier((both_every, partial[0]))
+        halves = 0.5 * jnp.take(late_every, perm, axis=0).astype(jnp.float32)
+        mats = transposed(halves)
+        tail_own = lax.dynamic_slice_in_dim(halves, panel + device * tail, tail, 0)
+        tail_cols = columns(tail_own)
         block_rows = gathered.reshape(groups, share + pad, panel)[:, :share, :].reshape(panel, panel)
         blocks = electrons // width
         early = (blocks - 1) // 2

time: 263 us -> 261 us (level)
  Pallas kernels: 85 us -> 76.1 us
  local copies, waits for them, and re-layouts: 30.3 us -> 34.4 us
  waiting for transfers between devices: 43.3 us -> 47.3 us
    pallas_call x4, Pallas kernels: 62.8 us -> 53.9 us  [orbital_rows(): pl.pallas_call(orbital_kernel, grid=(blocks,), out_shape=jax.ShapeDtypeSt...]
    all_gather x3, waiting for transfers between devices: 43.2 us -> 47.3 us  [gather_stages(): x = lax.all_gather(x, axes, axis=0, tiled=True)]
    gather x2 -> x4, local copies, waits for them, and re-layouts: 11.9 us -> 15.3 us  [the longest x2 12.1 us: on_device(): halves = 0.5 * jnp.take(late_every, perm, axis=0).astype(jnp.float32)]
    broadcast_in_dim x3 -> x5, local copies, waits for them, and re-layouts: 4.92 us -> 5.74 us  [the longest x2 3.33 us: columns(): return jnp.broadcast_to(stacked, stacked.shape[:-1] + (lanes,))]
  transfers between devices with their start and end apart: 3 -> 3, of which waited for: 2 -> 2; matrix products, arithmetic and copies ran while one was open for 6% -> 12% of each run, Pallas kernels for 23% -> 20%
where the time goes in v4:
time: 261 us; the launch traced here: 260 us
  Pallas kernels  76.1 us (29%)
  blocking collectives  72.4 us (28%)
  waiting for transfers between devices  47.3 us (18%)
  local copies, waits for them, and re-layouts  34.4 us (13%)
  between operations  13.9 us (5%)
  other arithmetic  11.3 us (4%)
  matrix products  4.86 us (2%)
    all_gather x3, blocking collectives, gather_stages(): x = lax.all_gather(x, axes, axis=0, tiled=True)  72.4 us
    pallas_call x4, Pallas kernels, orbital_rows(): pl.pallas_call(orbital_kernel, grid=(blocks,), out_shape=jax.ShapeDtypeSt...  53.9 us
    all_gather x3, waiting for transfers between devices, gather_stages(): x = lax.all_gather(x, axes, axis=0, tiled=True)  47.3 us
    pallas_call x1, Pallas kernels, factor_augmented(): pl.pallas_call(factor_kernel, out_shape=(jax.ShapeDtypeStruct((below, wid...  22.2 us
    gather x2, local copies, waits for them, and re-layouts, on_device(): halves = 0.5 * jnp.take(late_every, perm, axis=0).astype(jnp.float32)  12.1 us
  transfers between devices with their start and end apart: 3, of which 2 were waited for; matrix products, arithmetic and copies ran while one was open for 12% of the time, Pallas kernels for 20%

profile of v4, /device:TPU:6, one launch (start us, length us, event | category | flops | bytes accessed | tf_op | source)
XLA Modules:
  0.0 260.4 jit_solution(706915672323005546)
XLA Ops:
  7.9 1.1 fusion
  9.0 25.6 %all_gather.18 = bf16[256,512]{1,0:T(8,128)(2,1)} all-gather(bf16[16,512]{1,0:T(8,128)(2,1)S(1)} %fusion), channel_id=1, replica_groups=mesh['walker'=2,'z'=8,'x'=4,'y'=4] {'x','y'}, dimensions={0}, use_global_device_ids=true | all-gather | bytes 278528 | tf_op jit(solution)/shard_map/all_gather | solution.py:129
  35.5 1.0 copy.35
  42.2 34.5 %all-gather.5.cloned.1.call-done = bf16[2048,512]{1,0:T(8,128)(2,1)} async-done(((bf16[256,512]{1,0:T(8,128)(2,1)}), bf16[2048,512]{1,0:T(8,128)(2,1)}) %all-gather.5.cloned.1.call-update) | async-done | bytes 2097168 | tf_op jit(solution)/shard_map/all_gather | solution.py:129
  76.8 3.1 %gather_fusion = bf16[256,512]{1,0:T(8,128)(2,1)S(1)} fusion(bf16[2048,512]{1,0:T(8,128)(2,1)} %all-gather.5.cloned.1.call-done, s32[1024]{0:T(1024)S(1)} %pad_clamp_fusion), kind=kCustom, calls=%fused_computation | custom fusion | bytes 525312 | tf_op jit(solution)/shard_map/jit(_take)/gather | solution.py:162
  84.7 2.8 %shard_map.112 = f32[2,256]{1,0:T(2,128)} custom-call(f32[2,2,256,128]{3,2,1,0:T(8,128)} %broadcast_in_dim.66.col_ref, f32[2,256,256]{2,1,0:T(8,128)} %pad_maximum_fusion.1.mat_ref, f32[256,256]{1,0:T(8,128)} %broadcast_in_dim.67.bias_in_ref, bf16[256,256]{1,0:T(8,128)(2,1)} %multiply_bitcast_fusion.w_hid_t_ref, f32[256,256]{1,0:T(8,128)} %broadcast_in_dim.68.bias_hid_ref, ...), custom_call_target="tpu_custom_call" | custom-call | flops 137363456 | bytes 526336 | tf_op jit(solution)/shard_map/pallas_call | solution.py:48
  88.2 25.1 %all_gather.20 = f32[128,256]{1,0:T(8,128)} all-gather(f32[8,256]{1,0:T(8,128)S(1)} %pad.5), channel_id=1, replica_groups=mesh['walker'=2,'z'=8,'x'=4,'y'=4] {'x','y'}, dimensions={0}, use_global_device_ids=true | all-gather | bytes 139264 | tf_op jit(solution)/shard_map/all_gather | solution.py:129
  113.4 9.2 %gather_fusion.1 = bf16[2048,512]{1,0:T(8,128)(2,1)} fusion(bf16[2048,512]{1,0:T(8,128)(2,1)S(1)} %copy-done.1, s32[2048]{0:T(1024)S(1)} %fusion.4), kind=kCustom, calls=%fused_computation.1 | custom fusion | bytes 4202496 | tf_op jit(solution)/shard_map/jit(_take)/gather | solution.py:170
  122.5 2.9 %copy.36 = bf16[2048,512]{0,1:T(8,128)(2,1)S(1)} copy(bf16[2048,512]{1,0:T(8,128)(2,1)} %gather_fusion.1) | data formatting | bytes 4194304 | tf_op jit(solution)/shard_map/jit(_take)/gather | solution.py:170
  126.1 1.9 copy-done.2
  128.3 2.5 slice_bitcast_fusion.1
  130.8 2.2 pad_maximum_fusion.mat_ref
  133.1 2.3 broadcast_in_dim.73.col_ref
  135.4 18.8 %shard_map.114 = f32[14,768]{1,0:T(8,128)} custom-call(f32[2,14,256,128]{3,2,1,0:T(8,128)} %broadcast_in_dim.73.col_ref, f32[2,256,2048]{2,1,0:T(8,128)} %pad_maximum_fusion.mat_ref, f32[256,256]{1,0:T(8,128)} %broadcast_in_dim.67.bias_in_ref, bf16[256,256]{1,0:T(8,128)(2,1)} %multiply_bitcast_fusion.w_hid_t_ref, f32[256,256]{1,0:T(8,128)} %broadcast_in_dim.68.bias_hid_ref, ...), custom_call_target="tpu_custom_call" | custom-call | flops 2884632576 | bytes 1615872 | tf_op jit(solution)/shard_map/pallas_call | solution.py:48
  154.2 1.3 slice.65.after_ref
  155.5 8.2 %shard_map.113 = f32[14,256]{1,0:T(8,128)} custom-call(f32[2,14,256,128]{3,2,1,0:T(8,128)} %broadcast_in_dim.73.col_ref, f32[2,256,2048]{2,1,0:T(8,128)} %pad_maximum_fusion.mat_ref, f32[256,256]{1,0:T(8,128)} %broadcast_in_dim.67.bias_in_ref, bf16[256,256]{1,0:T(8,128)(2,1)} %multiply_bitcast_fusion.w_hid_t_ref, f32[256,256]{1,0:T(8,128)} %broadcast_in_dim.68.bias_hid_ref, ...), custom_call_target="tpu_custom_call" | custom-call | flops 961544192 | bytes 538624 | tf_op jit(solution)/shard_map/pallas_call | solution.py:48
  163.7 1.3 slice.62
  165.2 1.6 maximum_maximum_fusion.m_in_ref
  166.7 22.2 %shard_map.115 = (f32[16,256]{1,0:T(8,128)}, f32[1,256]{1,0:T(1,128)}, f32[16,256]{1,0:T(8,128)}) custom-call(f32[272,256]{1,0:T(8,128)} %maximum_maximum_fusion.m_in_ref, f32[272,1]{1,0:T(8,128)} %broadcast_in_dim.77.ps_ref, f32[8,128]{1,0:T(8,128)} %slice.65.after_ref), custom_call_target="tpu_custom_call" | custom-call | tf_op jit(solution)/shard_map/pallas_call | solution.py:109
  189.7 21.7 %all-gather = f32[16,14,256]{2,1,0:T(8,128)S(1)} all-gather(f32[1,14,256]{2,1,0:T(8,128)S(1)} %slice_bitcast_fusion.4), channel_id=1, replica_groups=mesh['walker'=2,'z'=8,'x'=4,'y'=4] {'x','y'}, dimensions={0}, use_global_device_ids=true | all-gather | bytes 243712 | tf_op jit(solution)/shard_map/all_gather | solution.py:129
  212.1 1.2 log_bitcast_fusion
  213.3 24.1 %shard_map.116 = f32[14,1024]{1,0:T(8,128)} custom-call(f32[2,14,256,128]{3,2,1,0:T(8,128)} %broadcast_in_dim.73.col_ref, f32[2,256,2048]{2,1,0:T(8,128)} %pad_maximum_fusion.mat_ref, f32[256,256]{1,0:T(8,128)} %broadcast_in_dim.67.bias_in_ref, bf16[256,256]{1,0:T(8,128)(2,1)} %multiply_bitcast_fusion.w_hid_t_ref, f32[256,256]{1,0:T(8,128)} %broadcast_in_dim.68.bias_hid_ref, ...), custom_call_target="tpu_custom_call" | custom-call | flops 3846176768 | bytes 2154496 | tf_op jit(solution)/shard_map/pallas_call | solution.py:48
  237.4 12.7 %all-gather.9.cloned.1.call-done = f32[1792,256]{1,0:T(8,128)} async-done(((f32[224,256]{1,0:T(8,128)}), f32[1792,256]{1,0:T(8,128)}) %all-gather.9.cloned.1.call-update) | async-done | bytes 1835024 | tf_op jit(solution)/shard_map/all_gather | solution.py:129
  250.1 3.7 %convolution_subtract_fusion = f32[14,1792]{1,0:T(8,128)} fusion(f32[14,256]{1,0:T(8,128)S(1)} %bitcast.39, f32[1792,256]{1,0:T(8,128)} %all-gather.9.cloned.1.call-done, f32[14,1024]{1,0:T(8,128)} %shard_map.116, f32[14,768]{1,0:T(8,128)S(1)} %copy-done.3), kind=kOutput, calls=%fused_computation.4 | convolution fusion | flops 77120512 | bytes 2050048 | tf_op jit(solution)/shard_map/dot_general | solution.py:196
  (52 shorter events, 15.4 us)
Async XLA Ops:
  7.2 0.7 copy-start
  7.2 69.6 %all-gather.5.cloned.1.call-start = ((), (), s32[]{:S(2)}) async-start(), calls=%async_computation | async-start | bytes 2359296 | tf_op jit(solution)/shard_map/all_gather | solution.py:129
  34.6 129.1 %all-gather.7.cloned.1.call-start = ((), (), s32[]{:S(2)}) async-start(), calls=%async_computation.1 | async-start | bytes 1179648 | tf_op jit(solution)/shard_map/all_gather | solution.py:129
  80.0 2.9 %copy-start.5 = (f32[256]{0:T(256)S(1)}, f32[256]{0:T(256)}, u32[]{:S(2)}) copy-start(f32[256]{0:T(256)} %param.16) | copy-start | bytes 3076
  80.4 32.9 %copy-start.1 = (bf16[2048,512]{1,0:T(8,128)(2,1)S(1)}, bf16[2048,512]{1,0:T(8,128)(2,1)}, u32[]{:S(2)}) copy-start(bf16[2048,512]{1,0:T(8,128)(2,1)} %all-gather.5.cloned.1.call-done) | copy-start | bytes 6291460
  113.3 136.8 %all-gather.9.cloned.1.call-start = ((), (), s32[]{:S(2)}) async-start(), calls=%async_computation.2 | async-start | bytes 2064384 | tf_op jit(solution)/shard_map/all_gather | solution.py:129
  126.1 2.0 copy-start.2
  213.3 36.8 %copy-start.3 = (f32[14,768]{1,0:T(8,128)S(1)}, f32[14,768]{1,0:T(8,128)}, u32[]{:S(2)}) copy-start(f32[14,768]{1,0:T(8,128)} %shard_map.114) | copy-start | bytes 129028
  213.3 36.8 %copy-start.4 = (f32[16,256]{1,0:T(8,128)S(1)}, f32[16,256]{1,0:T(8,128)}, u32[]{:S(2)}) copy-start(f32[16,256]{1,0:T(8,128)} %get-tuple-element.9) | copy-start | bytes 49156
Sparse Core Ops, SparseCore 0:
  34.7 42.0 all-gather.4
  113.4 34.9 all-gather.6
  212.3 37.7 all-gather.8

commit v5 on v4

--- a/solution.py
+++ b/solution.py
@@ -173,7 +173,7 @@
         tail_cols = columns(tail_own)
         block_rows = gathered.reshape(groups, share + pad, panel)[:, :share, :].reshape(panel, panel)
         blocks = electrons // width
-        early = (blocks - 1) // 2
+        early = 1
         below_own = orbital_rows(tail_cols, mats, params, 0, 1, width)
         trailing_a = orbital_rows(tail_cols, mats, params, 1, early, width)
         extra = (-tail) % 8

time: 261 us -> 251 us (0.962)
  waiting for transfers between devices: 47.3 us -> 37 us
    all_gather x3, waiting for transfers between devices: 47.3 us -> 36.9 us  [gather_stages(): x = lax.all_gather(x, axes, axis=0, tiled=True)]
where the time goes in v5:
time: 251 us; the launch traced here: 250 us
  Pallas kernels  76.1 us (30%)
  blocking collectives  72.4 us (29%)
  waiting for transfers between devices  37 us (15%)
  local copies, waits for them, and re-layouts  34.4 us (14%)
  between operations  13.9 us (6%)
  other arithmetic  11.3 us (5%)
  matrix products  4.86 us (2%)
    all_gather x3, blocking collectives, gather_stages(): x = lax.all_gather(x, axes, axis=0, tiled=True)  72.4 us
    pallas_call x4, Pallas kernels, orbital_rows(): pl.pallas_call(orbital_kernel, grid=(blocks,), out_shape=jax.ShapeDtypeSt...  53.8 us
    all_gather x3, waiting for transfers between devices, gather_stages(): x = lax.all_gather(x, axes, axis=0, tiled=True)  36.9 us
    pallas_call x1, Pallas kernels, factor_augmented(): pl.pallas_call(factor_kernel, out_shape=(jax.ShapeDtypeStruct((below, wid...  22.2 us
    gather x2, local copies, waits for them, and re-layouts, on_device(): halves = 0.5 * jnp.take(late_every, perm, axis=0).astype(jnp.float32)  12.1 us
    unnamed x15, local copies, waits for them, and re-layouts  5.07 us
  transfers between devices with their start and end apart: 3, of which 2 were waited for; matrix products, arithmetic and copies ran while one was open for 12% of the time, Pallas kernels for 20%

profile of v5, /device:TPU:6, one launch (start us, length us, event | category | flops | bytes accessed | tf_op | source)
XLA Modules:
  0.0 250.0 jit_solution(11655363111497233047)
XLA Ops:
  7.9 1.1 fusion
  9.0 25.6 %all_gather.18 = bf16[256,512]{1,0:T(8,128)(2,1)} all-gather(bf16[16,512]{1,0:T(8,128)(2,1)S(1)} %fusion), channel_id=1, replica_groups=mesh['walker'=2,'z'=8,'x'=4,'y'=4] {'x','y'}, dimensions={0}, use_global_device_ids=true | all-gather | bytes 278528 | tf_op jit(solution)/shard_map/all_gather | solution.py:129
  35.5 1.0 copy.35
  42.2 34.5 %all-gather.5.cloned.1.call-done = bf16[2048,512]{1,0:T(8,128)(2,1)} async-done(((bf16[256,512]{1,0:T(8,128)(2,1)}), bf16[2048,512]{1,0:T(8,128)(2,1)}) %all-gather.5.cloned.1.call-update) | async-done | bytes 2097168 | tf_op jit(solution)/shard_map/all_gather | solution.py:129
  76.8 3.1 %gather_fusion = bf16[256,512]{1,0:T(8,128)(2,1)S(1)} fusion(bf16[2048,512]{1,0:T(8,128)(2,1)} %all-gather.5.cloned.1.call-done, s32[1024]{0:T(1024)S(1)} %pad_clamp_fusion), kind=kCustom, calls=%fused_computation | custom fusion | bytes 525312 | tf_op jit(solution)/shard_map/jit(_take)/gather | solution.py:162
  84.7 2.8 %shard_map.112 = f32[2,256]{1,0:T(2,128)} custom-call(f32[2,2,256,128]{3,2,1,0:T(8,128)} %broadcast_in_dim.66.col_ref, f32[2,256,256]{2,1,0:T(8,128)} %pad_maximum_fusion.1.mat_ref, f32[256,256]{1,0:T(8,128)} %broadcast_in_dim.67.bias_in_ref, bf16[256,256]{1,0:T(8,128)(2,1)} %multiply_bitcast_fusion.w_hid_t_ref, f32[256,256]{1,0:T(8,128)} %broadcast_in_dim.68.bias_hid_ref, ...), custom_call_target="tpu_custom_call" | custom-call | flops 137363456 | bytes 526336 | tf_op jit(solution)/shard_map/pallas_call | solution.py:48
  88.2 25.1 %all_gather.20 = f32[128,256]{1,0:T(8,128)} all-gather(f32[8,256]{1,0:T(8,128)S(1)} %pad.5), channel_id=1, replica_groups=mesh['walker'=2,'z'=8,'x'=4,'y'=4] {'x','y'}, dimensions={0}, use_global_device_ids=true | all-gather | bytes 139264 | tf_op jit(solution)/shard_map/all_gather | solution.py:129
  113.4 9.2 %gather_fusion.1 = bf16[2048,512]{1,0:T(8,128)(2,1)} fusion(bf16[2048,512]{1,0:T(8,128)(2,1)S(1)} %copy-done.1, s32[2048]{0:T(1024)S(1)} %fusion.4), kind=kCustom, calls=%fused_computation.1 | custom fusion | bytes 4202496 | tf_op jit(solution)/shard_map/jit(_take)/gather | solution.py:170
  122.5 2.9 %copy.36 = bf16[2048,512]{0,1:T(8,128)(2,1)S(1)} copy(bf16[2048,512]{1,0:T(8,128)(2,1)} %gather_fusion.1) | data formatting | bytes 4194304 | tf_op jit(solution)/shard_map/jit(_take)/gather | solution.py:170
  126.1 1.9 copy-done.2
  128.3 2.5 %slice_bitcast_fusion.1 = (f32[1,256,2048]{2,1,0:T(8,128)S(1)}, f32[1,256,2048]{2,1,0:T(8,128)S(1)}) fusion(f32[2048,512]{0,1:T(8,128)} %copy-done.2), kind=kLoop, calls=%fused_computation.6 | loop fusion | bytes 8388608 | tf_op jit(solution)/shard_map/stack | solution.py:154
  130.8 2.2 pad_maximum_fusion.mat_ref
  133.1 2.3 broadcast_in_dim.73.col_ref
  135.4 8.2 %shard_map.114 = f32[14,256]{1,0:T(8,128)} custom-call(f32[2,14,256,128]{3,2,1,0:T(8,128)} %broadcast_in_dim.73.col_ref, f32[2,256,2048]{2,1,0:T(8,128)} %pad_maximum_fusion.mat_ref, f32[256,256]{1,0:T(8,128)} %broadcast_in_dim.67.bias_in_ref, bf16[256,256]{1,0:T(8,128)(2,1)} %multiply_bitcast_fusion.w_hid_t_ref, f32[256,256]{1,0:T(8,128)} %broadcast_in_dim.68.bias_hid_ref, ...), custom_call_target="tpu_custom_call" | custom-call | flops 961544192 | bytes 538624 | tf_op jit(solution)/shard_map/pallas_call | solution.py:48
  143.6 1.3 slice.65.after_ref
  144.9 8.2 %shard_map.113 = f32[14,256]{1,0:T(8,128)} custom-call(f32[2,14,256,128]{3,2,1,0:T(8,128)} %broadcast_in_dim.73.col_ref, f32[2,256,2048]{2,1,0:T(8,128)} %pad_maximum_fusion.mat_ref, f32[256,256]{1,0:T(8,128)} %broadcast_in_dim.67.bias_in_ref, bf16[256,256]{1,0:T(8,128)(2,1)} %multiply_bitcast_fusion.w_hid_t_ref, f32[256,256]{1,0:T(8,128)} %broadcast_in_dim.68.bias_hid_ref, ...), custom_call_target="tpu_custom_call" | custom-call | flops 961544192 | bytes 538624 | tf_op jit(solution)/shard_map/pallas_call | solution.py:48
  153.2 1.3 slice.62
  154.6 1.6 maximum_maximum_fusion.m_in_ref
  156.2 22.2 %shard_map.115 = (f32[16,256]{1,0:T(8,128)}, f32[1,256]{1,0:T(1,128)}, f32[16,256]{1,0:T(8,128)}) custom-call(f32[272,256]{1,0:T(8,128)} %maximum_maximum_fusion.m_in_ref, f32[272,1]{1,0:T(8,128)} %broadcast_in_dim.77.ps_ref, f32[8,128]{1,0:T(8,128)} %slice.65.after_ref), custom_call_target="tpu_custom_call" | custom-call | tf_op jit(solution)/shard_map/pallas_call | solution.py:109
  179.2 21.7 %all-gather = f32[16,14,256]{2,1,0:T(8,128)S(1)} all-gather(f32[1,14,256]{2,1,0:T(8,128)S(1)} %slice_bitcast_fusion.4), channel_id=1, replica_groups=mesh['walker'=2,'z'=8,'x'=4,'y'=4] {'x','y'}, dimensions={0}, use_global_device_ids=true | all-gather | bytes 243712 | tf_op jit(solution)/shard_map/all_gather | solution.py:129
  201.6 1.1 log_bitcast_fusion
  202.8 34.6 %shard_map.116 = f32[14,1536]{1,0:T(8,128)} custom-call(f32[2,14,256,128]{3,2,1,0:T(8,128)} %broadcast_in_dim.73.col_ref, f32[2,256,2048]{2,1,0:T(8,128)} %pad_maximum_fusion.mat_ref, f32[256,256]{1,0:T(8,128)} %broadcast_in_dim.67.bias_in_ref, bf16[256,256]{1,0:T(8,128)(2,1)} %multiply_bitcast_fusion.w_hid_t_ref, f32[256,256]{1,0:T(8,128)} %broadcast_in_dim.68.bias_hid_ref, ...), custom_call_target="tpu_custom_call" | custom-call | flops 5769265152 | bytes 3231744 | tf_op jit(solution)/shard_map/pallas_call | solution.py:48
  237.4 2.4 all-gather.9.cloned.1.call-done
  239.7 3.8 %convolution_subtract_fusion = f32[14,1792]{1,0:T(8,128)} fusion(f32[14,256]{1,0:T(8,128)S(1)} %bitcast.39, f32[1792,256]{1,0:T(8,128)} %all-gather.9.cloned.1.call-done, f32[14,1536]{1,0:T(8,128)} %shard_map.116, f32[14,256]{1,0:T(8,128)S(1)} %copy-done.3), kind=kOutput, calls=%fused_computation.4 | convolution fusion | flops 77120512 | bytes 2050048 | tf_op jit(solution)/shard_map/dot_general | solution.py:196
  (52 shorter events, 15.4 us)
Async XLA Ops:
  7.2 0.7 copy-start
  7.2 69.6 %all-gather.5.cloned.1.call-start = ((), (), s32[]{:S(2)}) async-start(), calls=%async_computation | async-start | bytes 2359296 | tf_op jit(solution)/shard_map/all_gather | solution.py:129
  34.6 118.5 %all-gather.7.cloned.1.call-start = ((), (), s32[]{:S(2)}) async-start(), calls=%async_computation.1 | async-start | bytes 1179648 | tf_op jit(solution)/shard_map/all_gather | solution.py:129
  80.0 2.9 %copy-start.5 = (f32[256]{0:T(256)S(1)}, f32[256]{0:T(256)}, u32[]{:S(2)}) copy-start(f32[256]{0:T(256)} %param.16) | copy-start | bytes 3076
  80.4 32.9 %copy-start.1 = (bf16[2048,512]{1,0:T(8,128)(2,1)S(1)}, bf16[2048,512]{1,0:T(8,128)(2,1)}, u32[]{:S(2)}) copy-start(bf16[2048,512]{1,0:T(8,128)(2,1)} %all-gather.5.cloned.1.call-done) | copy-start | bytes 6291460
  113.3 126.4 %all-gather.9.cloned.1.call-start = ((), (), s32[]{:S(2)}) async-start(), calls=%async_computation.2 | async-start | bytes 2064384 | tf_op jit(solution)/shard_map/all_gather | solution.py:129
  126.1 2.0 copy-start.2
  202.8 37.0 %copy-start.3 = (f32[14,256]{1,0:T(8,128)S(1)}, f32[14,256]{1,0:T(8,128)}, u32[]{:S(2)}) copy-start(f32[14,256]{1,0:T(8,128)} %shard_map.114) | copy-start | bytes 43012
  202.8 37.0 %copy-start.4 = (f32[16,256]{1,0:T(8,128)S(1)}, f32[16,256]{1,0:T(8,128)}, u32[]{:S(2)}) copy-start(f32[16,256]{1,0:T(8,128)} %get-tuple-element.9) | copy-start | bytes 49156
Sparse Core Ops, SparseCore 0:
  34.7 42.0 all-gather.4
  113.4 35.1 all-gather.6
  201.7 37.9 all-gather.8

commit v6 on v5

--- a/solution.py
+++ b/solution.py
@@ -61,42 +61,54 @@
 
 def factor_kernel(m_in_ref, ps_ref, after_ref, pc_ref, piv_ref, scaled_ref, m_ref):
     rows, size = m_ref.shape
-    lane = lax.broadcasted_iota(jnp.int32, (1, size), 1)
-    lanes = lax.broadcasted_iota(jnp.int32, (rows, size), 1)
-    row_idx = lax.broadcasted_iota(jnp.int32, (rows, 1), 0)
+    half = size // 2
+    below = rows - size
+    lanes_all = lax.broadcasted_iota(jnp.int32, (rows, size), 1)
+    row_all = lax.broadcasted_iota(jnp.int32, (rows, 1), 0)
     m0 = m_in_ref[...]
     strength = ps_ref[...]
-    m0 = m0 + jnp.where((row_idx % 2 == 0) & (lanes == row_idx + 1) & (row_idx < size), strength, 0.0)
-    m0 = m0 - jnp.where((row_idx % 2 == 1) & (lanes == row_idx - 1) & (row_idx < size), strength, 0.0)
+    m0 = m0 + jnp.where((row_all % 2 == 0) & (lanes_all == row_all + 1) & (row_all < size), strength, 0.0)
+    m0 = m0 - jnp.where((row_all % 2 == 1) & (lanes_all == row_all - 1) & (row_all < size), strength, 0.0)
     m_ref[...] = m0
-    below = rows - size
-
-    def step(k, carry):
-        pivots, scaled = carry
-        first = 2 * k
-        r0 = m_ref[pl.ds(first, 1), :]
-        r1 = m_ref[pl.ds(first + 1, 1), :]
-        pivot = jnp.sum(jnp.where(lane == first + 1, r0, 0.0), axis=1, keepdims=True)
-        keep_lane = lane > first + 1
-        even_lane = jnp.where(keep_lane, -r0 / pivot, 0.0)
-        odd_lane = jnp.where(keep_lane, -r1 / pivot, 0.0)
-        m = m_ref[...]
-        col_even = jnp.sum(jnp.where(lanes == first, m, 0.0), axis=1, keepdims=True)
-        col_odd = jnp.sum(jnp.where(lanes == first + 1, m, 0.0), axis=1, keepdims=True)
-        low_even = col_even[size:]
-        low_odd = col_odd[size:]
-        low_lanes = lanes[size:]
-        scaled = jnp.where(low_lanes == first, low_odd / pivot, scaled)
-        scaled = jnp.where(low_lanes == first + 1, -low_even / pivot, scaled)
-        pivots = jnp.where(lane == k, pivot, pivots)
-        keep_row = row_idx > first + 1
-        col_even = jnp.where(keep_row, col_even, 0.0)
-        col_odd = jnp.where(keep_row, col_odd, 0.0)
-        m_ref[...] = m + (col_odd * even_lane - col_even * odd_lane)
-        return (pivots, scaled)
-
-    start = (jnp.zeros((1, size), jnp.float32), jnp.zeros((below, size), jnp.float32))
-    pivots, scaled = lax.fori_loop(0, size // 2, step, start)
+    lane_full = lax.broadcasted_iota(jnp.int32, (1, size), 1)
+    low_lanes = lax.broadcasted_iota(jnp.int32, (below, size), 1)
+
+    def make_step(lo):
+        sub_rows, sub_cols = rows - lo, size - lo
+        reach = min(half, sub_cols)
+        lane = lax.broadcasted_iota(jnp.int32, (1, sub_cols), 1) + lo
+        lanes = lax.broadcasted_iota(jnp.int32, (sub_rows, reach), 1) + lo
+        row_idx = lax.broadcasted_iota(jnp.int32, (sub_rows, 1), 0) + lo
+
+        def step(k, carry):
+            pivots, scaled = carry
+            first = 2 * k
+            r0 = m_ref[pl.ds(first, 1), :][:, lo:]
+            r1 = m_ref[pl.ds(first + 1, 1), :][:, lo:]
+            pivot = jnp.sum(jnp.where(lane == first + 1, r0, 0.0), axis=1, keepdims=True)
+            keep_lane = lane > first + 1
+            even_lane = jnp.where(keep_lane, -r0 / pivot, 0.0)
+            odd_lane = jnp.where(keep_lane, -r1 / pivot, 0.0)
+            m = m_ref[lo:, lo:]
+            window = m[:, :reach]
+            col_even = jnp.sum(jnp.where(lanes == first, window, 0.0), axis=1, keepdims=True)
+            col_odd = jnp.sum(jnp.where(lanes == first + 1, window, 0.0), axis=1, keepdims=True)
+            low_even = col_even[size - lo:]
+            low_odd = col_odd[size - lo:]
+            scaled = jnp.where(low_lanes == first, low_odd / pivot, scaled)
+            scaled = jnp.where(low_lanes == first + 1, -low_even / pivot, scaled)
+            pivots = jnp.where(lane_full == k, pivot, pivots)
+            keep_row = row_idx > first + 1
+            col_even = jnp.where(keep_row, col_even, 0.0)
+            col_odd = jnp.where(keep_row, col_odd, 0.0)
+            m_ref[lo:, lo:] = m + (col_odd * even_lane - col_even * odd_lane)
+            return (pivots, scaled)
+
+        return step
+
+    carry = (jnp.zeros((1, size), jnp.float32), jnp.zeros((below, size), jnp.float32))
+    carry = lax.fori_loop(0, half // 2, make_step(0), carry)
+    pivots, scaled = lax.fori_loop(half // 2, size // 2, make_step(half), carry)
     pc_ref[...] = m_ref[size:, :]
     piv_ref[...] = pivots
     scaled_ref[...] = scaled

time: 251 us -> 248 us (0.988)
  Pallas kernels: 76.1 us -> 73.5 us
    pallas_call x1, Pallas kernels: 22.2 us -> 19.7 us  [factor_augmented(): pl.pallas_call(factor_kernel, out_shape=(jax.ShapeDtypeStruct((below, wid...]
  transfers between devices with their start and end apart: 3 -> 3, of which waited for: 2 -> 2; matrix products, arithmetic and copies ran while one was open for 12% -> 12% of each run, Pallas kernels for 20% -> 21%
where the time goes in v6:
time: 248 us; the launch traced here: 247 us
  Pallas kernels  73.5 us (30%)
  blocking collectives  72.4 us (29%)
  waiting for transfers between devices  37 us (15%)
  local copies, waits for them, and re-layouts  34.4 us (14%)
  between operations  13.9 us (6%)
  other arithmetic  11.3 us (5%)
  matrix products  4.86 us (2%)
    all_gather x3, blocking collectives, gather_stages(): x = lax.all_gather(x, axes, axis=0, tiled=True)  72.4 us
    pallas_call x4, Pallas kernels, orbital_rows(): pl.pallas_call(orbital_kernel, grid=(blocks,), out_shape=jax.ShapeDtypeSt...  53.8 us
    all_gather x3, waiting for transfers between devices, gather_stages(): x = lax.all_gather(x, axes, axis=0, tiled=True)  36.9 us
    pallas_call x1, Pallas kernels, factor_augmented(): pl.pallas_call(factor_kernel, out_shape=(jax.ShapeDtypeStruct((below, wid...  19.7 us
    gather x2, local copies, waits for them, and re-layouts, on_device(): halves = 0.5 * jnp.take(late_every, perm, axis=0).astype(jnp.float32)  12.1 us
    unnamed x15, local copies, waits for them, and re-layouts  5.07 us
  transfers between devices with their start and end apart: 3, of which 2 were waited for; matrix products, arithmetic and copies ran while one was open for 12% of the time, Pallas kernels for 21%

profile of v6, /device:TPU:6, one launch (start us, length us, event | category | flops | bytes accessed | tf_op | source)
XLA Modules:
  0.0 247.5 jit_solution(8566882193452974687)
XLA Ops:
  7.9 1.1 fusion
  9.0 25.6 %all_gather.18 = bf16[256,512]{1,0:T(8,128)(2,1)} all-gather(bf16[16,512]{1,0:T(8,128)(2,1)S(1)} %fusion), channel_id=1, replica_groups=mesh['walker'=2,'z'=8,'x'=4,'y'=4] {'x','y'}, dimensions={0}, use_global_device_ids=true | all-gather | bytes 278528 | tf_op jit(solution)/shard_map/all_gather | solution.py:141
  35.5 1.0 copy.35
  42.2 34.5 %all-gather.5.cloned.1.call-done = bf16[2048,512]{1,0:T(8,128)(2,1)} async-done(((bf16[256,512]{1,0:T(8,128)(2,1)}), bf16[2048,512]{1,0:T(8,128)(2,1)}) %all-gather.5.cloned.1.call-update) | async-done | bytes 2097168 | tf_op jit(solution)/shard_map/all_gather | solution.py:141
  76.8 3.1 %gather_fusion = bf16[256,512]{1,0:T(8,128)(2,1)S(1)} fusion(bf16[2048,512]{1,0:T(8,128)(2,1)} %all-gather.5.cloned.1.call-done, s32[1024]{0:T(1024)S(1)} %pad_clamp_fusion), kind=kCustom, calls=%fused_computation | custom fusion | bytes 525312 | tf_op jit(solution)/shard_map/jit(_take)/gather | solution.py:174
  84.7 2.8 %shard_map.112 = f32[2,256]{1,0:T(2,128)} custom-call(f32[2,2,256,128]{3,2,1,0:T(8,128)} %broadcast_in_dim.66.col_ref, f32[2,256,256]{2,1,0:T(8,128)} %pad_maximum_fusion.1.mat_ref, f32[256,256]{1,0:T(8,128)} %broadcast_in_dim.67.bias_in_ref, bf16[256,256]{1,0:T(8,128)(2,1)} %multiply_bitcast_fusion.w_hid_t_ref, f32[256,256]{1,0:T(8,128)} %broadcast_in_dim.68.bias_hid_ref, ...), custom_call_target="tpu_custom_call" | custom-call | flops 137363456 | bytes 526336 | tf_op jit(solution)/shard_map/pallas_call | solution.py:48
  88.2 25.1 %all_gather.20 = f32[128,256]{1,0:T(8,128)} all-gather(f32[8,256]{1,0:T(8,128)S(1)} %pad.5), channel_id=1, replica_groups=mesh['walker'=2,'z'=8,'x'=4,'y'=4] {'x','y'}, dimensions={0}, use_global_device_ids=true | all-gather | bytes 139264 | tf_op jit(solution)/shard_map/all_gather | solution.py:141
  113.4 9.2 %gather_fusion.1 = bf16[2048,512]{1,0:T(8,128)(2,1)} fusion(bf16[2048,512]{1,0:T(8,128)(2,1)S(1)} %copy-done.1, s32[2048]{0:T(1024)S(1)} %fusion.4), kind=kCustom, calls=%fused_computation.1 | custom fusion | bytes 4202496 | tf_op jit(solution)/shard_map/jit(_take)/gather | solution.py:182
  122.5 2.9 %copy.36 = bf16[2048,512]{0,1:T(8,128)(2,1)S(1)} copy(bf16[2048,512]{1,0:T(8,128)(2,1)} %gather_fusion.1) | data formatting | bytes 4194304 | tf_op jit(solution)/shard_map/jit(_take)/gather | solution.py:182
  126.1 1.9 copy-done.2
  128.3 2.5 %slice_bitcast_fusion.1 = (f32[1,256,2048]{2,1,0:T(8,128)S(1)}, f32[1,256,2048]{2,1,0:T(8,128)S(1)}) fusion(f32[2048,512]{0,1:T(8,128)} %copy-done.2), kind=kLoop, calls=%fused_computation.6 | loop fusion | bytes 8388608 | tf_op jit(solution)/shard_map/stack | solution.py:166
  130.8 2.2 pad_maximum_fusion.mat_ref
  133.1 2.3 broadcast_in_dim.73.col_ref
  135.4 8.2 %shard_map.114 = f32[14,256]{1,0:T(8,128)} custom-call(f32[2,14,256,128]{3,2,1,0:T(8,128)} %broadcast_in_dim.73.col_ref, f32[2,256,2048]{2,1,0:T(8,128)} %pad_maximum_fusion.mat_ref, f32[256,256]{1,0:T(8,128)} %broadcast_in_dim.67.bias_in_ref, bf16[256,256]{1,0:T(8,128)(2,1)} %multiply_bitcast_fusion.w_hid_t_ref, f32[256,256]{1,0:T(8,128)} %broadcast_in_dim.68.bias_hid_ref, ...), custom_call_target="tpu_custom_call" | custom-call | flops 961544192 | bytes 538624 | tf_op jit(solution)/shard_map/pallas_call | solution.py:48
  143.6 1.3 slice.65.after_ref
  144.9 8.2 %shard_map.113 = f32[14,256]{1,0:T(8,128)} custom-call(f32[2,14,256,128]{3,2,1,0:T(8,128)} %broadcast_in_dim.73.col_ref, f32[2,256,2048]{2,1,0:T(8,128)} %pad_maximum_fusion.mat_ref, f32[256,256]{1,0:T(8,128)} %broadcast_in_dim.67.bias_in_ref, bf16[256,256]{1,0:T(8,128)(2,1)} %multiply_bitcast_fusion.w_hid_t_ref, f32[256,256]{1,0:T(8,128)} %broadcast_in_dim.68.bias_hid_ref, ...), custom_call_target="tpu_custom_call" | custom-call | flops 961544192 | bytes 538624 | tf_op jit(solution)/shard_map/pallas_call | solution.py:48
  153.2 1.3 slice.62
  154.6 1.6 maximum_maximum_fusion.m_in_ref
  156.2 19.7 %shard_map.115 = (f32[16,256]{1,0:T(8,128)}, f32[1,256]{1,0:T(1,128)}, f32[16,256]{1,0:T(8,128)}) custom-call(f32[272,256]{1,0:T(8,128)} %maximum_maximum_fusion.m_in_ref, f32[272,1]{1,0:T(8,128)} %broadcast_in_dim.77.ps_ref, f32[8,128]{1,0:T(8,128)} %slice.65.after_ref), custom_call_target="tpu_custom_call" | custom-call | tf_op jit(solution)/shard_map/pallas_call | solution.py:121
  176.6 21.7 %all-gather = f32[16,14,256]{2,1,0:T(8,128)S(1)} all-gather(f32[1,14,256]{2,1,0:T(8,128)S(1)} %slice_bitcast_fusion.4), channel_id=1, replica_groups=mesh['walker'=2,'z'=8,'x'=4,'y'=4] {'x','y'}, dimensions={0}, use_global_device_ids=true | all-gather | bytes 243712 | tf_op jit(solution)/shard_map/all_gather | solution.py:141
  199.1 1.1 log_bitcast_fusion
  200.2 34.6 %shard_map.116 = f32[14,1536]{1,0:T(8,128)} custom-call(f32[2,14,256,128]{3,2,1,0:T(8,128)} %broadcast_in_dim.73.col_ref, f32[2,256,2048]{2,1,0:T(8,128)} %pad_maximum_fusion.mat_ref, f32[256,256]{1,0:T(8,128)} %broadcast_in_dim.67.bias_in_ref, bf16[256,256]{1,0:T(8,128)(2,1)} %multiply_bitcast_fusion.w_hid_t_ref, f32[256,256]{1,0:T(8,128)} %broadcast_in_dim.68.bias_hid_ref, ...), custom_call_target="tpu_custom_call" | custom-call | flops 5769265152 | bytes 3231744 | tf_op jit(solution)/shard_map/pallas_call | solution.py:48
  234.8 2.4 all-gather.9.cloned.1.call-done
  237.2 3.8 %convolution_subtract_fusion = f32[14,1792]{1,0:T(8,128)} fusion(f32[14,256]{1,0:T(8,128)S(1)} %bitcast.39, f32[1792,256]{1,0:T(8,128)} %all-gather.9.cloned.1.call-done, f32[14,1536]{1,0:T(8,128)} %shard_map.116, f32[14,256]{1,0:T(8,128)S(1)} %copy-done.3), kind=kOutput, calls=%fused_computation.4 | convolution fusion | flops 77120512 | bytes 2050048 | tf_op jit(solution)/shard_map/dot_general | solution.py:208
  (52 shorter events, 15.4 us)
Async XLA Ops:
  7.2 0.7 copy-start
  7.2 69.6 %all-gather.5.cloned.1.call-start = ((), (), s32[]{:S(2)}) async-start(), calls=%async_computation | async-start | bytes 2359296 | tf_op jit(solution)/shard_map/all_gather | solution.py:141
  34.6 118.5 %all-gather.7.cloned.1.call-start = ((), (), s32[]{:S(2)}) async-start(), calls=%async_computation.1 | async-start | bytes 1179648 | tf_op jit(solution)/shard_map/all_gather | solution.py:141
  80.0 2.9 %copy-start.5 = (f32[256]{0:T(256)S(1)}, f32[256]{0:T(256)}, u32[]{:S(2)}) copy-start(f32[256]{0:T(256)} %param.16) | copy-start | bytes 3076
  80.4 32.9 %copy-start.1 = (bf16[2048,512]{1,0:T(8,128)(2,1)S(1)}, bf16[2048,512]{1,0:T(8,128)(2,1)}, u32[]{:S(2)}) copy-start(bf16[2048,512]{1,0:T(8,128)(2,1)} %all-gather.5.cloned.1.call-done) | copy-start | bytes 6291460
  113.3 123.9 %all-gather.9.cloned.1.call-start = ((), (), s32[]{:S(2)}) async-start(), calls=%async_computation.2 | async-start | bytes 2064384 | tf_op jit(solution)/shard_map/all_gather | solution.py:141
  126.1 2.0 copy-start.2
  200.2 37.0 %copy-start.3 = (f32[14,256]{1,0:T(8,128)S(1)}, f32[14,256]{1,0:T(8,128)}, u32[]{:S(2)}) copy-start(f32[14,256]{1,0:T(8,128)} %shard_map.114) | copy-start | bytes 43012
  200.2 37.0 %copy-start.4 = (f32[16,256]{1,0:T(8,128)S(1)}, f32[16,256]{1,0:T(8,128)}, u32[]{:S(2)}) copy-start(f32[16,256]{1,0:T(8,128)} %get-tuple-element.9) | copy-start | bytes 49156
Sparse Core Ops, SparseCore 0:
  34.7 42.0 all-gather.4
  113.4 35.1 all-gather.6
  199.2 37.9 all-gather.8

commit v7 on v6

--- a/solution.py
+++ b/solution.py
@@ -107,8 +107,8 @@
         return step
 
     carry = (jnp.zeros((1, size), jnp.float32), jnp.zeros((below, size), jnp.float32))
-    carry = lax.fori_loop(0, half // 2, make_step(0), carry)
-    pivots, scaled = lax.fori_loop(half // 2, size // 2, make_step(half), carry)
+    carry = lax.fori_loop(0, half // 2, make_step(0), carry, unroll=2)
+    pivots, scaled = lax.fori_loop(half // 2, size // 2, make_step(half), carry, unroll=2)
     pc_ref[...] = m_ref[size:, :]
     piv_ref[...] = pivots
     scaled_ref[...] = scaled
@@ -186,8 +186,9 @@
         block_rows = gathered.reshape(groups, share + pad, panel)[:, :share, :].reshape(panel, panel)
         blocks = electrons // width
         early = 1
-        below_own = orbital_rows(tail_cols, mats, params, 0, 1, width)
-        trailing_a = orbital_rows(tail_cols, mats, params, 1, early, width)
+        first_part = orbital_rows(tail_cols, mats, params, 0, 1 + early, width)
+        below_own = first_part[:, :panel]
+        trailing_a = first_part[:, panel:]
         extra = (-tail) % 8
         augmented = jnp.concatenate(
             [block_rows, below_own, jnp.zeros((extra, panel), jnp.float32)], axis=0

time: 248 us -> 244 us (0.984)
  Pallas kernels: 73.5 us -> 69.7 us
    pallas_call x4 -> x3, Pallas kernels: 53.8 us -> 50.9 us  [orbital_rows(): pl.pallas_call(orbital_kernel, grid=(blocks,), out_shape=jax.ShapeDtypeSt...]
    unnamed x15 -> x13, local copies, waits for them, and re-layouts: 5.07 us -> 5.06 us
  transfers between devices with their start and end apart: 3 -> 3, of which waited for: 2 -> 2; matrix products, arithmetic and copies ran while one was open for 12% -> 13% of each run, Pallas kernels for 21% -> 20%
where the time goes in v7:
time: 244 us
  blocking collectives  72.4 us (30%)
  Pallas kernels  69.7 us (29%)
  waiting for transfers between devices  37 us (15%)
  local copies, waits for them, and re-layouts  35.1 us (14%)
  between operations  13.9 us (6%)
  other arithmetic  10.6 us (4%)
  matrix products  4.86 us (2%)
    all_gather x3, blocking collectives, gather_stages(): x = lax.all_gather(x, axes, axis=0, tiled=True)  72.4 us
    pallas_call x3, Pallas kernels, orbital_rows(): pl.pallas_call(orbital_kernel, grid=(blocks,), out_shape=jax.ShapeDtypeSt...  50.9 us
    all_gather x3, waiting for transfers between devices, gather_stages(): x = lax.all_gather(x, axes, axis=0, tiled=True)  36.9 us
    pallas_call x1, Pallas kernels, factor_augmented(): pl.pallas_call(factor_kernel, out_shape=(jax.ShapeDtypeStruct((below, wid...  18.8 us
    gather x2, local copies, waits for them, and re-layouts, on_device(): halves = 0.5 * jnp.take(late_every, perm, axis=0).astype(jnp.float32)  12.1 us
    unnamed x13, local copies, waits for them, and re-layouts  5.06 us
  transfers between devices with their start and end apart: 3, of which 2 were waited for; matrix products, arithmetic and copies ran while one was open for 13% of the time, Pallas kernels for 20%

profile of v7, /device:TPU:6, one launch (start us, length us, event | category | flops | bytes accessed | tf_op | source)
XLA Modules:
  0.0 243.6 jit_solution(18298976039857890606)
XLA Ops:
  7.9 1.1 fusion
  9.0 25.6 %all_gather.18 = bf16[256,512]{1,0:T(8,128)(2,1)} all-gather(bf16[16,512]{1,0:T(8,128)(2,1)S(1)} %fusion), channel_id=1, replica_groups=mesh['walker'=2,'z'=8,'x'=4,'y'=4] {'x','y'}, dimensions={0}, use_global_device_ids=true | all-gather | bytes 278528 | tf_op jit(solution)/shard_map/all_gather | solution.py:141
  35.5 1.0 copy.35
  42.2 34.5 %all-gather.5.cloned.1.call-done = bf16[2048,512]{1,0:T(8,128)(2,1)} async-done(((bf16[256,512]{1,0:T(8,128)(2,1)}), bf16[2048,512]{1,0:T(8,128)(2,1)}) %all-gather.5.cloned.1.call-update) | async-done | bytes 2097168 | tf_op jit(solution)/shard_map/all_gather | solution.py:141
  76.8 3.1 %gather_fusion = bf16[256,512]{1,0:T(8,128)(2,1)S(1)} fusion(bf16[2048,512]{1,0:T(8,128)(2,1)} %all-gather.5.cloned.1.call-done, s32[1024]{0:T(1024)S(1)} %pad_clamp_fusion), kind=kCustom, calls=%fused_computation | custom fusion | bytes 525312 | tf_op jit(solution)/shard_map/jit(_take)/gather | solution.py:174
  83.7 1.0 broadcast_in_dim.66.col_ref
  84.7 2.8 %shard_map.112 = f32[2,256]{1,0:T(2,128)} custom-call(f32[2,2,256,128]{3,2,1,0:T(8,128)} %broadcast_in_dim.66.col_ref, f32[2,256,256]{2,1,0:T(8,128)} %pad_maximum_fusion.1.mat_ref, f32[256,256]{1,0:T(8,128)} %broadcast_in_dim.67.bias_in_ref, bf16[256,256]{1,0:T(8,128)(2,1)} %multiply_bitcast_fusion.w_hid_t_ref, f32[256,256]{1,0:T(8,128)} %broadcast_in_dim.68.bias_hid_ref, ...), custom_call_target="tpu_custom_call" | custom-call | flops 137363456 | bytes 526336 | tf_op jit(solution)/shard_map/pallas_call | solution.py:48
  88.2 25.1 %all_gather.20 = f32[128,256]{1,0:T(8,128)} all-gather(f32[8,256]{1,0:T(8,128)S(1)} %pad.5), channel_id=1, replica_groups=mesh['walker'=2,'z'=8,'x'=4,'y'=4] {'x','y'}, dimensions={0}, use_global_device_ids=true | all-gather | bytes 139264 | tf_op jit(solution)/shard_map/all_gather | solution.py:141
  113.4 9.2 %gather_fusion.1 = bf16[2048,512]{1,0:T(8,128)(2,1)} fusion(bf16[2048,512]{1,0:T(8,128)(2,1)S(1)} %copy-done.1, s32[2048]{0:T(1024)S(1)} %fusion.4), kind=kCustom, calls=%fused_computation.1 | custom fusion | bytes 4202496 | tf_op jit(solution)/shard_map/jit(_take)/gather | solution.py:182
  122.5 2.9 %copy.36 = bf16[2048,512]{0,1:T(8,128)(2,1)S(1)} copy(bf16[2048,512]{1,0:T(8,128)(2,1)} %gather_fusion.1) | data formatting | bytes 4194304 | tf_op jit(solution)/shard_map/jit(_take)/gather | solution.py:182
  126.1 1.9 copy-done.2
  128.3 2.5 %slice_bitcast_fusion.1 = (f32[1,256,2048]{2,1,0:T(8,128)S(1)}, f32[1,256,2048]{2,1,0:T(8,128)S(1)}) fusion(f32[2048,512]{0,1:T(8,128)} %copy-done.2), kind=kLoop, calls=%fused_computation.6 | loop fusion | bytes 8388608 | tf_op jit(solution)/shard_map/stack | solution.py:166
  130.8 2.2 pad_maximum_fusion.mat_ref
  133.1 2.3 broadcast_in_dim.73.col_ref
  135.4 13.5 %shard_map.113 = f32[14,512]{1,0:T(8,128)} custom-call(f32[2,14,256,128]{3,2,1,0:T(8,128)} %broadcast_in_dim.73.col_ref, f32[2,256,2048]{2,1,0:T(8,128)} %pad_maximum_fusion.mat_ref, f32[256,256]{1,0:T(8,128)} %broadcast_in_dim.67.bias_in_ref, bf16[256,256]{1,0:T(8,128)(2,1)} %multiply_bitcast_fusion.w_hid_t_ref, f32[256,256]{1,0:T(8,128)} %broadcast_in_dim.68.bias_hid_ref, ...), custom_call_target="tpu_custom_call" | custom-call | flops 1923088384 | bytes 1077248 | tf_op jit(solution)/shard_map/pallas_call | solution.py:48
  148.9 1.3 slice.75.after_ref
  150.9 1.3 slice.71
  152.4 0.9 maximum_maximum_fusion.m_in_ref
  153.3 18.8 %shard_map.114 = (f32[16,256]{1,0:T(8,128)}, f32[1,256]{1,0:T(1,128)}, f32[16,256]{1,0:T(8,128)}) custom-call(f32[272,256]{1,0:T(8,128)} %maximum_maximum_fusion.m_in_ref, f32[272,1]{1,0:T(8,128)} %broadcast_in_dim.77.ps_ref, f32[8,128]{1,0:T(8,128)} %slice.75.after_ref), custom_call_target="tpu_custom_call" | custom-call | tf_op jit(solution)/shard_map/pallas_call | solution.py:121
  172.8 21.7 %all-gather = f32[16,14,256]{2,1,0:T(8,128)S(1)} all-gather(f32[1,14,256]{2,1,0:T(8,128)S(1)} %slice_bitcast_fusion.4), channel_id=1, replica_groups=mesh['walker'=2,'z'=8,'x'=4,'y'=4] {'x','y'}, dimensions={0}, use_global_device_ids=true | all-gather | bytes 243712 | tf_op jit(solution)/shard_map/all_gather | solution.py:141
  195.2 1.1 log_bitcast_fusion
  196.4 34.6 %shard_map.115 = f32[14,1536]{1,0:T(8,128)} custom-call(f32[2,14,256,128]{3,2,1,0:T(8,128)} %broadcast_in_dim.73.col_ref, f32[2,256,2048]{2,1,0:T(8,128)} %pad_maximum_fusion.mat_ref, f32[256,256]{1,0:T(8,128)} %broadcast_in_dim.67.bias_in_ref, bf16[256,256]{1,0:T(8,128)(2,1)} %multiply_bitcast_fusion.w_hid_t_ref, f32[256,256]{1,0:T(8,128)} %broadcast_in_dim.68.bias_hid_ref, ...), custom_call_target="tpu_custom_call" | custom-call | flops 5769265152 | bytes 3231744 | tf_op jit(solution)/shard_map/pallas_call | solution.py:48
  231.0 2.4 all-gather.9.cloned.1.call-done
  233.4 3.7 %convolution_subtract_fusion = f32[14,1792]{1,0:T(8,128)} fusion(f32[14,256]{1,0:T(8,128)S(1)} %bitcast.39, f32[1792,256]{1,0:T(8,128)} %all-gather.9.cloned.1.call-done, f32[14,1536]{1,0:T(8,128)} %shard_map.115, f32[14,256]{1,0:T(8,128)S(1)} %get-tuple-element.19), kind=kOutput, calls=%fused_computation.4 | convolution fusion | flops 77120512 | bytes 2050048 | tf_op jit(solution)/shard_map/dot_general | solution.py:209
  (50 shorter events, 15.1 us)
Async XLA Ops:
  7.2 0.7 copy-start
  7.2 69.6 %all-gather.5.cloned.1.call-start = ((), (), s32[]{:S(2)}) async-start(), calls=%async_computation | async-start | bytes 2359296 | tf_op jit(solution)/shard_map/all_gather | solution.py:141
  34.6 116.3 %all-gather.7.cloned.1.call-start = ((), (), s32[]{:S(2)}) async-start(), calls=%async_computation.1 | async-start | bytes 1179648 | tf_op jit(solution)/shard_map/all_gather | solution.py:141
  80.0 2.9 %copy-start.4 = (f32[256]{0:T(256)S(1)}, f32[256]{0:T(256)}, u32[]{:S(2)}) copy-start(f32[256]{0:T(256)} %param.16) | copy-start | bytes 3076
  80.4 32.9 %copy-start.1 = (bf16[2048,512]{1,0:T(8,128)(2,1)S(1)}, bf16[2048,512]{1,0:T(8,128)(2,1)}, u32[]{:S(2)}) copy-start(bf16[2048,512]{1,0:T(8,128)(2,1)} %all-gather.5.cloned.1.call-done) | copy-start | bytes 6291460
  113.3 120.0 %all-gather.9.cloned.1.call-start = ((), (), s32[]{:S(2)}) async-start(), calls=%async_computation.2 | async-start | bytes 2064384 | tf_op jit(solution)/shard_map/all_gather | solution.py:141
  126.1 2.0 copy-start.2
  196.4 37.0 %copy-start.3 = (f32[16,256]{1,0:T(8,128)S(1)}, f32[16,256]{1,0:T(8,128)}, u32[]{:S(2)}) copy-start(f32[16,256]{1,0:T(8,128)} %get-tuple-element.9) | copy-start | bytes 49156
Sparse Core Ops, SparseCore 0:
  34.7 42.0 all-gather.4
  113.4 34.9 all-gather.6
  195.4 37.9 all-gather.8

commit v8 on v7

--- a/solution.py
+++ b/solution.py
@@ -59,17 +59,20 @@
     )(*operands)
 
 
-def factor_kernel(m_in_ref, ps_ref, after_ref, pc_ref, piv_ref, scaled_ref, m_ref):
+def factor_kernel(block_ref, first_ref, ps_ref, pc_ref, piv_ref, scaled_ref, m_ref):
     rows, size = m_ref.shape
     half = size // 2
     below = rows - size
-    lanes_all = lax.broadcasted_iota(jnp.int32, (rows, size), 1)
-    row_all = lax.broadcasted_iota(jnp.int32, (rows, 1), 0)
-    m0 = m_in_ref[...]
+    own = first_ref.shape[0]
+    lanes_blk = lax.broadcasted_iota(jnp.int32, (size, size), 1)
+    row_blk = lax.broadcasted_iota(jnp.int32, (size, 1), 0)
     strength = ps_ref[...]
-    m0 = m0 + jnp.where((row_all % 2 == 0) & (lanes_all == row_all + 1) & (row_all < size), strength, 0.0)
-    m0 = m0 - jnp.where((row_all % 2 == 1) & (lanes_all == row_all - 1) & (row_all < size), strength, 0.0)
-    m_ref[...] = m0
+    m0 = block_ref[...]
+    m0 = m0 + jnp.where((row_blk % 2 == 0) & (lanes_blk == row_blk + 1), strength, 0.0)
+    m0 = m0 - jnp.where((row_blk % 2 == 1) & (lanes_blk == row_blk - 1), strength, 0.0)
+    m_ref[:size, :] = m0
+    m_ref[size:, :] = jnp.zeros((below, size), jnp.float32)
+    m_ref[size:size + own, :] = first_ref[:, :size]
     lane_full = lax.broadcasted_iota(jnp.int32, (1, size), 1)
     low_lanes = lax.broadcasted_iota(jnp.int32, (below, size), 1)
 
@@ -114,9 +117,9 @@
     scaled_ref[...] = scaled
 
 
-def factor_augmented(matrix, strength_col, size, after):
-    rows, width = matrix.shape
-    below = rows - size
+def factor_augmented(block, first, strength_col, below):
+    size, width = block.shape
+    rows = size + below
     vmem = pl.BlockSpec(memory_space=pltpu.VMEM)
     return pl.pallas_call(
         factor_kernel,
@@ -128,7 +131,7 @@
         in_specs=[vmem, vmem, vmem],
         out_specs=(vmem, vmem, vmem),
         scratch_shapes=[pltpu.VMEM((rows, width), jnp.float32)],
-    )(matrix, strength_col, after)
+    )(block, first, strength_col)
 
 
 def gather_rows(x, stages):
@@ -187,16 +190,10 @@
         blocks = electrons // width
         early = 1
         first_part = orbital_rows(tail_cols, mats, params, 0, 1 + early, width)
-        below_own = first_part[:, :panel]
         trailing_a = first_part[:, panel:]
         extra = (-tail) % 8
-        augmented = jnp.concatenate(
-            [block_rows, below_own, jnp.zeros((extra, panel), jnp.float32)], axis=0
-        )
-        strength_col = jnp.concatenate(
-            [jnp.repeat(pair_strength, 2), jnp.zeros((tail + extra,), jnp.float32)]
-        )[:, None]
-        pc, piv_row, scaled = factor_augmented(augmented, strength_col, panel, trailing_a[:8, :128])
+        strength_col = jnp.repeat(pair_strength, 2)[:, None]
+        pc, piv_row, scaled = factor_augmented(block_rows, first_part, strength_col, tail + extra)
         pivots = piv_row[0, : panel // 2]
         log_pivot = jnp.log(jnp.abs(pivots))
         panel_own = pc[:tail]

time: 244 us -> 243 us (level)
  transfers between devices with their start and end apart: 3 -> 3, of which waited for: 2 -> 2; matrix products, arithmetic and copies ran while one was open for 13% -> 12% of each run, Pallas kernels for 20% -> 20%
where the time goes in v8:
time: 243 us
  blocking collectives  74.1 us (30%)
  Pallas kernels  69.7 us (29%)
  waiting for transfers between devices  36.6 us (15%)
  local copies, waits for them, and re-layouts  33.6 us (14%)
  between operations  13.9 us (6%)
  other arithmetic  9.76 us (4%)
  matrix products  4.86 us (2%)
    all_gather x3, blocking collectives, gather_stages(): x = lax.all_gather(x, axes, axis=0, tiled=True)  74.1 us
    pallas_call x3, Pallas kernels, orbital_rows(): pl.pallas_call(orbital_kernel, grid=(blocks,), out_shape=jax.ShapeDtypeSt...  50.9 us
    all_gather x3, waiting for transfers between devices, gather_stages(): x = lax.all_gather(x, axes, axis=0, tiled=True)  36.5 us
    pallas_call x1, Pallas kernels, factor_augmented(): pl.pallas_call(factor_kernel, out_shape=(jax.ShapeDtypeStruct((below, wid...  18.8 us
    gather x2, local copies, waits for them, and re-layouts, on_device(): halves = 0.5 * jnp.take(late_every, perm, axis=0).astype(jnp.float32)  12.1 us
    unnamed x13, local copies, waits for them, and re-layouts  5.05 us
  transfers between devices with their start and end apart: 3, of which 2 were waited for; matrix products, arithmetic and copies ran while one was open for 12% of the time, Pallas kernels for 20%

profile of v8, /device:TPU:6, one launch (start us, length us, event | category | flops | bytes accessed | tf_op | source)
XLA Modules:
  0.0 242.6 jit_solution(3468012722408013822)
XLA Ops:
  7.9 1.1 fusion
  9.0 25.6 %all_gather.18 = bf16[256,512]{1,0:T(8,128)(2,1)} all-gather(bf16[16,512]{1,0:T(8,128)(2,1)S(1)} %fusion), channel_id=1, replica_groups=mesh['walker'=2,'z'=8,'x'=4,'y'=4] {'x','y'}, dimensions={0}, use_global_device_ids=true | all-gather | bytes 278528 | tf_op jit(solution)/shard_map/all_gather | solution.py:144
  36.1 1.0 copy.35
  42.0 34.8 %all-gather.5.cloned.1.call-done = bf16[2048,512]{1,0:T(8,128)(2,1)} async-done(((bf16[256,512]{1,0:T(8,128)(2,1)}), bf16[2048,512]{1,0:T(8,128)(2,1)}) %all-gather.5.cloned.1.call-update) | async-done | bytes 2097168 | tf_op jit(solution)/shard_map/all_gather | solution.py:144
  76.8 3.1 %gather_fusion = bf16[256,512]{1,0:T(8,128)(2,1)S(1)} fusion(bf16[2048,512]{1,0:T(8,128)(2,1)} %all-gather.5.cloned.1.call-done, s32[1024]{0:T(1024)S(1)} %pad_clamp_fusion), kind=kCustom, calls=%fused_computation | custom fusion | bytes 525312 | tf_op jit(solution)/shard_map/jit(_take)/gather | solution.py:177
  80.4 0.8 pad_maximum_fusion.1.mat_ref
  83.7 1.0 broadcast_in_dim.60.col_ref
  84.7 2.8 %shard_map.112 = f32[2,256]{1,0:T(2,128)} custom-call(f32[2,2,256,128]{3,2,1,0:T(8,128)} %broadcast_in_dim.60.col_ref, f32[2,256,256]{2,1,0:T(8,128)} %pad_maximum_fusion.1.mat_ref, f32[256,256]{1,0:T(8,128)} %broadcast_in_dim.61.bias_in_ref, bf16[256,256]{1,0:T(8,128)(2,1)} %multiply_bitcast_fusion.w_hid_t_ref, f32[256,256]{1,0:T(8,128)} %broadcast_in_dim.62.bias_hid_ref, ...), custom_call_target="tpu_custom_call" | custom-call | flops 137363456 | bytes 526336 | tf_op jit(solution)/shard_map/pallas_call | solution.py:48
  88.1 25.3 %all_gather.20 = f32[128,256]{1,0:T(8,128)} all-gather(f32[8,256]{1,0:T(8,128)S(1)} %pad.4), channel_id=1, replica_groups=mesh['walker'=2,'z'=8,'x'=4,'y'=4] {'x','y'}, dimensions={0}, use_global_device_ids=true | all-gather | bytes 139264 | tf_op jit(solution)/shard_map/all_gather | solution.py:144
  113.5 9.2 %gather_fusion.1 = bf16[2048,512]{1,0:T(8,128)(2,1)} fusion(bf16[2048,512]{1,0:T(8,128)(2,1)S(1)} %copy-done.1, s32[2048]{0:T(1024)S(1)} %fusion.4), kind=kCustom, calls=%fused_computation.1 | custom fusion | bytes 4202496 | tf_op jit(solution)/shard_map/jit(_take)/gather | solution.py:185
  122.7 2.9 %copy.36 = bf16[2048,512]{0,1:T(8,128)(2,1)S(1)} copy(bf16[2048,512]{1,0:T(8,128)(2,1)} %gather_fusion.1) | data formatting | bytes 4194304 | tf_op jit(solution)/shard_map/jit(_take)/gather | solution.py:185
  126.2 1.9 copy-done.2
  128.5 2.5 %slice_bitcast_fusion.1 = (f32[1,256,2048]{2,1,0:T(8,128)S(1)}, f32[1,256,2048]{2,1,0:T(8,128)S(1)}) fusion(f32[2048,512]{0,1:T(8,128)} %copy-done.2), kind=kLoop, calls=%fused_computation.6 | loop fusion | bytes 8388608 | tf_op jit(solution)/shard_map/stack | solution.py:169
  131.0 2.2 pad_maximum_fusion.mat_ref
  133.2 2.3 broadcast_in_dim.67.col_ref
  135.5 13.5 %shard_map.113.first_ref = f32[14,512]{1,0:T(8,128)} custom-call(f32[2,14,256,128]{3,2,1,0:T(8,128)} %broadcast_in_dim.67.col_ref, f32[2,256,2048]{2,1,0:T(8,128)} %pad_maximum_fusion.mat_ref, f32[256,256]{1,0:T(8,128)} %broadcast_in_dim.61.bias_in_ref, bf16[256,256]{1,0:T(8,128)(2,1)} %multiply_bitcast_fusion.w_hid_t_ref, ...), custom_call_target="tpu_custom_call" | custom-call | flops 1923088384 | bytes 1077248 | tf_op jit(solution)/shard_map/pallas_call | solution.py:48
  149.0 1.3 slice.62
  150.3 0.9 reshape.32.block_ref
  151.3 18.8 %shard_map.114 = (f32[16,256]{1,0:T(8,128)}, f32[1,256]{1,0:T(1,128)}, f32[16,256]{1,0:T(8,128)}) custom-call(f32[256,256]{1,0:T(8,128)} %reshape.32.block_ref, f32[14,512]{1,0:T(8,128)} %shard_map.113.first_ref, f32[256,1]{1,0:T(8,128)} %broadcast_in_dim_reshape.4.ps_ref), custom_call_target="tpu_custom_call" | custom-call | tf_op jit(solution)/shard_map/pallas_call | solution.py:124
  170.8 23.3 %all-gather = f32[16,14,256]{2,1,0:T(8,128)S(1)} all-gather(f32[1,14,256]{2,1,0:T(8,128)S(1)} %slice_bitcast_fusion.4), channel_id=1, replica_groups=mesh['walker'=2,'z'=8,'x'=4,'y'=4] {'x','y'}, dimensions={0}, use_global_device_ids=true | all-gather | bytes 243712 | tf_op jit(solution)/shard_map/all_gather | solution.py:144
  194.8 1.2 log_bitcast_fusion
  196.0 34.6 %shard_map.115 = f32[14,1536]{1,0:T(8,128)} custom-call(f32[2,14,256,128]{3,2,1,0:T(8,128)} %broadcast_in_dim.67.col_ref, f32[2,256,2048]{2,1,0:T(8,128)} %pad_maximum_fusion.mat_ref, f32[256,256]{1,0:T(8,128)} %broadcast_in_dim.61.bias_in_ref, bf16[256,256]{1,0:T(8,128)(2,1)} %multiply_bitcast_fusion.w_hid_t_ref, f32[256,256]{1,0:T(8,128)} %broadcast_in_dim.62.bias_hid_ref, ...), custom_call_target="tpu_custom_call" | custom-call | flops 5769265152 | bytes 3231744 | tf_op jit(solution)/shard_map/pallas_call | solution.py:48
  230.6 1.7 all-gather.9.cloned.1.call-done
  232.3 3.8 %convolution_subtract_fusion = f32[14,1792]{1,0:T(8,128)} fusion(f32[14,256]{1,0:T(8,128)S(1)} %bitcast.39, f32[1792,256]{1,0:T(8,128)} %all-gather.9.cloned.1.call-done, f32[14,1536]{1,0:T(8,128)} %shard_map.115, f32[14,256]{1,0:T(8,128)S(1)} %slice-done), kind=kOutput, calls=%fused_computation.4 | convolution fusion | flops 77120512 | bytes 2050048 | tf_op jit(solution)/shard_map/dot_general | solution.py:206
  (45 shorter events, 13.1 us)
Async XLA Ops:
  7.2 0.7 copy-start
  7.2 69.6 %all-gather.5.cloned.1.call-start = ((), (), s32[]{:S(2)}) async-start(), calls=%async_computation | async-start | bytes 2359296 | tf_op jit(solution)/shard_map/all_gather | solution.py:144
  34.6 114.5 %all-gather.7.cloned.1.call-start = ((), (), s32[]{:S(2)}) async-start(), calls=%async_computation.1 | async-start | bytes 1179648 | tf_op jit(solution)/shard_map/all_gather | solution.py:144
  80.0 2.9 %copy-start.4 = (f32[256]{0:T(256)S(1)}, f32[256]{0:T(256)}, u32[]{:S(2)}) copy-start(f32[256]{0:T(256)} %param.16) | copy-start | bytes 3076
  80.4 33.1 %copy-start.1 = (bf16[2048,512]{1,0:T(8,128)(2,1)S(1)}, bf16[2048,512]{1,0:T(8,128)(2,1)}, u32[]{:S(2)}) copy-start(bf16[2048,512]{1,0:T(8,128)(2,1)} %all-gather.5.cloned.1.call-done) | copy-start | bytes 6291460
  113.4 118.8 %all-gather.9.cloned.1.call-start = ((), (), s32[]{:S(2)}) async-start(), calls=%async_computation.2 | async-start | bytes 2064384 | tf_op jit(solution)/shard_map/all_gather | solution.py:144
  126.2 2.0 copy-start.2
  196.0 36.3 %slice-start = ((f32[14,512]{1,0:T(8,128)}), f32[14,256]{1,0:T(8,128)S(1)}, s32[]{:S(2)}) async-start(f32[14,512]{1,0:T(8,128)} %shard_map.113.first_ref), calls=%async_computation.3 | async-start | bytes 32768 | tf_op jit(solution)/shard_map/slice | solution.py:193
  196.0 36.3 %copy-start.3 = (f32[16,256]{1,0:T(8,128)S(1)}, f32[16,256]{1,0:T(8,128)}, u32[]{:S(2)}) copy-start(f32[16,256]{1,0:T(8,128)} %get-tuple-element.9) | copy-start | bytes 49156
Sparse Core Ops, SparseCore 0:
  34.7 42.0 all-gather.4
  113.6 35.2 all-gather.6
  194.9 37.3 all-gather.8

commit v9 on v8

--- a/solution.py
+++ b/solution.py
@@ -1,3 +1,5 @@
+import functools
+
 import numpy as np
 import jax
 import jax.numpy as jnp
@@ -59,7 +61,7 @@
     )(*operands)
 
 
-def factor_kernel(block_ref, first_ref, ps_ref, pc_ref, piv_ref, scaled_ref, m_ref):
+def factor_kernel(share, block_ref, first_ref, ps_ref, pc_ref, piv_ref, scaled_ref, m_ref):
     rows, size = m_ref.shape
     half = size // 2
     below = rows - size
@@ -67,7 +69,11 @@
     lanes_blk = lax.broadcasted_iota(jnp.int32, (size, size), 1)
     row_blk = lax.broadcasted_iota(jnp.int32, (size, 1), 0)
     strength = ps_ref[...]
-    m0 = block_ref[...]
+    stride = block_ref.shape[0] * share // size
+
+    for g in range(size // share):
+        m_ref[g * share:(g + 1) * share, :] = block_ref[g * stride:g * stride + share, :]
+    m0 = m_ref[:size, :]
     m0 = m0 + jnp.where((row_blk % 2 == 0) & (lanes_blk == row_blk + 1), strength, 0.0)
     m0 = m0 - jnp.where((row_blk % 2 == 1) & (lanes_blk == row_blk - 1), strength, 0.0)
     m_ref[:size, :] = m0
@@ -117,12 +123,13 @@
     scaled_ref[...] = scaled
 
 
-def factor_augmented(block, first, strength_col, below):
-    size, width = block.shape
+def factor_augmented(block, first, strength_col, below, share):
+    width = block.shape[1]
+    size = width
     rows = size + below
     vmem = pl.BlockSpec(memory_space=pltpu.VMEM)
     return pl.pallas_call(
-        factor_kernel,
+        functools.partial(factor_kernel, share),
         out_shape=(
             jax.ShapeDtypeStruct((below, width), jnp.float32),
             jax.ShapeDtypeStruct((1, width), jnp.float32),
@@ -186,14 +193,13 @@
         mats = transposed(halves)
         tail_own = lax.dynamic_slice_in_dim(halves, panel + device * tail, tail, 0)
         tail_cols = columns(tail_own)
-        block_rows = gathered.reshape(groups, share + pad, panel)[:, :share, :].reshape(panel, panel)
         blocks = electrons // width
         early = 1
         first_part = orbital_rows(tail_cols, mats, params, 0, 1 + early, width)
         trailing_a = first_part[:, panel:]
         extra = (-tail) % 8
         strength_col = jnp.repeat(pair_strength, 2)[:, None]
-        pc, piv_row, scaled = factor_augmented(block_rows, first_part, strength_col, tail + extra)
+        pc, piv_row, scaled = factor_augmented(gathered, first_part, strength_col, tail + extra, share)
         pivots = piv_row[0, : panel // 2]
         log_pivot = jnp.log(jnp.abs(pivots))
         panel_own = pc[:tail]

time: 243 us -> 241 us (level)
  no operation moved by 1% of the time
where the time goes in v9:
time: 241 us; the launch traced here: 240 us
  blocking collectives  74.1 us (31%)
  Pallas kernels  69.9 us (29%)
  waiting for transfers between devices  36.4 us (15%)
  local copies, waits for them, and re-layouts  31.4 us (13%)
  between operations  13.9 us (6%)
  other arithmetic  9.76 us (4%)
  matrix products  4.86 us (2%)
    all_gather x3, blocking collectives, gather_stages(): x = lax.all_gather(x, axes, axis=0, tiled=True)  74.1 us
    pallas_call x3, Pallas kernels, orbital_rows(): pl.pallas_call(orbital_kernel, grid=(blocks,), out_shape=jax.ShapeDtypeSt...  50.9 us
    all_gather x3, waiting for transfers between devices, gather_stages(): x = lax.all_gather(x, axes, axis=0, tiled=True)  36.3 us
    pallas_call x1, Pallas kernels, factor_augmented(): pl.pallas_call(functools.partial(factor_kernel, share), out_shape=(jax.Sh...  19.1 us
    gather x2, local copies, waits for them, and re-layouts, on_device(): halves = 0.5 * jnp.take(late_every, perm, axis=0).astype(jnp.float32)  12.1 us
    unnamed x13, local copies, waits for them, and re-layouts  5.05 us
  transfers between devices with their start and end apart: 3, of which 2 were waited for; matrix products, arithmetic and copies ran while one was open for 12% of the time, Pallas kernels for 20%

profile of v9, /device:TPU:6, one launch (start us, length us, event | category | flops | bytes accessed | tf_op | source)
XLA Modules:
  0.0 240.5 jit_solution(12941750424602562655)
XLA Ops:
  7.9 1.1 fusion
  9.0 25.6 %all_gather.18 = bf16[256,512]{1,0:T(8,128)(2,1)} all-gather(bf16[16,512]{1,0:T(8,128)(2,1)S(1)} %fusion), channel_id=1, replica_groups=mesh['walker'=2,'z'=8,'x'=4,'y'=4] {'x','y'}, dimensions={0}, use_global_device_ids=true | all-gather | bytes 278528 | tf_op jit(solution)/shard_map/all_gather | solution.py:151
  36.1 1.0 copy.35
  42.0 34.8 %all-gather.5.cloned.1.call-done = bf16[2048,512]{1,0:T(8,128)(2,1)} async-done(((bf16[256,512]{1,0:T(8,128)(2,1)}), bf16[2048,512]{1,0:T(8,128)(2,1)}) %all-gather.5.cloned.1.call-update) | async-done | bytes 2097168 | tf_op jit(solution)/shard_map/all_gather | solution.py:151
  76.8 3.1 %gather_fusion = bf16[256,512]{1,0:T(8,128)(2,1)S(1)} fusion(bf16[2048,512]{1,0:T(8,128)(2,1)} %all-gather.5.cloned.1.call-done, s32[1024]{0:T(1024)S(1)} %pad_clamp_fusion), kind=kCustom, calls=%fused_computation | custom fusion | bytes 525312 | tf_op jit(solution)/shard_map/jit(_take)/gather | solution.py:184
  80.4 0.8 pad_maximum_fusion.1.mat_ref
  82.1 0.8 broadcast_in_dim.61.bias_in_ref
  82.9 0.8 broadcast_in_dim.63.w_out_ref
  83.7 1.0 broadcast_in_dim.60.col_ref
  84.7 2.8 %shard_map.112 = f32[2,256]{1,0:T(2,128)} custom-call(f32[2,2,256,128]{3,2,1,0:T(8,128)} %broadcast_in_dim.60.col_ref, f32[2,256,256]{2,1,0:T(8,128)} %pad_maximum_fusion.1.mat_ref, f32[256,256]{1,0:T(8,128)} %broadcast_in_dim.61.bias_in_ref, bf16[256,256]{1,0:T(8,128)(2,1)} %multiply_bitcast_fusion.w_hid_t_ref, f32[256,256]{1,0:T(8,128)} %broadcast_in_dim.62.bias_hid_ref, ...), custom_call_target="tpu_custom_call" | custom-call | flops 137363456 | bytes 526336 | tf_op jit(solution)/shard_map/pallas_call | solution.py:50
  88.1 25.3 %all_gather.20 = f32[128,256]{1,0:T(8,128)} all-gather(f32[8,256]{1,0:T(8,128)S(1)} %pad.4), channel_id=1, replica_groups=mesh['walker'=2,'z'=8,'x'=4,'y'=4] {'x','y'}, dimensions={0}, use_global_device_ids=true | all-gather | bytes 139264 | tf_op jit(solution)/shard_map/all_gather | solution.py:151
  113.5 9.2 %gather_fusion.1 = bf16[2048,512]{1,0:T(8,128)(2,1)} fusion(bf16[2048,512]{1,0:T(8,128)(2,1)S(1)} %copy-done.1, s32[2048]{0:T(1024)S(1)} %fusion.4), kind=kCustom, calls=%fused_computation.1 | custom fusion | bytes 4202496 | tf_op jit(solution)/shard_map/jit(_take)/gather | solution.py:192
  122.7 2.9 %copy.36 = bf16[2048,512]{0,1:T(8,128)(2,1)S(1)} copy(bf16[2048,512]{1,0:T(8,128)(2,1)} %gather_fusion.1) | data formatting | bytes 4194304 | tf_op jit(solution)/shard_map/jit(_take)/gather | solution.py:192
  126.2 1.9 copy-done.2
  128.5 2.5 %slice_bitcast_fusion.1 = (f32[1,256,2048]{2,1,0:T(8,128)S(1)}, f32[1,256,2048]{2,1,0:T(8,128)S(1)}) fusion(f32[2048,512]{0,1:T(8,128)} %copy-done.2), kind=kLoop, calls=%fused_computation.6 | loop fusion | bytes 8388608 | tf_op jit(solution)/shard_map/stack | solution.py:176
  131.0 2.2 pad_maximum_fusion.mat_ref
  133.2 2.3 broadcast_in_dim.67.col_ref
  135.5 13.5 %shard_map.113.first_ref = f32[14,512]{1,0:T(8,128)} custom-call(f32[2,14,256,128]{3,2,1,0:T(8,128)} %broadcast_in_dim.67.col_ref, f32[2,256,2048]{2,1,0:T(8,128)} %pad_maximum_fusion.mat_ref, f32[256,256]{1,0:T(8,128)} %broadcast_in_dim.61.bias_in_ref, bf16[256,256]{1,0:T(8,128)(2,1)} %multiply_bitcast_fusion.w_hid_t_ref, ...), custom_call_target="tpu_custom_call" | custom-call | flops 1923088384 | bytes 1077248 | tf_op jit(solution)/shard_map/pallas_call | solution.py:50
  149.0 19.1 %shard_map.114 = (f32[16,256]{1,0:T(8,128)}, f32[1,256]{1,0:T(1,128)}, f32[16,256]{1,0:T(8,128)}) custom-call(f32[1024,256]{1,0:T(8,128)} %all-gather.7.cloned.1.call-done.block_ref, f32[14,512]{1,0:T(8,128)} %shard_map.113.first_ref, f32[256,1]{1,0:T(8,128)} %broadcast_in_dim_reshape.4.ps_ref), custom_call_target="tpu_custom_call" | custom-call | tf_op jit(solution)/shard_map/pallas_call | solution.py:131
  168.8 23.3 %all-gather = f32[16,14,256]{2,1,0:T(8,128)S(1)} all-gather(f32[1,14,256]{2,1,0:T(8,128)S(1)} %slice_bitcast_fusion.4), channel_id=1, replica_groups=mesh['walker'=2,'z'=8,'x'=4,'y'=4] {'x','y'}, dimensions={0}, use_global_device_ids=true | all-gather | bytes 243712 | tf_op jit(solution)/shard_map/all_gather | solution.py:151
  192.9 1.2 log_bitcast_fusion
  194.1 34.6 %shard_map.115 = f32[14,1536]{1,0:T(8,128)} custom-call(f32[2,14,256,128]{3,2,1,0:T(8,128)} %broadcast_in_dim.67.col_ref, f32[2,256,2048]{2,1,0:T(8,128)} %pad_maximum_fusion.mat_ref, f32[256,256]{1,0:T(8,128)} %broadcast_in_dim.61.bias_in_ref, bf16[256,256]{1,0:T(8,128)(2,1)} %multiply_bitcast_fusion.w_hid_t_ref, f32[256,256]{1,0:T(8,128)} %broadcast_in_dim.62.bias_hid_ref, ...), custom_call_target="tpu_custom_call" | custom-call | flops 5769265152 | bytes 3231744 | tf_op jit(solution)/shard_map/pallas_call | solution.py:50
  228.6 1.5 all-gather.9.cloned.1.call-done
  230.2 3.8 %convolution_subtract_fusion = f32[14,1792]{1,0:T(8,128)} fusion(f32[14,256]{1,0:T(8,128)S(1)} %bitcast.37, f32[1792,256]{1,0:T(8,128)} %all-gather.9.cloned.1.call-done, f32[14,1536]{1,0:T(8,128)} %shard_map.115, f32[14,256]{1,0:T(8,128)S(1)} %slice-done), kind=kOutput, calls=%fused_computation.4 | convolution fusion | flops 77120512 | bytes 2050048 | tf_op jit(solution)/shard_map/dot_general | solution.py:212
  (43 shorter events, 11.5 us)
Async XLA Ops:
  7.2 0.7 copy-start
  7.2 69.6 %all-gather.5.cloned.1.call-start = ((), (), s32[]{:S(2)}) async-start(), calls=%async_computation | async-start | bytes 2359296 | tf_op jit(solution)/shard_map/all_gather | solution.py:151
  34.6 114.5 %all-gather.7.cloned.1.call-start = ((), (), s32[]{:S(2)}) async-start(), calls=%async_computation.1 | async-start | bytes 1179648 | tf_op jit(solution)/shard_map/all_gather | solution.py:151
  80.0 2.9 %copy-start.4 = (f32[256]{0:T(256)S(1)}, f32[256]{0:T(256)}, u32[]{:S(2)}) copy-start(f32[256]{0:T(256)} %param.16) | copy-start | bytes 3076
  80.4 33.1 %copy-start.1 = (bf16[2048,512]{1,0:T(8,128)(2,1)S(1)}, bf16[2048,512]{1,0:T(8,128)(2,1)}, u32[]{:S(2)}) copy-start(bf16[2048,512]{1,0:T(8,128)(2,1)} %all-gather.5.cloned.1.call-done) | copy-start | bytes 6291460
  113.4 116.7 %all-gather.9.cloned.1.call-start = ((), (), s32[]{:S(2)}) async-start(), calls=%async_computation.2 | async-start | bytes 2064384 | tf_op jit(solution)/shard_map/all_gather | solution.py:151
  126.2 2.0 copy-start.2
  194.1 36.1 %slice-start = ((f32[14,512]{1,0:T(8,128)}), f32[14,256]{1,0:T(8,128)S(1)}, s32[]{:S(2)}) async-start(f32[14,512]{1,0:T(8,128)} %shard_map.113.first_ref), calls=%async_computation.3 | async-start | bytes 32768 | tf_op jit(solution)/shard_map/slice | solution.py:199
  194.1 36.1 %copy-start.3 = (f32[16,256]{1,0:T(8,128)S(1)}, f32[16,256]{1,0:T(8,128)}, u32[]{:S(2)}) copy-start(f32[16,256]{1,0:T(8,128)} %get-tuple-element.9) | copy-start | bytes 49156
Sparse Core Ops, SparseCore 0:
  34.7 42.0 all-gather.4
  113.6 35.2 all-gather.6
  193.0 37.1 all-gather.8

commit v10 on v9

--- a/solution.py
+++ b/solution.py
@@ -164,7 +164,8 @@
         tail = (electrons - panel) // groups
         w_both = jnp.concatenate([w_left, w_right], axis=1)
         both_own = jnp.dot(feats, w_both, preferred_element_type=jnp.float32).astype(jnp.bfloat16)
-        both_every = gather_rows(both_own, stages)
+        lr_partial = gather_stages(both_own, stages)
+        both_every = lr_partial[-1]
         width = panel
         lanes = 128
 
@@ -181,6 +182,7 @@
             jnp.broadcast_to(0.5 * bias_hidden[:, None], (hid, width)),
             jnp.broadcast_to(w_out[:, None], (hid, width)),
         )
+        _, params = lax.optimization_barrier((lr_partial[0], params))
         top_both = 0.5 * jnp.take(both_every, perm[:panel], axis=0).astype(jnp.float32)
         top_own = lax.dynamic_slice_in_dim(top_both, device * share, share, 0)
         top_rows = orbital_rows(columns(top_own), transposed(top_both), params, 0, 1, width)

time: 241 us -> 238 us (0.988)
  other arithmetic: 9.76 us -> 6.94 us
    unnamed x13 -> x15, local copies, waits for them, and re-layouts: 5.05 us -> 5.02 us
where the time goes in v10:
time: 238 us
  blocking collectives  74.1 us (31%)
  Pallas kernels  69.9 us (29%)
  waiting for transfers between devices  36.8 us (15%)
  local copies, waits for them, and re-layouts  31.3 us (13%)
  between operations  13.9 us (6%)
  other arithmetic  6.94 us (3%)
  matrix products  4.86 us (2%)
    all_gather x3, blocking collectives, gather_stages(): x = lax.all_gather(x, axes, axis=0, tiled=True)  74.1 us
    pallas_call x3, Pallas kernels, orbital_rows(): pl.pallas_call(orbital_kernel, grid=(blocks,), out_shape=jax.ShapeDtypeSt...  50.9 us
    all_gather x3, waiting for transfers between devices, gather_stages(): x = lax.all_gather(x, axes, axis=0, tiled=True)  36.8 us
    pallas_call x1, Pallas kernels, factor_augmented(): pl.pallas_call(functools.partial(factor_kernel, share), out_shape=(jax.Sh...  19.1 us
    gather x2, local copies, waits for them, and re-layouts, on_device(): halves = 0.5 * jnp.take(late_every, perm, axis=0).astype(jnp.float32)  12.1 us
    unnamed x15, local copies, waits for them, and re-layouts  5.02 us
  transfers between devices with their start and end apart: 3, of which 2 were waited for; matrix products, arithmetic and copies ran while one was open for 12% of the time, Pallas kernels for 20%

profile of v10, /device:TPU:6, one launch (start us, length us, event | category | flops | bytes accessed | tf_op | source)
XLA Modules:
  0.0 237.9 jit_solution(4432007925088055419)
XLA Ops:
  7.9 1.1 fusion
  9.0 25.6 %all_gather.18 = bf16[256,512]{1,0:T(8,128)(2,1)} all-gather(bf16[16,512]{1,0:T(8,128)(2,1)S(1)} %fusion), channel_id=1, replica_groups=mesh['walker'=2,'z'=8,'x'=4,'y'=4] {'x','y'}, dimensions={0}, use_global_device_ids=true | all-gather | bytes 278528 | tf_op jit(solution)/shard_map/all_gather | solution.py:151
  36.1 1.0 copy.35
  39.2 0.8 broadcast_in_dim.62.bias_hid_ref
  40.8 0.8 broadcast_in_dim.63.w_out_ref
  41.6 35.1 %all-gather.5.cloned.1.call-done = bf16[2048,512]{1,0:T(8,128)(2,1)} async-done(((bf16[256,512]{1,0:T(8,128)(2,1)}), bf16[2048,512]{1,0:T(8,128)(2,1)}) %all-gather.5.cloned.1.call-update) | async-done | bytes 2097168 | tf_op jit(solution)/shard_map/all_gather | solution.py:151
  76.8 3.1 %gather_fusion = bf16[256,512]{1,0:T(8,128)(2,1)S(1)} fusion(bf16[2048,512]{1,0:T(8,128)(2,1)} %all-gather.5.cloned.1.call-done, s32[1024]{0:T(1024)S(1)} %pad_clamp_fusion), kind=kCustom, calls=%fused_computation | custom fusion | bytes 525312 | tf_op jit(solution)/shard_map/jit(_take)/gather | solution.py:186
  80.4 0.8 pad_maximum_fusion.1.mat_ref
  81.2 1.0 broadcast_in_dim.60.col_ref
  82.2 2.8 %shard_map.112 = f32[2,256]{1,0:T(2,128)} custom-call(f32[2,2,256,128]{3,2,1,0:T(8,128)} %broadcast_in_dim.60.col_ref, f32[2,256,256]{2,1,0:T(8,128)} %pad_maximum_fusion.1.mat_ref, f32[256,256]{1,0:T(8,128)} %broadcast_in_dim.61.bias_in_ref, bf16[256,256]{1,0:T(8,128)(2,1)} %multiply_bitcast_fusion.w_hid_t_ref, f32[256,256]{1,0:T(8,128)} %broadcast_in_dim.62.bias_hid_ref, ...), custom_call_target="tpu_custom_call" | custom-call | flops 137363456 | bytes 526336 | tf_op jit(solution)/shard_map/pallas_call | solution.py:50
  85.7 25.2 %all_gather.20 = f32[128,256]{1,0:T(8,128)} all-gather(f32[8,256]{1,0:T(8,128)S(1)} %pad.4), channel_id=1, replica_groups=mesh['walker'=2,'z'=8,'x'=4,'y'=4] {'x','y'}, dimensions={0}, use_global_device_ids=true | all-gather | bytes 139264 | tf_op jit(solution)/shard_map/all_gather | solution.py:151
  111.0 9.1 %gather_fusion.1 = bf16[2048,512]{1,0:T(8,128)(2,1)} fusion(bf16[2048,512]{1,0:T(8,128)(2,1)S(1)} %copy-done.1, s32[2048]{0:T(1024)S(1)} %fusion.4), kind=kCustom, calls=%fused_computation.1 | custom fusion | bytes 4202496 | tf_op jit(solution)/shard_map/jit(_take)/gather | solution.py:194
  120.1 2.9 %copy.36 = bf16[2048,512]{0,1:T(8,128)(2,1)S(1)} copy(bf16[2048,512]{1,0:T(8,128)(2,1)} %gather_fusion.1) | data formatting | bytes 4194304 | tf_op jit(solution)/shard_map/jit(_take)/gather | solution.py:194
  123.7 1.9 copy-done.2
  125.9 2.5 %slice_bitcast_fusion.1 = (f32[1,256,2048]{2,1,0:T(8,128)S(1)}, f32[1,256,2048]{2,1,0:T(8,128)S(1)}) fusion(f32[2048,512]{0,1:T(8,128)} %copy-done.2), kind=kLoop, calls=%fused_computation.6 | loop fusion | bytes 8388608 | tf_op jit(solution)/shard_map/stack | solution.py:177
  128.4 2.2 pad_maximum_fusion.mat_ref
  130.6 2.3 broadcast_in_dim.67.col_ref
  133.0 13.5 %shard_map.113.first_ref = f32[14,512]{1,0:T(8,128)} custom-call(f32[2,14,256,128]{3,2,1,0:T(8,128)} %broadcast_in_dim.67.col_ref, f32[2,256,2048]{2,1,0:T(8,128)} %pad_maximum_fusion.mat_ref, f32[256,256]{1,0:T(8,128)} %broadcast_in_dim.61.bias_in_ref, bf16[256,256]{1,0:T(8,128)(2,1)} %multiply_bitcast_fusion.w_hid_t_ref, ...), custom_call_target="tpu_custom_call" | custom-call | flops 1923088384 | bytes 1077248 | tf_op jit(solution)/shard_map/pallas_call | solution.py:50
  146.5 19.1 %shard_map.114 = (f32[16,256]{1,0:T(8,128)}, f32[1,256]{1,0:T(1,128)}, f32[16,256]{1,0:T(8,128)}) custom-call(f32[1024,256]{1,0:T(8,128)} %all-gather.7.cloned.1.call-done.block_ref, f32[14,512]{1,0:T(8,128)} %shard_map.113.first_ref, f32[256,1]{1,0:T(8,128)} %broadcast_in_dim_reshape.4.ps_ref), custom_call_target="tpu_custom_call" | custom-call | tf_op jit(solution)/shard_map/pallas_call | solution.py:131
  166.3 23.3 %all-gather = f32[16,14,256]{2,1,0:T(8,128)S(1)} all-gather(f32[1,14,256]{2,1,0:T(8,128)S(1)} %slice_bitcast_fusion.4), channel_id=1, replica_groups=mesh['walker'=2,'z'=8,'x'=4,'y'=4] {'x','y'}, dimensions={0}, use_global_device_ids=true | all-gather | bytes 243712 | tf_op jit(solution)/shard_map/all_gather | solution.py:151
  190.3 1.1 log_bitcast_fusion
  191.4 34.6 %shard_map.115 = f32[14,1536]{1,0:T(8,128)} custom-call(f32[2,14,256,128]{3,2,1,0:T(8,128)} %broadcast_in_dim.67.col_ref, f32[2,256,2048]{2,1,0:T(8,128)} %pad_maximum_fusion.mat_ref, f32[256,256]{1,0:T(8,128)} %broadcast_in_dim.61.bias_in_ref, bf16[256,256]{1,0:T(8,128)(2,1)} %multiply_bitcast_fusion.w_hid_t_ref, f32[256,256]{1,0:T(8,128)} %broadcast_in_dim.62.bias_hid_ref, ...), custom_call_target="tpu_custom_call" | custom-call | flops 5769265152 | bytes 3231744 | tf_op jit(solution)/shard_map/pallas_call | solution.py:50
  226.0 1.6 all-gather.9.cloned.1.call-done
  227.6 3.8 %convolution_subtract_fusion = f32[14,1792]{1,0:T(8,128)} fusion(f32[14,256]{1,0:T(8,128)S(1)} %bitcast.37, f32[1792,256]{1,0:T(8,128)} %all-gather.9.cloned.1.call-done, f32[14,1536]{1,0:T(8,128)} %shard_map.115, f32[14,256]{1,0:T(8,128)S(1)} %slice-done), kind=kOutput, calls=%fused_computation.4 | convolution fusion | flops 77120512 | bytes 2050048 | tf_op jit(solution)/shard_map/dot_general | solution.py:214
  (45 shorter events, 8.7 us)
Async XLA Ops:
  7.2 0.7 copy-start
  7.2 33.6 %copy-start.5 = (f32[256]{0:T(256)S(1)}, f32[256]{0:T(256)}, u32[]{:S(2)}) copy-start(f32[256]{0:T(256)} %param.16) | copy-start | bytes 3076
  7.2 34.4 %copy-start.3 = (s32[2048]{0:T(1024)S(1)}, s32[2048]{0:T(1024)}, u32[]{:S(2)}) copy-start(s32[2048]{0:T(1024)} %param.10) | copy-start | bytes 24580
  7.2 69.6 %all-gather.5.cloned.1.call-start = ((), (), s32[]{:S(2)}) async-start(), calls=%async_computation | async-start | bytes 2359296 | tf_op jit(solution)/shard_map/all_gather | solution.py:151
  34.6 111.9 %all-gather.7.cloned.1.call-start = ((), (), s32[]{:S(2)}) async-start(), calls=%async_computation.1 | async-start | bytes 1179648 | tf_op jit(solution)/shard_map/all_gather | solution.py:151
  80.2 30.8 %copy-start.1 = (bf16[2048,512]{1,0:T(8,128)(2,1)S(1)}, bf16[2048,512]{1,0:T(8,128)(2,1)}, u32[]{:S(2)}) copy-start(bf16[2048,512]{1,0:T(8,128)(2,1)} %all-gather.5.cloned.1.call-done) | copy-start | bytes 6291460
  110.9 116.7 %all-gather.9.cloned.1.call-start = ((), (), s32[]{:S(2)}) async-start(), calls=%async_computation.2 | async-start | bytes 2064384 | tf_op jit(solution)/shard_map/all_gather | solution.py:151
  123.7 1.9 copy-start.2
  191.4 36.2 %slice-start = ((f32[14,512]{1,0:T(8,128)}), f32[14,256]{1,0:T(8,128)S(1)}, s32[]{:S(2)}) async-start(f32[14,512]{1,0:T(8,128)} %shard_map.113.first_ref), calls=%async_computation.3 | async-start | bytes 32768 | tf_op jit(solution)/shard_map/slice | solution.py:201
  191.4 36.2 %copy-start.4 = (f32[16,256]{1,0:T(8,128)S(1)}, f32[16,256]{1,0:T(8,128)}, u32[]{:S(2)}) copy-start(f32[16,256]{1,0:T(8,128)} %get-tuple-element.17) | copy-start | bytes 49156
Sparse Core Ops, SparseCore 0:
  34.7 41.9 all-gather.4
  111.1 35.1 all-gather.6
  190.4 37.1 all-gather.8

commit v11 on v10

--- a/solution.py
+++ b/solution.py
@@ -183,7 +183,10 @@
             jnp.broadcast_to(w_out[:, None], (hid, width)),
         )
         _, params = lax.optimization_barrier((lr_partial[0], params))
-        top_both = 0.5 * jnp.take(both_every, perm[:panel], axis=0).astype(jnp.float32)
+        selector = jnp.where(
+            jnp.arange(electrons, dtype=perm.dtype)[None, :] == perm[:panel, None], 0.5, 0.0
+        ).astype(jnp.bfloat16)
+        top_both = jnp.dot(selector, both_every, preferred_element_type=jnp.float32)
         top_own = lax.dynamic_slice_in_dim(top_both, device * share, share, 0)
         top_rows = orbital_rows(columns(top_own), transposed(top_both), params, 0, 1, width)
         pad = (-share) % 8

time: 238 us -> 238 us (level)
  local copies, waits for them, and re-layouts: 31.3 us -> 28.1 us
    gather x2 -> x0, local copies, waits for them, and re-layouts: 3.2 us -> none  [on_device(): jnp.take(both_every, perm[:panel], axis=0).astype(jnp.float32)]
    unnamed x15 -> x17, local copies, waits for them, and re-layouts: 5.02 us -> 5.24 us
where the time goes in v11:
time: 238 us; the launch traced here: 237 us
  blocking collectives  74.2 us (31%)
  Pallas kernels  70 us (29%)
  waiting for transfers between devices  36.7 us (15%)
  local copies, waits for them, and re-layouts  28.1 us (12%)
  between operations  13.9 us (6%)
  matrix products  7.19 us (3%)
  other arithmetic  6.87 us (3%)
    all_gather x3, blocking collectives, gather_stages(): x = lax.all_gather(x, axes, axis=0, tiled=True)  74.2 us
    pallas_call x3, Pallas kernels, orbital_rows(): pl.pallas_call(orbital_kernel, grid=(blocks,), out_shape=jax.ShapeDtypeSt...  50.9 us
    all_gather x3, waiting for transfers between devices, gather_stages(): x = lax.all_gather(x, axes, axis=0, tiled=True)  36.7 us
    pallas_call x1, Pallas kernels, factor_augmented(): pl.pallas_call(functools.partial(factor_kernel, share), out_shape=(jax.Sh...  19.1 us
    gather x2, local copies, waits for them, and re-layouts, on_device(): halves = 0.5 * jnp.take(late_every, perm, axis=0).astype(jnp.float32)  12.1 us
    unnamed x17, local copies, waits for them, and re-layouts  5.24 us
  transfers between devices with their start and end apart: 3, of which 2 were waited for; matrix products, arithmetic and copies ran while one was open for 12% of the time, Pallas kernels for 20%

profile of v11, /device:TPU:6, one launch (start us, length us, event | category | flops | bytes accessed | tf_op | source)
XLA Modules:
  0.0 237.1 jit_solution(18045163241338010853)
XLA Ops:
  7.9 1.1 fusion
  9.0 25.6 %all_gather.18 = bf16[256,512]{1,0:T(8,128)(2,1)} all-gather(bf16[16,512]{1,0:T(8,128)(2,1)S(1)} %fusion), channel_id=1, replica_groups=mesh['walker'=2,'z'=8,'x'=4,'y'=4] {'x','y'}, dimensions={0}, use_global_device_ids=true | all-gather | bytes 278528 | tf_op jit(solution)/shard_map/all_gather | solution.py:151
  36.2 1.0 copy.33
  39.2 0.8 broadcast_in_dim.59.bias_hid_ref
  40.8 0.8 broadcast_in_dim.60.w_out_ref
  41.6 35.1 %all-gather.5.cloned.1.call-done = bf16[2048,512]{1,0:T(8,128)(2,1)} async-done(((bf16[256,512]{1,0:T(8,128)(2,1)}), bf16[2048,512]{1,0:T(8,128)(2,1)}) %all-gather.5.cloned.1.call-update) | async-done | bytes 2097168 | tf_op jit(solution)/shard_map/all_gather | solution.py:151
  76.7 2.3 fusion.1
  79.5 0.8 pad_maximum_fusion.1.mat_ref
  80.3 1.0 broadcast_in_dim.57.col_ref
  81.3 2.8 %shard_map.112 = f32[2,256]{1,0:T(2,128)} custom-call(f32[2,2,256,128]{3,2,1,0:T(8,128)} %broadcast_in_dim.57.col_ref, f32[2,256,256]{2,1,0:T(8,128)} %pad_maximum_fusion.1.mat_ref, f32[256,256]{1,0:T(8,128)} %broadcast_in_dim.58.bias_in_ref, bf16[256,256]{1,0:T(8,128)(2,1)} %multiply_bitcast_fusion.w_hid_t_ref, f32[256,256]{1,0:T(8,128)} %broadcast_in_dim.59.bias_hid_ref, ...), custom_call_target="tpu_custom_call" | custom-call | flops 137363456 | bytes 526336 | tf_op jit(solution)/shard_map/pallas_call | solution.py:50
  84.8 25.2 %all_gather.20 = f32[128,256]{1,0:T(8,128)} all-gather(f32[8,256]{1,0:T(8,128)S(1)} %pad.4), channel_id=1, replica_groups=mesh['walker'=2,'z'=8,'x'=4,'y'=4] {'x','y'}, dimensions={0}, use_global_device_ids=true | all-gather | bytes 139264 | tf_op jit(solution)/shard_map/all_gather | solution.py:151
  110.0 9.2 %gather_fusion = bf16[2048,512]{1,0:T(8,128)(2,1)} fusion(bf16[2048,512]{1,0:T(8,128)(2,1)S(1)} %copy-done.1, s32[2048]{0:T(1024)S(1)} %fusion.8), kind=kCustom, calls=%fused_computation | custom fusion | bytes 4202496 | tf_op jit(solution)/shard_map/jit(_take)/gather | solution.py:197
  119.2 2.9 %copy.34 = bf16[2048,512]{0,1:T(8,128)(2,1)S(1)} copy(bf16[2048,512]{1,0:T(8,128)(2,1)} %gather_fusion) | data formatting | bytes 4194304 | tf_op jit(solution)/shard_map/jit(_take)/gather | solution.py:197
  122.8 1.9 copy-done.2
  125.0 2.5 %slice_bitcast_fusion.1 = (f32[1,256,2048]{2,1,0:T(8,128)S(1)}, f32[1,256,2048]{2,1,0:T(8,128)S(1)}) fusion(f32[2048,512]{0,1:T(8,128)} %copy-done.2), kind=kLoop, calls=%fused_computation.5 | loop fusion | bytes 8388608 | tf_op jit(solution)/shard_map/stack | solution.py:177
  127.5 2.2 pad_maximum_fusion.mat_ref
  129.7 2.4 broadcast_in_dim.64.col_ref
  132.0 13.5 %shard_map.113.first_ref = f32[14,512]{1,0:T(8,128)} custom-call(f32[2,14,256,128]{3,2,1,0:T(8,128)} %broadcast_in_dim.64.col_ref, f32[2,256,2048]{2,1,0:T(8,128)} %pad_maximum_fusion.mat_ref, f32[256,256]{1,0:T(8,128)} %broadcast_in_dim.58.bias_in_ref, bf16[256,256]{1,0:T(8,128)(2,1)} %multiply_bitcast_fusion.w_hid_t_ref, ...), custom_call_target="tpu_custom_call" | custom-call | flops 1923088384 | bytes 1077248 | tf_op jit(solution)/shard_map/pallas_call | solution.py:50
  145.6 19.1 %shard_map.114 = (f32[16,256]{1,0:T(8,128)}, f32[1,256]{1,0:T(1,128)}, f32[16,256]{1,0:T(8,128)}) custom-call(f32[1024,256]{1,0:T(8,128)} %all-gather.7.cloned.1.call-done.block_ref, f32[14,512]{1,0:T(8,128)} %shard_map.113.first_ref, f32[256,1]{1,0:T(8,128)} %broadcast_in_dim_reshape.4.ps_ref), custom_call_target="tpu_custom_call" | custom-call | tf_op jit(solution)/shard_map/pallas_call | solution.py:131
  165.3 23.4 %all-gather = f32[16,14,256]{2,1,0:T(8,128)S(1)} all-gather(f32[1,14,256]{2,1,0:T(8,128)S(1)} %slice_bitcast_fusion.2), channel_id=1, replica_groups=mesh['walker'=2,'z'=8,'x'=4,'y'=4] {'x','y'}, dimensions={0}, use_global_device_ids=true | all-gather | bytes 243712 | tf_op jit(solution)/shard_map/all_gather | solution.py:151
  189.5 1.2 log_bitcast_fusion
  190.7 34.6 %shard_map.115 = f32[14,1536]{1,0:T(8,128)} custom-call(f32[2,14,256,128]{3,2,1,0:T(8,128)} %broadcast_in_dim.64.col_ref, f32[2,256,2048]{2,1,0:T(8,128)} %pad_maximum_fusion.mat_ref, f32[256,256]{1,0:T(8,128)} %broadcast_in_dim.58.bias_in_ref, bf16[256,256]{1,0:T(8,128)(2,1)} %multiply_bitcast_fusion.w_hid_t_ref, f32[256,256]{1,0:T(8,128)} %broadcast_in_dim.59.bias_hid_ref, ...), custom_call_target="tpu_custom_call" | custom-call | flops 5769265152 | bytes 3231744 | tf_op jit(solution)/shard_map/pallas_call | solution.py:50
  225.3 1.5 all-gather.9.cloned.1.call-done
  226.8 3.8 %convolution_subtract_fusion = f32[14,1792]{1,0:T(8,128)} fusion(f32[14,256]{1,0:T(8,128)S(1)} %bitcast.38, f32[1792,256]{1,0:T(8,128)} %all-gather.9.cloned.1.call-done, f32[14,1536]{1,0:T(8,128)} %shard_map.115, f32[14,256]{1,0:T(8,128)S(1)} %slice-done), kind=kOutput, calls=%fused_computation.3 | convolution fusion | flops 77120512 | bytes 2050048 | tf_op jit(solution)/shard_map/dot_general | solution.py:217
  (42 shorter events, 8.5 us)
Async XLA Ops:
  7.2 0.7 copy-start
  7.2 34.4 %copy-start.3 = (s32[2048]{0:T(1024)S(1)}, s32[2048]{0:T(1024)}, u32[]{:S(2)}) copy-start(s32[2048]{0:T(1024)} %param.10) | copy-start | bytes 24580
  7.2 69.5 %slice-start.1 = ((s32[2048]{0:T(1024)}), s32[256]{0:T(256)S(1)}, s32[]{:S(2)}) async-start(s32[2048]{0:T(1024)} %param.10), calls=%async_computation.4 | async-start | bytes 2048 | tf_op jit(solution)/shard_map/slice | solution.py:187
  7.2 33.6 %copy-start.5 = (f32[256]{0:T(256)S(1)}, f32[256]{0:T(256)}, u32[]{:S(2)}) copy-start(f32[256]{0:T(256)} %param.16) | copy-start | bytes 3076
  7.2 69.5 %all-gather.5.cloned.1.call-start = ((), (), s32[]{:S(2)}) async-start(), calls=%async_computation | async-start | bytes 2359296 | tf_op jit(solution)/shard_map/all_gather | solution.py:151
  34.6 110.9 %all-gather.7.cloned.1.call-start = ((), (), s32[]{:S(2)}) async-start(), calls=%async_computation.1 | async-start | bytes 1179648 | tf_op jit(solution)/shard_map/all_gather | solution.py:151
  79.2 30.8 %copy-start.1 = (bf16[2048,512]{1,0:T(8,128)(2,1)S(1)}, bf16[2048,512]{1,0:T(8,128)(2,1)}, u32[]{:S(2)}) copy-start(bf16[2048,512]{1,0:T(8,128)(2,1)} %all-gather.5.cloned.1.call-done) | copy-start | bytes 6291460
  110.0 116.8 %all-gather.9.cloned.1.call-start = ((), (), s32[]{:S(2)}) async-start(), calls=%async_computation.2 | async-start | bytes 2064384 | tf_op jit(solution)/shard_map/all_gather | solution.py:151
  122.7 1.9 copy-start.2
  190.7 36.1 %slice-start = ((f32[14,512]{1,0:T(8,128)}), f32[14,256]{1,0:T(8,128)S(1)}, s32[]{:S(2)}) async-start(f32[14,512]{1,0:T(8,128)} %shard_map.113.first_ref), calls=%async_computation.3 | async-start | bytes 32768 | tf_op jit(solution)/shard_map/slice | solution.py:204
  190.7 36.1 %copy-start.4 = (f32[16,256]{1,0:T(8,128)S(1)}, f32[16,256]{1,0:T(8,128)}, u32[]{:S(2)}) copy-start(f32[16,256]{1,0:T(8,128)} %get-tuple-element.17) | copy-start | bytes 49156
Sparse Core Ops, SparseCore 0:
  34.7 41.9 all-gather.4
  110.1 35.2 all-gather.6
  189.6 37.1 all-gather.8

commit v12 on v11

--- a/solution.py
+++ b/solution.py
@@ -28,11 +28,14 @@
         out_ref[pl.ds(r, 1), :] = one(0, r) - one(1, r)
         return carry
 
+    if out_ref.shape[0] > rows:
+        out_ref[...] = jnp.zeros(out_ref.shape, out_ref.dtype)
     lax.fori_loop(0, rows, body, 0)
 
 
-def orbital_rows(cols, mats, params, first, blocks, width, after=None):
+def orbital_rows(cols, mats, params, first, blocks, width, after=None, out_rows=None):
     _, rows, feat, lanes = cols.shape
+    out_rows = rows if out_rows is None else out_rows
     count = blocks * width
     flops = 2 * rows * count * (2 * feat * feat + 12 * feat)
     operands = [cols, mats, *params]
@@ -50,9 +53,9 @@
     return pl.pallas_call(
         orbital_kernel,
         grid=(blocks,),
-        out_shape=jax.ShapeDtypeStruct((rows, count), jnp.float32),
+        out_shape=jax.ShapeDtypeStruct((out_rows, count), jnp.float32),
         in_specs=in_specs,
-        out_specs=pl.BlockSpec((rows, width), lambda j: (0, j)),
+        out_specs=pl.BlockSpec((out_rows, width), lambda j: (0, j)),
         cost_estimate=pl.CostEstimate(
             flops=flops,
             transcendentals=4 * rows * count * feat,
@@ -116,8 +119,8 @@
         return step
 
     carry = (jnp.zeros((1, size), jnp.float32), jnp.zeros((below, size), jnp.float32))
-    carry = lax.fori_loop(0, half // 2, make_step(0), carry, unroll=2)
-    pivots, scaled = lax.fori_loop(half // 2, size // 2, make_step(half), carry, unroll=2)
+    carry = lax.fori_loop(0, half // 2, make_step(0), carry, unroll=4)
+    pivots, scaled = lax.fori_loop(half // 2, size // 2, make_step(half), carry, unroll=4)
     pc_ref[...] = m_ref[size:, :]
     piv_ref[...] = pivots
     scaled_ref[...] = scaled
@@ -188,9 +191,10 @@
         ).astype(jnp.bfloat16)
         top_both = jnp.dot(selector, both_every, preferred_element_type=jnp.float32)
         top_own = lax.dynamic_slice_in_dim(top_both, device * share, share, 0)
-        top_rows = orbital_rows(columns(top_own), transposed(top_both), params, 0, 1, width)
         pad = (-share) % 8
-        top_padded = jnp.pad(top_rows, ((0, pad), (0, 0)))
+        top_padded = orbital_rows(
+            columns(top_own), transposed(top_both), params, 0, 1, width, out_rows=share + pad
+        )
         partial = gather_stages(top_padded, stages)
         gathered = partial[-1]
         late_every, _ = lax.optimization_barrier((both_every, partial[0]))

time: 238 us -> 239 us (level)
  no operation moved by 1% of the time
where the time goes in v12:
time: 239 us; the launch traced here: 238 us
  blocking collectives  74.2 us (31%)
  Pallas kernels  71.6 us (30%)
  waiting for transfers between devices  36.8 us (15%)
  local copies, waits for them, and re-layouts  27.4 us (11%)
  between operations  13.9 us (6%)
  matrix products  7.19 us (3%)
  other arithmetic  6.87 us (3%)
    all_gather x3, blocking collectives, gather_stages(): x = lax.all_gather(x, axes, axis=0, tiled=True)  74.2 us
    pallas_call x3, Pallas kernels, orbital_rows(): pl.pallas_call(orbital_kernel, grid=(blocks,), out_shape=jax.ShapeDtypeSt...  50.9 us
    all_gather x3, waiting for transfers between devices, gather_stages(): x = lax.all_gather(x, axes, axis=0, tiled=True)  36.8 us
    pallas_call x1, Pallas kernels, factor_augmented(): pl.pallas_call(functools.partial(factor_kernel, share), out_shape=(jax.Sh...  20.7 us
    gather x2, local copies, waits for them, and re-layouts, on_device(): halves = 0.5 * jnp.take(late_every, perm, axis=0).astype(jnp.float32)  12.1 us
    unnamed x17, local copies, waits for them, and re-layouts  5.24 us
  transfers between devices with their start and end apart: 3, of which 2 were waited for; matrix products, arithmetic and copies ran while one was open for 12% of the time, Pallas kernels for 20%

profile of v12, /device:TPU:6, one launch (start us, length us, event | category | flops | bytes accessed | tf_op | source)
XLA Modules:
  0.0 238.2 jit_solution(14453125652889470527)
XLA Ops:
  7.9 1.1 fusion
  9.0 25.6 %all_gather.18 = bf16[256,512]{1,0:T(8,128)(2,1)} all-gather(bf16[16,512]{1,0:T(8,128)(2,1)S(1)} %fusion), channel_id=1, replica_groups=mesh['walker'=2,'z'=8,'x'=4,'y'=4] {'x','y'}, dimensions={0}, use_global_device_ids=true | all-gather | bytes 278528 | tf_op jit(solution)/shard_map/all_gather | solution.py:154
  36.2 1.0 copy.33
  39.2 0.8 broadcast_in_dim.59.bias_hid_ref
  40.8 0.8 broadcast_in_dim.60.w_out_ref
  41.6 35.1 %all-gather.5.cloned.1.call-done = bf16[2048,512]{1,0:T(8,128)(2,1)} async-done(((bf16[256,512]{1,0:T(8,128)(2,1)}), bf16[2048,512]{1,0:T(8,128)(2,1)}) %all-gather.5.cloned.1.call-update) | async-done | bytes 2097168 | tf_op jit(solution)/shard_map/all_gather | solution.py:154
  76.7 2.3 fusion.1
  79.5 0.8 pad_maximum_fusion.1.mat_ref
  80.3 1.0 broadcast_in_dim.57.col_ref
  81.3 2.8 %shard_map.112 = f32[8,256]{1,0:T(8,128)} custom-call(f32[2,2,256,128]{3,2,1,0:T(8,128)} %broadcast_in_dim.57.col_ref, f32[2,256,256]{2,1,0:T(8,128)} %pad_maximum_fusion.1.mat_ref, f32[256,256]{1,0:T(8,128)} %broadcast_in_dim.58.bias_in_ref, bf16[256,256]{1,0:T(8,128)(2,1)} %multiply_bitcast_fusion.w_hid_t_ref, f32[256,256]{1,0:T(8,128)} %broadcast_in_dim.59.bias_hid_ref, ...), custom_call_target="tpu_custom_call" | custom-call | flops 137363456 | bytes 526336 | tf_op jit(solution)/shard_map/pallas_call | solution.py:53
  84.1 25.2 %all_gather.20 = f32[128,256]{1,0:T(8,128)} all-gather(f32[8,256]{1,0:T(8,128)} %shard_map.112), channel_id=1, replica_groups=mesh['walker'=2,'z'=8,'x'=4,'y'=4] {'x','y'}, dimensions={0}, use_global_device_ids=true | all-gather | bytes 139264 | tf_op jit(solution)/shard_map/all_gather | solution.py:154
  109.4 9.2 %gather_fusion = bf16[2048,512]{1,0:T(8,128)(2,1)} fusion(bf16[2048,512]{1,0:T(8,128)(2,1)S(1)} %copy-done.1, s32[2048]{0:T(1024)S(1)} %fusion.8), kind=kCustom, calls=%fused_computation | custom fusion | bytes 4202496 | tf_op jit(solution)/shard_map/jit(_take)/gather | solution.py:201
  118.5 2.9 %copy.34 = bf16[2048,512]{0,1:T(8,128)(2,1)S(1)} copy(bf16[2048,512]{1,0:T(8,128)(2,1)} %gather_fusion) | data formatting | bytes 4194304 | tf_op jit(solution)/shard_map/jit(_take)/gather | solution.py:201
  122.1 1.9 copy-done.2
  124.3 2.5 %slice_bitcast_fusion.1 = (f32[1,256,2048]{2,1,0:T(8,128)S(1)}, f32[1,256,2048]{2,1,0:T(8,128)S(1)}) fusion(f32[2048,512]{0,1:T(8,128)} %copy-done.2), kind=kLoop, calls=%fused_computation.5 | loop fusion | bytes 8388608 | tf_op jit(solution)/shard_map/stack | solution.py:180
  126.8 2.2 pad_maximum_fusion.mat_ref
  129.0 2.4 broadcast_in_dim.64.col_ref
  131.4 13.5 %shard_map.113.first_ref = f32[14,512]{1,0:T(8,128)} custom-call(f32[2,14,256,128]{3,2,1,0:T(8,128)} %broadcast_in_dim.64.col_ref, f32[2,256,2048]{2,1,0:T(8,128)} %pad_maximum_fusion.mat_ref, f32[256,256]{1,0:T(8,128)} %broadcast_in_dim.58.bias_in_ref, bf16[256,256]{1,0:T(8,128)(2,1)} %multiply_bitcast_fusion.w_hid_t_ref, ...), custom_call_target="tpu_custom_call" | custom-call | flops 1923088384 | bytes 1077248 | tf_op jit(solution)/shard_map/pallas_call | solution.py:53
  144.9 20.7 %shard_map.114 = (f32[16,256]{1,0:T(8,128)}, f32[1,256]{1,0:T(1,128)}, f32[16,256]{1,0:T(8,128)}) custom-call(f32[1024,256]{1,0:T(8,128)} %all-gather.7.cloned.1.call-done.block_ref, f32[14,512]{1,0:T(8,128)} %shard_map.113.first_ref, f32[256,1]{1,0:T(8,128)} %broadcast_in_dim_reshape.4.ps_ref), custom_call_target="tpu_custom_call" | custom-call | tf_op jit(solution)/shard_map/pallas_call | solution.py:134
  166.3 23.4 %all-gather = f32[16,14,256]{2,1,0:T(8,128)S(1)} all-gather(f32[1,14,256]{2,1,0:T(8,128)S(1)} %slice_bitcast_fusion.2), channel_id=1, replica_groups=mesh['walker'=2,'z'=8,'x'=4,'y'=4] {'x','y'}, dimensions={0}, use_global_device_ids=true | all-gather | bytes 243712 | tf_op jit(solution)/shard_map/all_gather | solution.py:154
  190.4 1.2 log_bitcast_fusion
  191.6 34.6 %shard_map.115 = f32[14,1536]{1,0:T(8,128)} custom-call(f32[2,14,256,128]{3,2,1,0:T(8,128)} %broadcast_in_dim.64.col_ref, f32[2,256,2048]{2,1,0:T(8,128)} %pad_maximum_fusion.mat_ref, f32[256,256]{1,0:T(8,128)} %broadcast_in_dim.58.bias_in_ref, bf16[256,256]{1,0:T(8,128)(2,1)} %multiply_bitcast_fusion.w_hid_t_ref, f32[256,256]{1,0:T(8,128)} %broadcast_in_dim.59.bias_hid_ref, ...), custom_call_target="tpu_custom_call" | custom-call | flops 5769265152 | bytes 3231744 | tf_op jit(solution)/shard_map/pallas_call | solution.py:53
  226.2 1.7 all-gather.9.cloned.1.call-done
  227.9 3.8 %convolution_subtract_fusion = f32[14,1792]{1,0:T(8,128)} fusion(f32[14,256]{1,0:T(8,128)S(1)} %bitcast.38, f32[1792,256]{1,0:T(8,128)} %all-gather.9.cloned.1.call-done, f32[14,1536]{1,0:T(8,128)} %shard_map.115, f32[14,256]{1,0:T(8,128)S(1)} %slice-done), kind=kOutput, calls=%fused_computation.3 | convolution fusion | flops 77120512 | bytes 2050048 | tf_op jit(solution)/shard_map/dot_general | solution.py:221
  (41 shorter events, 7.8 us)
Async XLA Ops:
  7.2 0.7 copy-start
  7.2 34.4 %copy-start.3 = (s32[2048]{0:T(1024)S(1)}, s32[2048]{0:T(1024)}, u32[]{:S(2)}) copy-start(s32[2048]{0:T(1024)} %param.10) | copy-start | bytes 24580
  7.2 69.5 %slice-start.1 = ((s32[2048]{0:T(1024)}), s32[256]{0:T(256)S(1)}, s32[]{:S(2)}) async-start(s32[2048]{0:T(1024)} %param.10), calls=%async_computation.4 | async-start | bytes 2048 | tf_op jit(solution)/shard_map/slice | solution.py:190
  7.2 33.6 %copy-start.5 = (f32[256]{0:T(256)S(1)}, f32[256]{0:T(256)}, u32[]{:S(2)}) copy-start(f32[256]{0:T(256)} %param.16) | copy-start | bytes 3076
  7.2 69.5 %all-gather.5.cloned.1.call-start = ((), (), s32[]{:S(2)}) async-start(), calls=%async_computation | async-start | bytes 2359296 | tf_op jit(solution)/shard_map/all_gather | solution.py:154
  34.6 110.3 %all-gather.7.cloned.1.call-start = ((), (), s32[]{:S(2)}) async-start(), calls=%async_computation.1 | async-start | bytes 1179648 | tf_op jit(solution)/shard_map/all_gather | solution.py:154
  79.2 30.1 %copy-start.1 = (bf16[2048,512]{1,0:T(8,128)(2,1)S(1)}, bf16[2048,512]{1,0:T(8,128)(2,1)}, u32[]{:S(2)}) copy-start(bf16[2048,512]{1,0:T(8,128)(2,1)} %all-gather.5.cloned.1.call-done) | copy-start | bytes 6291460
  109.3 118.6 %all-gather.9.cloned.1.call-start = ((), (), s32[]{:S(2)}) async-start(), calls=%async_computation.2 | async-start | bytes 2064384 | tf_op jit(solution)/shard_map/all_gather | solution.py:154
  122.1 1.9 copy-start.2
  191.6 36.3 %slice-start = ((f32[14,512]{1,0:T(8,128)}), f32[14,256]{1,0:T(8,128)S(1)}, s32[]{:S(2)}) async-start(f32[14,512]{1,0:T(8,128)} %shard_map.113.first_ref), calls=%async_computation.3 | async-start | bytes 32768 | tf_op jit(solution)/shard_map/slice | solution.py:208
  191.6 36.3 %copy-start.4 = (f32[16,256]{1,0:T(8,128)S(1)}, f32[16,256]{1,0:T(8,128)}, u32[]{:S(2)}) copy-start(f32[16,256]{1,0:T(8,128)} %get-tuple-element.17) | copy-start | bytes 49156
Sparse Core Ops, SparseCore 0:
  34.7 41.9 all-gather.4
  109.4 35.4 all-gather.6
  190.6 37.2 all-gather.8

commit v13 on v11

--- a/solution.py
+++ b/solution.py
@@ -18,7 +18,8 @@
 
     def one(d, r):
         col = col_ref[d, r]
-        col = jnp.concatenate([col] * copies, axis=1) if copies > 1 else col
+        if 1 < col.shape[1] < mat_ref.shape[2]:
+            col = jnp.concatenate([col] * copies, axis=1)
         half = (col + mat_ref[d]) + bias_in_ref[...]
         gated = (half * (1.0 + jnp.tanh(half))).astype(jnp.bfloat16)
         half = jnp.dot(w_hid_t, gated, preferred_element_type=jnp.float32) + bias_hid_ref[...]
@@ -169,9 +170,9 @@
         width = panel
         lanes = 128
 
-        def columns(rows_both):
+        def columns(rows_both, spread=lanes):
             stacked = jnp.stack([rows_both[:, :hid], rows_both[:, hid:]])[..., None]
-            return jnp.broadcast_to(stacked, stacked.shape[:-1] + (lanes,))
+            return jnp.broadcast_to(stacked, stacked.shape[:-1] + (spread,))
 
         def transposed(rows_both):
             return jnp.stack([rows_both[:, hid:].T, rows_both[:, :hid].T])
@@ -188,7 +189,7 @@
         ).astype(jnp.bfloat16)
         top_both = jnp.dot(selector, both_every, preferred_element_type=jnp.float32)
         top_own = lax.dynamic_slice_in_dim(top_both, device * share, share, 0)
-        top_rows = orbital_rows(columns(top_own), transposed(top_both), params, 0, 1, width)
+        top_rows = orbital_rows(columns(top_own, 1), transposed(top_both), params, 0, 1, width)
         pad = (-share) % 8
         top_padded = jnp.pad(top_rows, ((0, pad), (0, 0)))
         partial = gather_stages(top_padded, stages)

time: 238 us -> 238 us (level)
  no operation moved by 1% of the time
where the time goes in v13:
time: 238 us; the launch traced here: 237 us
  blocking collectives  74.2 us (31%)
  Pallas kernels  70.1 us (29%)
  waiting for transfers between devices  36.8 us (15%)
  local copies, waits for them, and re-layouts  28.2 us (12%)
  between operations  13.9 us (6%)
  matrix products  7.19 us (3%)
  other arithmetic  6.86 us (3%)
    all_gather x3, blocking collectives, gather_stages(): x = lax.all_gather(x, axes, axis=0, tiled=True)  74.2 us
    pallas_call x3, Pallas kernels, orbital_rows(): pl.pallas_call(orbital_kernel, grid=(blocks,), out_shape=jax.ShapeDtypeSt...  51 us
    all_gather x3, waiting for transfers between devices, gather_stages(): x = lax.all_gather(x, axes, axis=0, tiled=True)  36.7 us
    pallas_call x1, Pallas kernels, factor_augmented(): pl.pallas_call(functools.partial(factor_kernel, share), out_shape=(jax.Sh...  19.1 us
    gather x2, local copies, waits for them, and re-layouts, on_device(): halves = 0.5 * jnp.take(late_every, perm, axis=0).astype(jnp.float32)  12.1 us
    unnamed x17, local copies, waits for them, and re-layouts  5.24 us
  transfers between devices with their start and end apart: 3, of which 2 were waited for; matrix products, arithmetic and copies ran while one was open for 12% of the time, Pallas kernels for 20%

profile of v13, /device:TPU:6, one launch (start us, length us, event | category | flops | bytes accessed | tf_op | source)
XLA Modules:
  0.0 237.3 jit_solution(15745596635245549097)
XLA Ops:
  7.9 1.1 fusion
  9.0 25.6 %all_gather.18 = bf16[256,512]{1,0:T(8,128)(2,1)} all-gather(bf16[16,512]{1,0:T(8,128)(2,1)S(1)} %fusion), channel_id=1, replica_groups=mesh['walker'=2,'z'=8,'x'=4,'y'=4] {'x','y'}, dimensions={0}, use_global_device_ids=true | all-gather | bytes 278528 | tf_op jit(solution)/shard_map/all_gather | solution.py:152
  36.2 1.0 copy.35
  39.2 0.8 broadcast_in_dim.56.bias_hid_ref
  40.8 0.8 broadcast_in_dim.57.w_out_ref
  41.6 35.1 %all-gather.5.cloned.1.call-done = bf16[2048,512]{1,0:T(8,128)(2,1)} async-done(((bf16[256,512]{1,0:T(8,128)(2,1)}), bf16[2048,512]{1,0:T(8,128)(2,1)}) %all-gather.5.cloned.1.call-update) | async-done | bytes 2097168 | tf_op jit(solution)/shard_map/all_gather | solution.py:152
  76.7 2.3 fusion.1
  79.5 1.0 copy.36.col_ref
  80.5 0.8 pad_maximum_fusion.1.mat_ref
  81.3 2.9 %shard_map.112 = f32[2,256]{1,0:T(2,128)} custom-call(f32[2,2,256,1]{3,2,1,0:T(8,128)} %copy.36.col_ref, f32[2,256,256]{2,1,0:T(8,128)} %pad_maximum_fusion.1.mat_ref, f32[256,256]{1,0:T(8,128)} %broadcast_in_dim.55.bias_in_ref, bf16[256,256]{1,0:T(8,128)(2,1)} %multiply_bitcast_fusion.w_hid_t_ref, f32[256,256]{1,0:T(8,128)} %broadcast_in_dim.56.bias_hid_ref, ...), custom_call_target="tpu_custom_call" | custom-call | flops 137363456 | bytes 526336 | tf_op jit(solution)/shard_map/pallas_call | solution.py:51
  84.9 25.2 %all_gather.20 = f32[128,256]{1,0:T(8,128)} all-gather(f32[8,256]{1,0:T(8,128)S(1)} %pad.4), channel_id=1, replica_groups=mesh['walker'=2,'z'=8,'x'=4,'y'=4] {'x','y'}, dimensions={0}, use_global_device_ids=true | all-gather | bytes 139264 | tf_op jit(solution)/shard_map/all_gather | solution.py:152
  110.2 9.2 %gather_fusion = bf16[2048,512]{1,0:T(8,128)(2,1)} fusion(bf16[2048,512]{1,0:T(8,128)(2,1)S(1)} %copy-done.1, s32[2048]{0:T(1024)S(1)} %fusion.8), kind=kCustom, calls=%fused_computation | custom fusion | bytes 4202496 | tf_op jit(solution)/shard_map/jit(_take)/gather | solution.py:198
  119.4 2.9 %copy.37 = bf16[2048,512]{0,1:T(8,128)(2,1)S(1)} copy(bf16[2048,512]{1,0:T(8,128)(2,1)} %gather_fusion) | data formatting | bytes 4194304 | tf_op jit(solution)/shard_map/jit(_take)/gather | solution.py:198
  122.9 1.9 copy-done.2
  125.1 2.5 %slice_bitcast_fusion.1 = (f32[1,256,2048]{2,1,0:T(8,128)S(1)}, f32[1,256,2048]{2,1,0:T(8,128)S(1)}) fusion(f32[2048,512]{0,1:T(8,128)} %copy-done.2), kind=kLoop, calls=%fused_computation.5 | loop fusion | bytes 8388608 | tf_op jit(solution)/shard_map/stack | solution.py:178
  127.6 2.2 pad_maximum_fusion.mat_ref
  129.8 2.4 broadcast_in_dim.61.col_ref
  132.2 13.5 %shard_map.113.first_ref = f32[14,512]{1,0:T(8,128)} custom-call(f32[2,14,256,128]{3,2,1,0:T(8,128)} %broadcast_in_dim.61.col_ref, f32[2,256,2048]{2,1,0:T(8,128)} %pad_maximum_fusion.mat_ref, f32[256,256]{1,0:T(8,128)} %broadcast_in_dim.55.bias_in_ref, bf16[256,256]{1,0:T(8,128)(2,1)} %multiply_bitcast_fusion.w_hid_t_ref, ...), custom_call_target="tpu_custom_call" | custom-call | flops 1923088384 | bytes 1077248 | tf_op jit(solution)/shard_map/pallas_call | solution.py:51
  145.7 19.1 %shard_map.114 = (f32[16,256]{1,0:T(8,128)}, f32[1,256]{1,0:T(1,128)}, f32[16,256]{1,0:T(8,128)}) custom-call(f32[1024,256]{1,0:T(8,128)} %all-gather.7.cloned.1.call-done.block_ref, f32[14,512]{1,0:T(8,128)} %shard_map.113.first_ref, f32[256,1]{1,0:T(8,128)} %broadcast_in_dim_reshape.4.ps_ref), custom_call_target="tpu_custom_call" | custom-call | tf_op jit(solution)/shard_map/pallas_call | solution.py:132
  165.5 23.4 %all-gather = f32[16,14,256]{2,1,0:T(8,128)S(1)} all-gather(f32[1,14,256]{2,1,0:T(8,128)S(1)} %slice_bitcast_fusion.2), channel_id=1, replica_groups=mesh['walker'=2,'z'=8,'x'=4,'y'=4] {'x','y'}, dimensions={0}, use_global_device_ids=true | all-gather | bytes 243712 | tf_op jit(solution)/shard_map/all_gather | solution.py:152
  189.6 1.2 log_bitcast_fusion
  190.8 34.6 %shard_map.115 = f32[14,1536]{1,0:T(8,128)} custom-call(f32[2,14,256,128]{3,2,1,0:T(8,128)} %broadcast_in_dim.61.col_ref, f32[2,256,2048]{2,1,0:T(8,128)} %pad_maximum_fusion.mat_ref, f32[256,256]{1,0:T(8,128)} %broadcast_in_dim.55.bias_in_ref, bf16[256,256]{1,0:T(8,128)(2,1)} %multiply_bitcast_fusion.w_hid_t_ref, f32[256,256]{1,0:T(8,128)} %broadcast_in_dim.56.bias_hid_ref, ...), custom_call_target="tpu_custom_call" | custom-call | flops 5769265152 | bytes 3231744 | tf_op jit(solution)/shard_map/pallas_call | solution.py:51
  225.4 1.6 all-gather.9.cloned.1.call-done
  227.0 3.8 %convolution_subtract_fusion = f32[14,1792]{1,0:T(8,128)} fusion(f32[14,256]{1,0:T(8,128)S(1)} %bitcast.40, f32[1792,256]{1,0:T(8,128)} %all-gather.9.cloned.1.call-done, f32[14,1536]{1,0:T(8,128)} %shard_map.115, f32[14,256]{1,0:T(8,128)S(1)} %slice-done), kind=kOutput, calls=%fused_computation.3 | convolution fusion | flops 77120512 | bytes 2050048 | tf_op jit(solution)/shard_map/dot_general | solution.py:218
  (42 shorter events, 8.5 us)
Async XLA Ops:
  7.2 0.7 copy-start
  7.2 34.4 %copy-start.3 = (s32[2048]{0:T(1024)S(1)}, s32[2048]{0:T(1024)}, u32[]{:S(2)}) copy-start(s32[2048]{0:T(1024)} %param.10) | copy-start | bytes 24580
  7.2 69.5 %slice-start.1 = ((s32[2048]{0:T(1024)}), s32[256]{0:T(256)S(1)}, s32[]{:S(2)}) async-start(s32[2048]{0:T(1024)} %param.10), calls=%async_computation.4 | async-start | bytes 2048 | tf_op jit(solution)/shard_map/slice | solution.py:188
  7.2 33.6 %copy-start.5 = (f32[256]{0:T(256)S(1)}, f32[256]{0:T(256)}, u32[]{:S(2)}) copy-start(f32[256]{0:T(256)} %param.16) | copy-start | bytes 3076
  7.2 69.5 %all-gather.5.cloned.1.call-start = ((), (), s32[]{:S(2)}) async-start(), calls=%async_computation | async-start | bytes 2359296 | tf_op jit(solution)/shard_map/all_gather | solution.py:152
  34.6 111.1 %all-gather.7.cloned.1.call-start = ((), (), s32[]{:S(2)}) async-start(), calls=%async_computation.1 | async-start | bytes 1179648 | tf_op jit(solution)/shard_map/all_gather | solution.py:152
  79.2 30.9 %copy-start.1 = (bf16[2048,512]{1,0:T(8,128)(2,1)S(1)}, bf16[2048,512]{1,0:T(8,128)(2,1)}, u32[]{:S(2)}) copy-start(bf16[2048,512]{1,0:T(8,128)(2,1)} %all-gather.5.cloned.1.call-done) | copy-start | bytes 6291460
  110.1 116.9 %all-gather.9.cloned.1.call-start = ((), (), s32[]{:S(2)}) async-start(), calls=%async_computation.2 | async-start | bytes 2064384 | tf_op jit(solution)/shard_map/all_gather | solution.py:152
  122.9 1.9 copy-start.2
  190.8 36.2 %slice-start = ((f32[14,512]{1,0:T(8,128)}), f32[14,256]{1,0:T(8,128)S(1)}, s32[]{:S(2)}) async-start(f32[14,512]{1,0:T(8,128)} %shard_map.113.first_ref), calls=%async_computation.3 | async-start | bytes 32768 | tf_op jit(solution)/shard_map/slice | solution.py:205
  190.8 36.2 %copy-start.4 = (f32[16,256]{1,0:T(8,128)S(1)}, f32[16,256]{1,0:T(8,128)}, u32[]{:S(2)}) copy-start(f32[16,256]{1,0:T(8,128)} %get-tuple-element.17) | copy-start | bytes 49156
Sparse Core Ops, SparseCore 0:
  34.7 41.9 all-gather.4
  110.2 35.4 all-gather.6
  189.8 37.2 all-gather.8
